TPU v7x, 512 devices: a whole 4x4x16 slice. The times are simulated.
512 devices in a mesh: pool: 128 (over x, z, core), tp: 4 (over y).
Axes of the slice: x: 4, y: 4, z: 16, core: 2. Of those that a mesh axis runs over, the one named last changes fastest.
Arguments:
- hidden_rows: bfloat16 [16384, 8192], P('pool', 'tp'), may hold values from -6 to 6
- kv_weight: bfloat16 [8192, 1024], P('tp', 'pool'), may hold values from -0.0625 to 0.0625
- queries: bfloat16 [16384, 4096], P('pool', 'tp'), may hold values from -5 to 5
- cache_table: bfloat16 [1024, 128, 1024], P('pool', None, 'tp'), may hold values from -5 to 5
- retrieval: int32 [128, 64], P('pool'), may hold values from 0 to 1023, as said below
- pattern: int32 [128, 2, 64], P('pool'), may hold values 0 or 1
Outputs:
- attended: bfloat16 [16384, 4096], P('pool', 'tp')
- fresh_kv: bfloat16 [16384, 1024], P('pool', 'tp')
Inputs may be any that keep to these rules, and one draw needn't show every extreme that they name: `retrieval`: each request names 64 blocks held by 64 different devices (block b is held by device b // 8); one device, drawn from the seed, holds a block named by every request.
All inputs are finite; a program needn't handle non-finite values. No bound on the sum of `pattern` on one device may be relied on, other than what follows from the above.
Results may differ from a plain program's by a relative error of at most 0.025.
Values may be sent and summed in bfloat16 or wider, within the bound.
No kernel may reach another device: no remote copies, remote signals or barrier semaphores. Data moves between devices by JAX's collectives and lax.ppermute only.
A program may use at most 192 MiB of HBM per device.

v0:
```python
import math

import jax
import jax.numpy as jnp
from jax import lax
from jax.sharding import PartitionSpec as P

HD = 128
QH = 32
KVH = 4
BLK = 128
RBLK = 64


def rows_by_keys(left, right):
    return lax.dot_general(
        left, right, (((1,), (1,)), ((), ())), preferred_element_type=jnp.float32
    )


def body(hidden_rows, kv_weight, queries, cache_table, retrieval, pattern):
    partial_kv = jnp.dot(
        hidden_rows,
        lax.all_gather(kv_weight, "pool", axis=1, tiled=True),
        preferred_element_type=jnp.float32,
    )
    fresh = lax.psum_scatter(partial_kv.astype(jnp.bfloat16), "tp", scatter_dimension=1, tiled=True)
    wanted = retrieval[0]
    blocks_dev = cache_table.shape[0]
    npool = lax.axis_size("pool")
    owners = wanted // blocks_dev
    local = wanted % blocks_dev
    hits = (owners[:, None] == jnp.arange(npool, dtype=jnp.int32)[None, :]).astype(jnp.int32)
    request = jnp.sum(hits * (local + 1)[:, None], axis=0)
    incoming = lax.all_to_all(
        request.reshape(npool, 1), "pool", split_axis=0, concat_axis=0, tiled=True
    ).reshape(npool)
    reply = jnp.zeros((npool,) + cache_table.shape[1:], jnp.bfloat16)
    for slot in range(blocks_dev):
        reply = jnp.where((incoming == slot + 1)[:, None, None], cache_table[slot][None], reply)
    arrived = lax.all_to_all(reply, "pool", split_axis=0, concat_axis=0, tiled=True)
    fetched = jnp.take(arrived, owners, axis=0)
    count = hidden_rows.shape[0]
    fetch_count = wanted.shape[0]
    group = QH // KVH
    scale = float(HD) ** (-0.5)
    local_heads = fresh.shape[1] // (2 * HD)
    width = fetched.shape[2]
    per_step = math.gcd(fetch_count, 8)
    steps_count = fetch_count // per_step
    grouped = fetched.reshape(steps_count, per_step * BLK, width)
    pat_steps = jnp.transpose(
        pattern[0].reshape(pattern.shape[1], steps_count, per_step), (1, 0, 2)
    )
    token_of_row = jnp.arange(count * group) // group
    block_of_row = token_of_row // RBLK
    row_blocks = block_of_row[:, None, None] == jnp.arange(pattern.shape[1])[None, :, None]
    near_mask = token_of_row[:, None] >= jnp.arange(count)[None, :]
    q_heads = queries.reshape(count, local_heads, group * HD)
    q_rows = q_heads[:, 0].reshape(count * group, HD)
    near_keys = fresh[:, 0:HD]
    near_vals = fresh[:, HD : 2 * HD]
    near_scores = rows_by_keys(q_rows, near_keys) * scale
    top = jnp.max(jnp.where(near_mask, near_scores, -1e30), axis=1)
    weights = jnp.where(near_mask, jnp.exp(near_scores - top[:, None]), 0.0)
    total = jnp.sum(weights, axis=1)
    numer = jnp.dot(weights.astype(jnp.bfloat16), near_vals, preferred_element_type=jnp.float32)

    def visit(carry, items):
        top_now, total_now, numer_now = carry
        block_rows, pat_now = items
        keys = block_rows[:, 0:HD]
        vals = block_rows[:, HD : 2 * HD]
        scores = rows_by_keys(q_rows, keys) * scale
        row_pat = jnp.any(row_blocks & (pat_now[None] != 0), axis=1)
        mask = jnp.repeat(row_pat, BLK, axis=1)
        top_new = jnp.maximum(top_now, jnp.max(jnp.where(mask, scores, -1e30), axis=1))
        weights_now = jnp.where(mask, jnp.exp(scores - top_new[:, None]), 0.0)
        factor = jnp.exp(top_now - top_new)
        total_new = total_now * factor + jnp.sum(weights_now, axis=1)
        numer_new = numer_now * factor[:, None] + jnp.dot(
            weights_now.astype(jnp.bfloat16), vals, preferred_element_type=jnp.float32
        )
        return ((top_new, total_new, numer_new), None)

    (top, total, numer), unused = lax.scan(visit, (top, total, numer), (grouped, pat_steps))
    results = (numer / total[:, None]).reshape(count, group * HD)
    attended = results.astype(jnp.bfloat16)
    return (attended, fresh)


def solution(mesh):
    placed = (
        P("pool", "tp"),
        P("tp", "pool"),
        P("pool", "tp"),
        P("pool", None, "tp"),
        P("pool", None),
        P("pool", None, None),
    )
    return jax.shard_map(
        body,
        mesh=mesh,
        in_specs=placed,
        out_specs=(P("pool", "tp"), P("pool", "tp")),
        check_vma=False,
    )
```

profile of v0, /device:TPU:16, one launch (start us, length us, event | category | flops | bytes accessed | tf_op | source)
XLA Modules:
  0.0 508.4 jit_solution(17769728993314333137)
XLA Ops:
  7.2 0.7 and_select_fusion.2
  7.9 0.1 select_reduce_fusion.1
  8.0 0.7 copy.22
  8.8 19.8 %all-to-all-start = ((s32[128,1,1]{2,1,0:T(1,128)}), s32[128,1,1]{2,1,0:T(1,128)S(1)}, u32[]{:S(2)}, u32[]{:S(2)}) async-start(s32[128,1,1]{2,1,0:T(1,128)} %copy.22), calls=%async_computation.1 | async-start | bytes 131072 | tf_op jit(solution)/shard_map/all_to_all | solution.py:35
  28.5 1.1 slice_bitcast_fusion.7
  29.6 14.4 %all-to-all-done = s32[128,1,1]{2,1,0:T(1,128)S(1)} async-done(((s32[128,1,1]{2,1,0:T(1,128)}), s32[128,1,1]{2,1,0:T(1,128)S(1)}, u32[]{:S(2)}, u32[]{:S(2)}) %all-to-all-start) | async-done | bytes 544 | tf_op jit(solution)/shard_map/all_to_all | solution.py:35
  44.0 18.3 %compare_reduce_fusion.7 = (pred[128]{0:T(512)(128)(4,1)S(1)}, pred[128]{0:T(512)(128)(4,1)S(1)}, pred[128]{0:T(512)(128)(4,1)S(1)}, pred[128]{0:T(512)(128)(4,1...) fusion(s32[128,1,1]{2,1,0:T(1,128)S(1)} %all-to-all-done), kind=kLoop, calls=%fused_computation.42 | loop fusion | flops 1024 | bytes 1536 | tf_op jit(solution)/shard_map/eq | solution.py:40
  62.4 7.7 %select_select_fusion = bf16[128,128,256]{2,1,0:T(8,128)(2,1)} fusion(pred[128]{0:T(512)(128)(4,1)S(1)} %get-tuple-element.107, pred[128]{0:T(512)(128)(4,1)S(1)} %get-tuple-element.108, pred[128]{0:T(512)(128)(4,1)S(1)} %get-tuple-element.109, pred[128]{0:T(512)(128)(4,1)S(1)} %get-tuple-element.110, pred[128]{0:T(512)(128)(4,1)S(1)} %get-tuple-element.111, ...), kind=kLoop, calls=%fused_computation.20 | loop fusion | flops 33554432 | bytes 8913920 | tf_op jit(solution)/shard_map/jit(_where)/select_n | solution.py:40
  70.1 7.6 %all-to-all-start.1 = ((bf16[128,128,256]{2,1,0:T(8,128)(2,1)}), bf16[128,128,256]{2,1,0:T(8,128)(2,1)}, u32[]{:S(2)}, u32[]{:S(2)}) async-start(bf16[128,128,256]{2,1,0:T(8,128)(2,1)} %select_select_fusion), calls=%async_computation.2 | async-start | bytes 16777216 | tf_op jit(solution)/shard_map/all_to_all | solution.py:41
  77.7 0.7 all-gather.2.cloned.1.call-update
  78.5 0.5 broadcast.347
  79.0 0.7 reduce.19
  79.7 0.1 squeeze.13
  79.8 0.1 copy.21
  79.9 0.1 reshape_squeeze_reshape.3
  80.1 198.1 %all-gather.2.cloned.1.call-done = bf16[2048,1024]{0,1:T(8,128)(2,1)} async-done(((bf16[2048,8]{0,1:T(8,128)(2,1)}), bf16[2048,1024]{0,1:T(8,128)(2,1)}) %all-gather.2.cloned.1.call-update) | async-done | bytes 4194320 | tf_op jit(solution)/shard_map/all_gather | solution.py:24
  278.2 4.4 convolution_convert_fusion
  282.7 28.1 %reduce-scatter.2.cloned.1.call-done = bf16[128,256]{1,0:T(8,128)(2,1)} async-done(((bf16[128,1024]{1,0:T(8,128)(2,1)}), bf16[128,256]{1,0:T(8,128)(2,1)}) %reduce-scatter.2.cloned.1.call-update) | async-done | bytes 65552 | tf_op jit(solution)/shard_map/reduce_scatter | solution.py:27
  310.8 1.0 select_reduce_fusion
  311.8 0.1 fusion.11
  311.9 1.0 fusion.12
  313.0 144.7 %all-to-all-done.1 = bf16[128,128,256]{2,1,0:T(8,128)(2,1)} async-done(((bf16[128,128,256]{2,1,0:T(8,128)(2,1)}), bf16[128,128,256]{2,1,0:T(8,128)(2,1)}, u32[]{:S(2)}, u32[]{:S(2)}) %all-to-all-start.1) | async-done | bytes 8388640 | tf_op jit(solution)/shard_map/all_to_all | solution.py:41
  457.7 6.2 %gather_fusion = bf16[64,128,256]{2,1,0:T(8,128)(2,1)} fusion(bf16[128,128,256]{2,1,0:T(8,128)(2,1)} %all-to-all-done.1, s32[1024]{0:T(1024)S(1)} %pad_clamp_fusion), kind=kCustom, calls=%fused_computation | custom fusion | bytes 8388864 | tf_op jit(solution)/shard_map/jit(_take)/gather | solution.py:42
  463.8 5.3 %bitcast_select_fusion.2 = bf16[8,1024,256]{2,1,0:T(8,128)(2,1)} fusion(pred[8,1024]{1,0:T(8,128)(4,1)S(1)} %broadcast_bitcast_fusion, bf16[8,1024,256]{2,1,0:T(8,128)(2,1)} %bitcast.104), kind=kLoop, calls=%fused_computation.21 | loop fusion | flops 2097152 | bytes 8396800 | tf_op jit(solution)/shard_map/jit(_take)/select_n | solution.py:42
  469.1 31.4 %while.15 = (s32[]{:T(128)}, f32[1024]{0:T(1024)S(1)}, f32[1024]{0:T(1024)S(1)}, f32[1024,128]{1,0:T(8,128)S(1)}, s32[8,2,8]{2,0,1:T(8,128)S(1)}, /*index=5*/bf1...) while((s32[]{:T(128)}, f32[1024]{0:T(1024)S(1)}, ...), condition=%wide.region_8.9_spmd.clone, body=%wide.region_4.8_spmd.clone.sunk | while | flops 545550336 | bytes 15561029 | solution.py:86
  469.2 0.1 and_reduce_fusion.2
  469.2 1.1 dynamic-slice_bitcast_fusion.2
  470.3 0.7 fusion.42
  471.1 0.9 fusion.43
  472.0 1.0 convolution_add_fusion.2
  473.1 0.1 and_reduce_fusion.2
  473.2 1.1 dynamic-slice_bitcast_fusion.2
  474.2 0.7 fusion.42
  475.0 0.9 fusion.43
  476.0 1.0 convolution_add_fusion.2
  477.0 0.1 and_reduce_fusion.2
  477.1 1.1 dynamic-slice_bitcast_fusion.2
  478.2 0.7 fusion.42
  478.9 0.9 fusion.43
  479.9 1.0 convolution_add_fusion.2
  480.9 0.1 and_reduce_fusion.2
  481.0 1.1 dynamic-slice_bitcast_fusion.2
  482.1 0.7 fusion.42
  482.9 0.9 fusion.43
  483.8 1.0 convolution_add_fusion.2
  484.9 0.1 and_reduce_fusion.2
  485.0 1.1 dynamic-slice_bitcast_fusion.2
  486.0 0.7 fusion.42
  486.8 0.9 fusion.43
  487.7 1.0 convolution_add_fusion.2
  488.9 1.1 dynamic-slice_bitcast_fusion.2
  490.0 0.7 fusion.42
  490.7 0.9 fusion.43
  491.7 1.0 convolution_add_fusion.2
  492.8 1.1 dynamic-slice_bitcast_fusion.2
  493.9 0.7 fusion.42
  494.7 0.9 fusion.43
  495.6 1.0 convolution_add_fusion.2
  496.7 1.1 dynamic-slice_bitcast_fusion.2
  497.8 0.7 fusion.42
  498.6 0.9 fusion.43
  499.5 1.0 convolution_add_fusion.2
  500.5 0.2 divide_convert_fusion
  500.8 0.8 convert_element_type.19
  (69 shorter events, 0.9 us)
Async XLA Ops:
  7.2 271.0 %copy-start = (bf16[128,2048]{1,0:T(8,128)(2,1)S(1)}, bf16[128,2048]{1,0:T(8,128)(2,1)}, u32[]{:S(2)}) copy-start(bf16[128,2048]{1,0:T(8,128)(2,1)} %param.8) | copy-start | bytes 1572868
  8.8 35.3 %all-to-all-start = ((s32[128,1,1]{2,1,0:T(1,128)}), s32[128,1,1]{2,1,0:T(1,128)S(1)}, u32[]{:S(2)}, u32[]{:S(2)}) async-start(s32[128,1,1]{2,1,0:T(1,128)} %copy.22), calls=%async_computation.1 | async-start | bytes 131072 | tf_op jit(solution)/shard_map/all_to_all | solution.py:35
  70.1 8.9 %copy-start.3 = (s32[1,64]{1,0:T(1,128)S(1)}, s32[1,64]{1,0:T(1,128)}, u32[]{:S(2)}) copy-start(s32[1,64]{1,0:T(1,128)} %param.12) | copy-start | bytes 772
  70.1 9.8 %copy-start.1 = (bf16[128,1024]{1,0:T(8,128)(2,1)S(1)}, bf16[128,1024]{1,0:T(8,128)(2,1)}, u32[]{:S(2)}) copy-start(bf16[128,1024]{1,0:T(8,128)(2,1)} %param.10) | copy-start | bytes 786436
  70.1 9.9 %copy-start.2 = (s32[1,2,64]{2,1,0:T(2,128)S(1)}, s32[1,2,64]{2,1,0:T(2,128)}, u32[]{:S(2)}) copy-start(s32[1,2,64]{2,1,0:T(2,128)} %param.13) | copy-start | bytes 1540
  70.1 387.6 %all-to-all-start.1 = ((bf16[128,128,256]{2,1,0:T(8,128)(2,1)}), bf16[128,128,256]{2,1,0:T(8,128)(2,1)}, u32[]{:S(2)}, u32[]{:S(2)}) async-start(bf16[128,128,256]{2,1,0:T(8,128)(2,1)} %select_select_fusion), calls=%async_computation.2 | async-start | bytes 16777216 | tf_op jit(solution)/shard_map/all_to_all | solution.py:41
  77.7 200.5 %all-gather.2.cloned.1.call-start = ((), (), s32[]{:S(2)}) async-start(), calls=%async_computation.3 | async-start | bytes 4227072 | tf_op jit(solution)/shard_map/all_gather | solution.py:24
  78.4 232.4 %reduce-scatter.2.cloned.1.call-start = ((), (), s32[]{:S(2)}) async-start(), calls=%async_computation.4 | async-start | bytes 327680 | tf_op jit(solution)/shard_map/reduce_scatter | solution.py:27
Sparse Core Ops, SparseCore 0:
  81.7 196.4 all-gather.1
  282.7 28.0 reduce-scatter.1
where the time goes:
time: 509 us; the launch traced here: 508 us
  waiting for transfers between devices  386 us (76%)
  other arithmetic  41.6 us (8%)
  starting transfers between devices  27.5 us (5%)
  matrix products  20.2 us (4%)
  local copies, waits for them, and re-layouts  18.5 us (4%)
  between operations  14.1 us (3%)
    all_gather x1, waiting for transfers between devices, body(): lax.all_gather(kv_weight, 'pool', axis=1, tiled=True)  198 us
    all_to_all x1, waiting for transfers between devices, body(): lax.all_to_all(reply, 'pool', split_axis=0, concat_axis=0, tiled=True)  145 us
    reduce_scatter x1, waiting for transfers between devices, body(): lax.psum_scatter(partial_kv.astype(jnp.bfloat16), 'tp', scatter_dimension...  28.1 us
    all_to_all x1, starting transfers between devices, body(): lax.all_to_all(request.reshape(npool, 1), 'pool', split_axis=0, concat_ax...  19.8 us
    eq x1, other arithmetic, body(): incoming == slot + 1  18.3 us
    all_to_all x1, waiting for transfers between devices, body(): lax.all_to_all(request.reshape(npool, 1), 'pool', split_axis=0, concat_ax...  14.4 us
  transfers between devices with their start and end apart: 4, of which 4 were waited for; matrix products, arithmetic and copies ran while one was open for 2% of the time, Pallas kernels for 0%

commit v1 on v0

--- a/solution.py
+++ b/solution.py
@@ -26,20 +26,14 @@
     )
     fresh = lax.psum_scatter(partial_kv.astype(jnp.bfloat16), "tp", scatter_dimension=1, tiled=True)
     wanted = retrieval[0]
-    blocks_dev = cache_table.shape[0]
     npool = lax.axis_size("pool")
-    owners = wanted // blocks_dev
-    local = wanted % blocks_dev
-    hits = (owners[:, None] == jnp.arange(npool, dtype=jnp.int32)[None, :]).astype(jnp.int32)
-    request = jnp.sum(hits * (local + 1)[:, None], axis=0)
-    incoming = lax.all_to_all(
-        request.reshape(npool, 1), "pool", split_axis=0, concat_axis=0, tiled=True
-    ).reshape(npool)
-    reply = jnp.zeros((npool,) + cache_table.shape[1:], jnp.bfloat16)
-    for slot in range(blocks_dev):
-        reply = jnp.where((incoming == slot + 1)[:, None, None], cache_table[slot][None], reply)
-    arrived = lax.all_to_all(reply, "pool", split_axis=0, concat_axis=0, tiled=True)
-    fetched = jnp.take(arrived, owners, axis=0)
+    by_token = lax.all_to_all(cache_table, "pool", split_axis=1, concat_axis=0, tiled=True)
+    by_token = by_token.reshape(by_token.shape[0], by_token.shape[2])
+    wanted_all = lax.all_gather(retrieval, "pool", axis=0, tiled=True)
+    reply = jnp.take(by_token, wanted_all, axis=0)
+    fetched = lax.all_to_all(
+        reply[:, :, None, :], "pool", split_axis=0, concat_axis=2, tiled=True
+    )[0]
     count = hidden_rows.shape[0]
     fetch_count = wanted.shape[0]
     group = QH // KVH

time: 509 us -> 441 us (0.87)
  the two profiles are of different devices: /device:TPU:16 before, /device:TPU:4 now
where the time goes in v1:
time: 441 us; the launch traced here: 440 us
  waiting for transfers between devices  214 us (49%)
  blocking collectives  92 us (21%)
  local copies, waits for them, and re-layouts  51.6 us (12%)
  starting transfers between devices  34 us (8%)
  matrix products  20.2 us (5%)
  between operations  14.2 us (3%)
  other arithmetic  14 us (3%)
    all_gather x1, waiting for transfers between devices, body(): lax.all_gather(kv_weight, 'pool', axis=1, tiled=True)  184 us
    all_gather x1, blocking collectives, body(): wanted_all = lax.all_gather(retrieval, 'pool', axis=0, tiled=True)  92 us
    gather x1, local copies, waits for them, and re-layouts, body(): reply = jnp.take(by_token, wanted_all, axis=0)  33.1 us
    reduce_scatter x1, waiting for transfers between devices, body(): lax.psum_scatter(partial_kv.astype(jnp.bfloat16), 'tp', scatter_dimension...  29 us
    all_to_all x1, starting transfers between devices, body(): lax.all_to_all(cache_table, 'pool', split_axis=1, concat_axis=0, tiled=True)  19.7 us
    all_to_all x1, starting transfers between devices, body(): lax.all_to_all(reply[:, :, None, :], 'pool', split_axis=0, concat_axis=2,...  14 us
  transfers between devices with their start and end apart: 4, of which 2 were waited for; matrix products, arithmetic and copies ran while one was open for 2% of the time, Pallas kernels for 0%

profile of v1, /device:TPU:4, one launch (start us, length us, event | category | flops | bytes accessed | tf_op | source)
XLA Modules:
  0.0 440.1 jit_solution(318980175920545042)
XLA Ops:
  7.2 0.0 copy-start
  7.2 2.2 copy.24
  9.4 19.7 %all-to-all-start = ((bf16[8,128,256]{2,0,1:T(8,128)(2,1)}), bf16[8,128,256]{2,0,1:T(8,128)(2,1)S(1)}, u32[]{:S(2)}, u32[]{:S(2)}) async-start(bf16[8,128,256]{2,0,1:T(8,128)(2,1)} %copy.24), calls=%async_computation.1 | async-start | bytes 1048576 | tf_op jit(solution)/shard_map/all_to_all | solution.py:30
  29.1 92.0 %all-gather = s32[128,1,64]{2,1,0:T(1,128)S(1)} all-gather(s32[1,1,64]{2,1,0:T(1,128)} %bitcast.77), channel_id=1, replica_groups=mesh['pool'=128,'tp'=4] {'pool'}, dimensions={0}, use_global_device_ids=true | all-gather | bytes 33024 | tf_op jit(solution)/shard_map/all_gather | solution.py:32
  121.1 0.1 reshape.108
  121.2 33.1 %gather_fusion = bf16[8192,256]{1,0:T(8,128)(2,1)} fusion(bf16[1024,256]{1,0:T(8,128)(2,1)S(1)} %bitcast.70, s32[8192]{0:T(1024)S(1)} %broadcast_clamp_fusion), kind=kCustom, calls=%fused_computation | custom fusion | bytes 8421376 | tf_op jit(solution)/shard_map/jit(_take)/gather | solution.py:33
  154.4 5.2 %broadcast_select_fusion = bf16[128,64,1,256]{3,1,2,0:T(8,128)(2,1)} fusion(bf16[128,64,1,256]{3,1,2,0:T(8,128)(2,1)} %bitcast.71, pred[128,64]{1,0:T(8,128)(4,1)S(1)} %compare_and_fusion), kind=kLoop, calls=%fused_computation.20 | loop fusion | flops 2097152 | bytes 8396800 | tf_op jit(solution)/shard_map/jit(_take)/select_n | solution.py:33
  159.6 14.0 %all-to-all-start.1 = ((bf16[128,64,1,256]{3,1,2,0:T(8,128)(2,1)}), bf16[128,64,1,256]{3,1,2,0:T(8,128)(2,1)}, u32[]{:S(2)}, u32[]{:S(2)}) async-start(bf16[128,64,1,256]{3,1,2,0:T(8,128)(2,1)} %broadcast_select_fusion), calls=%async_computation.2 | async-start | bytes 8388608 | tf_op jit(solution)/shard_map/all_to_all | solution.py:34
  173.6 0.0 all-gather.3.cloned.1.call-start
  173.7 0.7 all-gather.3.cloned.1.call-update
  174.4 0.2 reduce-scatter.2.cloned.1.call-start
  174.6 183.9 %all-gather.3.cloned.1.call-done = bf16[2048,1024]{0,1:T(8,128)(2,1)} async-done(((bf16[2048,8]{0,1:T(8,128)(2,1)}), bf16[2048,1024]{0,1:T(8,128)(2,1)}) %all-gather.3.cloned.1.call-update) | async-done | bytes 4194320 | tf_op jit(solution)/shard_map/all_gather | solution.py:24
  358.5 4.4 %convolution_convert_fusion = bf16[128,1024]{1,0:T(8,128)(2,1)} fusion(bf16[128,2048]{1,0:T(8,128)(2,1)S(1)} %copy-done, bf16[2048,1024]{0,1:T(8,128)(2,1)} %all-gather.3.cloned.1.call-done), kind=kOutput, calls=%fused_computation.23 | convolution fusion | flops 537001984 | bytes 4980736 | tf_op jit(solution)/shard_map/dot_general | solution.py:22
  362.9 0.0 reduce-scatter.2.cloned.1.call-update
  362.9 0.1 reshape_squeeze.6
  363.0 0.1 reshape_squeeze_reshape.3
  363.1 29.0 %reduce-scatter.2.cloned.1.call-done = bf16[128,256]{1,0:T(8,128)(2,1)} async-done(((bf16[128,1024]{1,0:T(8,128)(2,1)}), bf16[128,256]{1,0:T(8,128)(2,1)}) %reduce-scatter.2.cloned.1.call-update) | async-done | bytes 65552 | tf_op jit(solution)/shard_map/reduce_scatter | solution.py:27
  392.1 1.0 select_reduce_fusion
  393.1 0.1 fusion.11
  393.3 1.0 fusion.12
  394.3 6.5 %copy.26 = bf16[128,64,1,256]{3,0,1,2:T(8,128)(2,1)} copy(bf16[128,64,1,256]{3,1,2,0:T(8,128)(2,1)} %all-to-all-done.1) | data formatting | bytes 8388608 | tf_op jit(solution)/shard_map/all_to_all | solution.py:34
  400.8 31.4 %while.15 = (s32[]{:T(128)}, f32[1024]{0:T(1024)S(1)}, f32[1024]{0:T(1024)S(1)}, f32[1024,128]{1,0:T(8,128)S(1)}, s32[8,2,8]{2,0,1:T(8,128)S(1)}, /*index=5*/bf1...) while((s32[]{:T(128)}, f32[1024]{0:T(1024)S(1)}, ...), condition=%wide.region_7.8_spmd.clone, body=%wide.region_3.7_spmd.clone.sunk | while | flops 545550336 | bytes 15561037 | solution.py:80
  400.9 0.1 and_reduce_fusion.2
  400.9 1.1 dynamic-slice_bitcast_fusion.2
  402.0 0.7 fusion.38
  402.8 0.9 fusion.39
  403.7 1.0 convolution_add_fusion.2
  404.8 0.1 and_reduce_fusion.2
  404.9 1.1 dynamic-slice_bitcast_fusion.2
  405.9 0.7 fusion.38
  406.7 0.9 fusion.39
  407.7 1.0 convolution_add_fusion.2
  408.7 0.1 and_reduce_fusion.2
  408.8 1.1 dynamic-slice_bitcast_fusion.2
  409.9 0.7 fusion.38
  410.6 0.9 fusion.39
  411.6 1.0 convolution_add_fusion.2
  412.7 0.1 and_reduce_fusion.2
  412.7 1.1 dynamic-slice_bitcast_fusion.2
  413.8 0.7 fusion.38
  414.6 0.9 fusion.39
  415.5 1.0 convolution_add_fusion.2
  416.6 0.1 and_reduce_fusion.2
  416.7 1.1 dynamic-slice_bitcast_fusion.2
  417.7 0.7 fusion.38
  418.5 0.9 fusion.39
  419.5 1.0 convolution_add_fusion.2
  420.5 0.1 and_reduce_fusion.2
  420.6 1.1 dynamic-slice_bitcast_fusion.2
  421.7 0.7 fusion.38
  422.4 0.9 fusion.39
  423.4 1.0 convolution_add_fusion.2
  424.5 0.1 and_reduce_fusion.2
  424.5 1.1 dynamic-slice_bitcast_fusion.2
  425.6 0.7 fusion.38
  426.4 0.9 fusion.39
  427.3 1.0 convolution_add_fusion.2
  428.4 0.1 and_reduce_fusion.2
  428.5 1.1 dynamic-slice_bitcast_fusion.2
  429.5 0.7 fusion.38
  430.3 0.9 fusion.39
  431.3 1.0 convolution_add_fusion.2
  432.3 0.2 divide_convert_fusion
  432.5 0.8 convert_element_type.18
  (60 shorter events, 0.4 us)
Async XLA Ops:
  7.2 351.3 %copy-start = (bf16[128,2048]{1,0:T(8,128)(2,1)S(1)}, bf16[128,2048]{1,0:T(8,128)(2,1)}, u32[]{:S(2)}) copy-start(bf16[128,2048]{1,0:T(8,128)(2,1)} %param.8) | copy-start | bytes 1572868
  9.4 111.9 %all-to-all-start = ((bf16[8,128,256]{2,0,1:T(8,128)(2,1)}), bf16[8,128,256]{2,0,1:T(8,128)(2,1)S(1)}, u32[]{:S(2)}, u32[]{:S(2)}) async-start(bf16[8,128,256]{2,0,1:T(8,128)(2,1)} %copy.24), calls=%async_computation.1 | async-start | bytes 1048576 | tf_op jit(solution)/shard_map/all_to_all | solution.py:30
  159.6 234.7 %all-to-all-start.1 = ((bf16[128,64,1,256]{3,1,2,0:T(8,128)(2,1)}), bf16[128,64,1,256]{3,1,2,0:T(8,128)(2,1)}, u32[]{:S(2)}, u32[]{:S(2)}) async-start(bf16[128,64,1,256]{3,1,2,0:T(8,128)(2,1)} %broadcast_select_fusion), calls=%async_computation.2 | async-start | bytes 8388608 | tf_op jit(solution)/shard_map/all_to_all | solution.py:34
  173.6 189.3 %copy-start.2 = (s32[1,2,64]{2,1,0:T(2,128)S(1)}, s32[1,2,64]{2,1,0:T(2,128)}, u32[]{:S(2)}) copy-start(s32[1,2,64]{2,1,0:T(2,128)} %param.13) | copy-start | bytes 1540
  173.6 189.4 %copy-start.1 = (bf16[128,1024]{1,0:T(8,128)(2,1)S(1)}, bf16[128,1024]{1,0:T(8,128)(2,1)}, u32[]{:S(2)}) copy-start(bf16[128,1024]{1,0:T(8,128)(2,1)} %param.10) | copy-start | bytes 786436
  173.6 184.8 %all-gather.3.cloned.1.call-start = ((), (), s32[]{:S(2)}) async-start(), calls=%async_computation.3 | async-start | bytes 4227072 | tf_op jit(solution)/shard_map/all_gather | solution.py:24
  174.4 217.8 %reduce-scatter.2.cloned.1.call-start = ((), (), s32[]{:S(2)}) async-start(), calls=%async_computation.4 | async-start | bytes 327680 | tf_op jit(solution)/shard_map/reduce_scatter | solution.py:27
Sparse Core Ops, SparseCore 0:
  177.6 180.8 all-gather.2
  363.0 29.0 reduce-scatter.1

commit v2 on v1

v2 whole, which is shorter than its diff:
```python
import math

import jax
import jax.numpy as jnp
import numpy as np
from jax import lax
from jax.sharding import Mesh
from jax.sharding import PartitionSpec as P

HD = 128
QH = 32
KVH = 4
BLK = 128
RBLK = 64
CHIPS = ("px", "pz")
POOL = ("px", "pz", "pc")
ID_SPLIT = 32


def rows_by_keys(left, right):
    return lax.dot_general(
        left, right, (((1,), (1,)), ((), ())), preferred_element_type=jnp.float32
    )


def merge(carry, scores, mask, vals):
    top_now, total_now, numer_now = carry
    top_new = jnp.maximum(top_now, jnp.max(jnp.where(mask, scores, -1e30), axis=1))
    weights_now = jnp.where(mask, jnp.exp(scores - top_new[:, None]), 0.0)
    factor = jnp.exp(top_now - top_new)
    total_new = total_now * factor + jnp.sum(weights_now, axis=1)
    numer_new = numer_now * factor[:, None] + jnp.dot(
        weights_now.astype(jnp.bfloat16), vals, preferred_element_type=jnp.float32
    )
    return (top_new, total_new, numer_new)


def body(hidden_rows, kv_weight, queries, cache_table, retrieval, pattern):
    blocks_dev, blk, width = cache_table.shape
    npool = lax.axis_size(POOL)
    fetch_count = retrieval.shape[1]
    wanted = retrieval[0]
    id_row = jnp.concatenate(
        [
            (wanted // ID_SPLIT).astype(jnp.bfloat16),
            (wanted % ID_SPLIT).astype(jnp.bfloat16),
            jnp.zeros((width - 2 * fetch_count,), jnp.bfloat16),
        ]
    )
    id_block = jnp.broadcast_to(id_row[None, None, :], (1, blk, width))
    outgoing = jnp.concatenate([cache_table, id_block], axis=0)
    by_token = lax.all_to_all(outgoing, POOL, split_axis=1, concat_axis=0, tiled=True)
    by_token = by_token.reshape(npool, blocks_dev + 1, width)
    table = by_token[:, :blocks_dev].reshape(npool * blocks_dev, width)
    id_rows = by_token[:, blocks_dev].astype(jnp.float32)
    wanted_all = (
        id_rows[:, :fetch_count] * ID_SPLIT + id_rows[:, fetch_count : 2 * fetch_count]
    ).astype(jnp.int32)
    picks = (
        wanted_all.reshape(-1)[:, None]
        == jnp.arange(npool * blocks_dev, dtype=jnp.int32)[None, :]
    ).astype(jnp.bfloat16)
    reply = jnp.dot(picks, table, preferred_element_type=jnp.float32).astype(jnp.bfloat16)
    reply = reply.reshape(npool, fetch_count, 1, width)
    fetched = lax.all_to_all(reply, POOL, split_axis=0, concat_axis=2, tiled=True)[0]

    w_chip = lax.all_gather(kv_weight, CHIPS, axis=1, tiled=True)
    w_all = lax.all_gather(w_chip, "pc", axis=1, tiled=True)
    partial_kv = jnp.dot(hidden_rows, w_all, preferred_element_type=jnp.float32)
    ncore = lax.axis_size("pc")
    nchip = npool // ncore
    cols = kv_weight.shape[1]
    partial_kv = (
        partial_kv.reshape(-1, ncore, nchip, cols)
        .transpose(0, 2, 1, 3)
        .reshape(partial_kv.shape[0], -1)
    )
    fresh = lax.psum_scatter(partial_kv.astype(jnp.bfloat16), "tp", scatter_dimension=1, tiled=True)

    count = hidden_rows.shape[0]
    group = QH // KVH
    scale = float(HD) ** (-0.5)
    local_heads = fresh.shape[1] // (2 * HD)
    per_step = math.gcd(fetch_count, 8)
    steps_count = fetch_count // per_step
    grouped = fetched.reshape(steps_count, per_step * BLK, width)
    pat_steps = jnp.transpose(
        pattern[0].reshape(pattern.shape[1], steps_count, per_step), (1, 0, 2)
    )
    token_of_row = jnp.arange(count * group) // group
    block_of_row = token_of_row // RBLK
    row_blocks = block_of_row[:, None, None] == jnp.arange(pattern.shape[1])[None, :, None]
    near_mask = token_of_row[:, None] >= jnp.arange(count)[None, :]
    q_heads = queries.reshape(count, local_heads, group * HD)
    q_rows = q_heads[:, 0].reshape(count * group, HD)
    rows = count * group
    start = (
        jnp.full((rows,), -1e30, jnp.float32),
        jnp.zeros((rows,), jnp.float32),
        jnp.zeros((rows, HD), jnp.float32),
    )

    def visit(carry, items):
        block_rows, pat_now = items
        keys = block_rows[:, 0:HD]
        vals = block_rows[:, HD : 2 * HD]
        scores = rows_by_keys(q_rows, keys) * scale
        row_pat = jnp.any(row_blocks & (pat_now[None] != 0), axis=1)
        mask = jnp.repeat(row_pat, BLK, axis=1)
        return (merge(carry, scores, mask, vals), None)

    carry, unused = lax.scan(visit, start, (grouped, pat_steps))
    near_keys = fresh[:, 0:HD]
    near_vals = fresh[:, HD : 2 * HD]
    near_scores = rows_by_keys(q_rows, near_keys) * scale
    top, total, numer = merge(carry, near_scores, near_mask, near_vals)
    results = (numer / total[:, None]).reshape(count, group * HD)
    attended = results.astype(jnp.bfloat16)
    return (attended, fresh)


def solution(mesh):
    npool = mesh.shape["pool"]
    ntp = mesh.shape["tp"]
    nx = 4 if npool % 8 == 0 else 1
    fine = Mesh(
        np.asarray(mesh.devices).reshape(nx, npool // (2 * nx), 2, ntp),
        ("px", "pz", "pc", "tp"),
    )
    placed = (
        P(POOL, "tp"),
        P("tp", POOL),
        P(POOL, "tp"),
        P(POOL, None, "tp"),
        P(POOL, None),
        P(POOL, None, None),
    )
    return jax.shard_map(
        body,
        mesh=fine,
        in_specs=placed,
        out_specs=(P(POOL, "tp"), P(POOL, "tp")),
        check_vma=False,
    )
```

time: 441 us -> 429 us (0.973)
  the two profiles are of different devices: /device:TPU:4 before, /device:TPU:2 now
where the time goes in v2:
time: 429 us; the launch traced here: 428 us
  waiting for transfers between devices  241 us (56%)
  blocking collectives  75.4 us (18%)
  matrix products  43 us (10%)
  other arithmetic  27.1 us (6%)
  local copies, waits for them, and re-layouts  20.2 us (5%)
  between operations  13.9 us (3%)
  starting transfers between devices  7.49 us (2%)
    all_gather x1, waiting for transfers between devices, body(): w_chip = lax.all_gather(kv_weight, CHIPS, axis=1, tiled=True)  184 us
    all_to_all x1, blocking collectives, body(): lax.all_to_all(outgoing, POOL, split_axis=1, concat_axis=0, tiled=True)  75.4 us
    reduce_scatter x1, waiting for transfers between devices, body(): lax.psum_scatter(partial_kv.astype(jnp.bfloat16), 'tp', scatter_dimension...  29.5 us
    all_gather x1, waiting for transfers between devices, body(): w_all = lax.all_gather(w_chip, 'pc', axis=1, tiled=True)  26.7 us
    convert_element_type x8, other arithmetic, merge(): weights_now.astype(jnp.bfloat16)  24.9 us
    dot_general x9, matrix products, rows_by_keys(): lax.dot_general(left, right, (((1,), (1,)), ((), ())), preferred_element_...  22.5 us
    squeeze x8, local copies, waits for them, and re-layouts, body(): carry, unused = lax.scan(visit, start, (grouped, pat_steps))  8.61 us
  transfers between devices with their start and end apart: 4, of which 3 were waited for; matrix products, arithmetic and copies ran while one was open for 2% of the time, Pallas kernels for 0%

profile of v2, /device:TPU:2, one launch (start us, length us, event | category | flops | bytes accessed | tf_op | source)
XLA Modules:
  0.0 428.3 jit_solution(18046132877166488671)
XLA Ops:
  7.2 0.7 fusion.31
  7.9 1.3 copy.33
  9.2 0.1 pad_maximum_fusion.1
  9.4 0.2 pad_maximum_fusion
  9.6 75.4 %all_to_all.30 = bf16[9,128,256]{2,0,1:T(8,128)(2,1)S(1)} all-to-all(bf16[9,128,256]{2,0,1:T(8,128)(2,1)S(1)} %pad_maximum_fusion), channel_id=1, replica_groups=mesh['px'=4,'pz'=16,'pc'=2,'tp'=4] {'px','pz','pc'}, dimensions={1} | all-to-all | bytes 1179648 | tf_op jit(solution)/shard_map/all_to_all | solution.py:52
  85.1 0.1 fusion.22
  85.3 8.3 %fusion.12 = bf16[8192,256]{1,0:T(8,128)(2,1)} fusion(s32[8192]{0:T(1024)S(1)} %eq.41, bf16[128,9,256]{2,1,0:T(8,128)(2,1)S(1)} %bitcast.98), kind=kOutput, calls=%fused_computation.25 | convolution fusion | flops 4305453056 | bytes 4751360 | tf_op jit(solution)/shard_map/dot_general | solution.py:63
  93.6 7.2 %all-to-all-start.1 = ((bf16[128,64,1,256]{3,1,2,0:T(8,128)(2,1)}), bf16[128,64,1,256]{3,1,2,0:T(8,128)(2,1)}, u32[]{:S(2)}, u32[]{:S(2)}) async-start(bf16[128,64,1,256]{3,1,2,0:T(8,128)(2,1)} %bitcast.96), calls=%async_computation.1 | async-start | bytes 8388608 | tf_op jit(solution)/shard_map/all_to_all | solution.py:65
  100.8 0.7 all-gather.3.cloned.1.call-update
  101.6 183.7 %all-gather.3.cloned.1.call-done = bf16[2048,512]{0,1:T(8,128)(2,1)} async-done(((bf16[2048,8]{0,1:T(8,128)(2,1)}), bf16[2048,512]{0,1:T(8,128)(2,1)}) %all-gather.3.cloned.1.call-update) | async-done | bytes 2097168 | tf_op jit(solution)/shard_map/all_gather | solution.py:67
  285.3 0.2 reduce-scatter.2.cloned.1.call-start
  285.5 26.7 %all-gather.5.cloned.1.call-done = bf16[2048,1024]{0,1:T(8,128)(2,1)} async-done(((bf16[2048,512]{0,1:T(8,128)(2,1)}), bf16[2048,1024]{0,1:T(8,128)(2,1)}) %all-gather.5.cloned.1.call-update) | async-done | bytes 4194320 | tf_op jit(solution)/shard_map/all_gather | solution.py:68
  312.2 3.7 convolution_convert_fusion
  315.9 0.2 copy.37
  316.1 0.8 copy.38
  316.9 0.1 reshape_squeeze_reshape.3
  317.2 29.5 %reduce-scatter.2.cloned.1.call-done = bf16[128,256]{0,1:T(8,128)(2,1)} async-done(((bf16[128,1024]{0,1:T(8,128)(2,1)}), bf16[128,256]{0,1:T(8,128)(2,1)}) %reduce-scatter.2.cloned.1.call-update) | async-done | bytes 65552 | tf_op jit(solution)/shard_map/reduce_scatter | solution.py:78
  346.7 1.6 copy.39
  348.2 1.0 select_reduce_fusion
  349.3 6.5 %copy.35 = bf16[128,64,1,256]{3,0,1,2:T(8,128)(2,1)} copy(bf16[128,64,1,256]{3,1,2,0:T(8,128)(2,1)} %all-to-all-done.1) | data formatting | bytes 8388608 | tf_op jit(solution)/shard_map/all_to_all | solution.py:65
  355.8 64.5 %while.15 = (s32[]{:T(128)}, f32[1024]{0:T(1024)S(1)}, f32[1024]{0:T(1024)S(1)}, f32[1024,128]{1,0:T(8,128)S(1)}, s32[8,2,8]{2,0,1:T(8,128)S(1)}, /*index=5*/bf1...) while((s32[]{:T(128)}, f32[1024]{0:T(1024)S(1)}, ...), condition=%wide.region_4.5_spmd.clone, body=%wide.region_0.4_spmd.clone.sunk | while | flops 545684480 | bytes 15561049 | solution.py:112
  355.8 0.1 and_reduce_fusion.2
  355.9 1.1 dynamic-slice_bitcast_fusion.2
  357.0 2.7 fusion.47
  359.7 3.1 fusion.48
  362.8 1.0 convolution_add_fusion.3
  363.9 0.1 and_reduce_fusion.2
  363.9 1.1 dynamic-slice_bitcast_fusion.2
  365.0 2.7 fusion.47
  367.7 3.1 fusion.48
  370.9 1.0 convolution_add_fusion.3
  371.9 0.1 and_reduce_fusion.2
  372.0 1.1 dynamic-slice_bitcast_fusion.2
  373.1 2.7 fusion.47
  375.8 3.1 fusion.48
  378.9 1.0 convolution_add_fusion.3
  380.0 0.1 and_reduce_fusion.2
  380.1 1.1 dynamic-slice_bitcast_fusion.2
  381.2 2.7 fusion.47
  383.9 3.1 fusion.48
  387.0 1.0 convolution_add_fusion.3
  388.1 0.1 and_reduce_fusion.2
  388.1 1.1 dynamic-slice_bitcast_fusion.2
  389.2 2.7 fusion.47
  391.9 3.1 fusion.48
  395.1 1.0 convolution_add_fusion.3
  396.1 0.1 and_reduce_fusion.2
  396.2 1.1 dynamic-slice_bitcast_fusion.2
  397.3 2.7 fusion.47
  400.0 3.1 fusion.48
  403.1 1.0 convolution_add_fusion.3
  404.2 0.1 and_reduce_fusion.2
  404.3 1.1 dynamic-slice_bitcast_fusion.2
  405.4 2.7 fusion.47
  408.1 3.1 fusion.48
  411.2 1.0 convolution_add_fusion.3
  412.3 0.1 and_reduce_fusion.2
  412.3 1.1 dynamic-slice_bitcast_fusion.2
  413.4 2.7 fusion.47
  416.1 3.1 fusion.48
  419.3 1.0 convolution_add_fusion.3
  420.3 0.1 fusion.16
  420.4 0.5 fusion.15
  420.9 0.8 convert_element_type.55
  (74 shorter events, 0.8 us)
Async XLA Ops:
  7.2 305.1 %copy-start = (bf16[128,2048]{1,0:T(8,128)(2,1)S(1)}, bf16[128,2048]{1,0:T(8,128)(2,1)}, u32[]{:S(2)}) copy-start(bf16[128,2048]{1,0:T(8,128)(2,1)} %param.8) | copy-start | bytes 1572868
  93.6 255.6 %all-to-all-start.1 = ((bf16[128,64,1,256]{3,1,2,0:T(8,128)(2,1)}), bf16[128,64,1,256]{3,1,2,0:T(8,128)(2,1)}, u32[]{:S(2)}, u32[]{:S(2)}) async-start(bf16[128,64,1,256]{3,1,2,0:T(8,128)(2,1)} %bitcast.96), calls=%async_computation.1 | async-start | bytes 8388608 | tf_op jit(solution)/shard_map/all_to_all | solution.py:65
  100.8 184.5 %all-gather.3.cloned.1.call-start = ((), (), s32[]{:S(2)}) async-start(), calls=%async_computation.3 | async-start | bytes 2129920 | tf_op jit(solution)/shard_map/all_gather | solution.py:67
  101.5 210.7 %all-gather.5.cloned.1.call-start = ((), (), s32[]{:S(2)}) async-start(), calls=%async_computation.4 | async-start | bytes 6291456 | tf_op jit(solution)/shard_map/all_gather | solution.py:68
  285.3 31.6 %copy-start.1 = (bf16[128,1024]{1,0:T(8,128)(2,1)S(1)}, bf16[128,1024]{1,0:T(8,128)(2,1)}, u32[]{:S(2)}) copy-start(bf16[128,1024]{1,0:T(8,128)(2,1)} %param.10) | copy-start | bytes 786436
  285.3 31.8 %copy-start.3 = (s32[1,2,64]{2,1,0:T(2,128)S(1)}, s32[1,2,64]{2,1,0:T(2,128)}, u32[]{:S(2)}) copy-start(s32[1,2,64]{2,1,0:T(2,128)} %param.13) | copy-start | bytes 1540
  285.3 61.4 %reduce-scatter.2.cloned.1.call-start = ((), (), s32[]{:S(2)}) async-start(), calls=%async_computation.5 | async-start | bytes 327680 | tf_op jit(solution)/shard_map/reduce_scatter | solution.py:78
  355.8 64.7 %copy-start.2 = (bf16[128,256]{0,1:T(8,128)(2,1)S(1)}, bf16[128,256]{0,1:T(8,128)(2,1)}, u32[]{:S(2)}) copy-start(bf16[128,256]{0,1:T(8,128)(2,1)} %reduce-scatter.2.cloned.1.call-done) | copy-start | bytes 196612
Sparse Core Ops, SparseCore 0:
  104.6 180.6 all-gather.2
  287.4 24.8 all-gather.4
  317.0 29.6 reduce-scatter.1

commit v3 on v2

--- a/solution.py
+++ b/solution.py
@@ -56,15 +56,16 @@
     wanted_all = (
         id_rows[:, :fetch_count] * ID_SPLIT + id_rows[:, fetch_count : 2 * fetch_count]
     ).astype(jnp.int32)
+    w_chip = lax.all_gather(kv_weight, CHIPS, axis=1, tiled=True)
     picks = (
         wanted_all.reshape(-1)[:, None]
         == jnp.arange(npool * blocks_dev, dtype=jnp.int32)[None, :]
     ).astype(jnp.bfloat16)
     reply = jnp.dot(picks, table, preferred_element_type=jnp.float32).astype(jnp.bfloat16)
     reply = reply.reshape(npool, fetch_count, 1, width)
+    reply, w_chip = lax.optimization_barrier((reply, w_chip))
     fetched = lax.all_to_all(reply, POOL, split_axis=0, concat_axis=2, tiled=True)[0]
 
-    w_chip = lax.all_gather(kv_weight, CHIPS, axis=1, tiled=True)
     w_all = lax.all_gather(w_chip, "pc", axis=1, tiled=True)
     partial_kv = jnp.dot(hidden_rows, w_all, preferred_element_type=jnp.float32)
     ncore = lax.axis_size("pc")
@@ -93,12 +94,13 @@
     near_mask = token_of_row[:, None] >= jnp.arange(count)[None, :]
     q_heads = queries.reshape(count, local_heads, group * HD)
     q_rows = q_heads[:, 0].reshape(count * group, HD)
-    rows = count * group
-    start = (
-        jnp.full((rows,), -1e30, jnp.float32),
-        jnp.zeros((rows,), jnp.float32),
-        jnp.zeros((rows, HD), jnp.float32),
-    )
+    near_keys = fresh[:, 0:HD]
+    near_vals = fresh[:, HD : 2 * HD]
+    near_scores = rows_by_keys(q_rows, near_keys) * scale
+    top = jnp.max(jnp.where(near_mask, near_scores, -1e30), axis=1)
+    weights = jnp.where(near_mask, jnp.exp(near_scores - top[:, None]), 0.0)
+    total = jnp.sum(weights, axis=1)
+    numer = jnp.dot(weights.astype(jnp.bfloat16), near_vals, preferred_element_type=jnp.float32)
 
     def visit(carry, items):
         block_rows, pat_now = items
@@ -109,11 +111,7 @@
         mask = jnp.repeat(row_pat, BLK, axis=1)
         return (merge(carry, scores, mask, vals), None)
 
-    carry, unused = lax.scan(visit, start, (grouped, pat_steps))
-    near_keys = fresh[:, 0:HD]
-    near_vals = fresh[:, HD : 2 * HD]
-    near_scores = rows_by_keys(q_rows, near_keys) * scale
-    top, total, numer = merge(carry, near_scores, near_mask, near_vals)
+    (top, total, numer), unused = lax.scan(visit, (top, total, numer), (grouped, pat_steps))
     results = (numer / total[:, None]).reshape(count, group * HD)
     attended = results.astype(jnp.bfloat16)
     return (attended, fresh)

time: 429 us -> 409 us (0.953)
  the two profiles are of different devices: /device:TPU:2 before, /device:TPU:34 now
where the time goes in v3:
time: 409 us; the launch traced here: 408 us
  waiting for transfers between devices  246 us (60%)
  blocking collectives  76.9 us (19%)
  matrix products  27.6 us (7%)
  local copies, waits for them, and re-layouts  20.1 us (5%)
  between operations  13.9 us (3%)
  starting transfers between devices  13.2 us (3%)
  other arithmetic  10.1 us (2%)
    all_to_all x1, waiting for transfers between devices, body(): lax.all_to_all(reply, POOL, split_axis=0, concat_axis=2, tiled=True)[0]  123 us
    all_to_all x1, blocking collectives, body(): lax.all_to_all(outgoing, POOL, split_axis=1, concat_axis=0, tiled=True)  76.9 us
    all_gather x1, waiting for transfers between devices, body(): w_chip = lax.all_gather(kv_weight, CHIPS, axis=1, tiled=True)  64.9 us
    reduce_scatter x1, waiting for transfers between devices, body(): lax.psum_scatter(partial_kv.astype(jnp.bfloat16), 'tp', scatter_dimension...  29.5 us
    all_gather x1, waiting for transfers between devices, body(): w_all = lax.all_gather(w_chip, 'pc', axis=1, tiled=True)  27.1 us
    all_to_all x1, starting transfers between devices, body(): lax.all_to_all(reply, POOL, split_axis=0, concat_axis=2, tiled=True)[0]  12.9 us
    squeeze x8, local copies, waits for them, and re-layouts, body(): lax.scan(visit, (top, total, numer), (grouped, pat_steps))  8.61 us
    dot_general x1, matrix products, body(): jnp.dot(picks, table, preferred_element_type=jnp.float32)  8.35 us
  transfers between devices with their start and end apart: 4, of which 4 were waited for; matrix products, arithmetic and copies ran while one was open for 5% of the time, Pallas kernels for 0%

profile of v3, /device:TPU:34, one launch (start us, length us, event | category | flops | bytes accessed | tf_op | source)
XLA Modules:
  0.0 408.3 jit_solution(17764476043358587831)
XLA Ops:
  7.2 0.7 all-gather.3.cloned.1.call-update
  7.9 1.3 copy.30
  9.2 0.7 fusion.29
  10.1 0.2 pad_maximum_fusion
  10.3 76.9 %all_to_all.30 = bf16[9,128,256]{2,0,1:T(8,128)(2,1)S(1)} all-to-all(bf16[9,128,256]{2,0,1:T(8,128)(2,1)S(1)} %pad_maximum_fusion), channel_id=1, replica_groups=mesh['px'=4,'pz'=16,'pc'=2,'tp'=4] {'px','pz','pc'}, dimensions={1} | all-to-all | bytes 1179648 | tf_op jit(solution)/shard_map/all_to_all | solution.py:52
  87.2 0.1 fusion.20
  87.4 8.4 %fusion.11 = bf16[8192,256]{1,0:T(8,128)(2,1)} fusion(s32[8192]{0:T(1024)S(1)} %eq.38, bf16[128,9,256]{2,1,0:T(8,128)(2,1)S(1)} %bitcast.99), kind=kOutput, calls=%fused_computation.22 | convolution fusion | flops 4305453056 | bytes 4751360 | tf_op jit(solution)/shard_map/dot_general | solution.py:64
  95.7 64.9 %all-gather.3.cloned.1.call-done = bf16[2048,512]{0,1:T(8,128)(2,1)} async-done(((bf16[2048,8]{0,1:T(8,128)(2,1)}), bf16[2048,512]{0,1:T(8,128)(2,1)}) %all-gather.3.cloned.1.call-update) | async-done | bytes 2097168 | tf_op jit(solution)/shard_map/all_gather | solution.py:59
  160.6 12.9 %all-to-all-start.1 = ((bf16[128,64,1,256]{3,1,2,0:T(8,128)(2,1)}), bf16[128,64,1,256]{3,1,2,0:T(8,128)(2,1)}, u32[]{:S(2)}, u32[]{:S(2)}) async-start(bf16[128,64,1,256]{3,1,2,0:T(8,128)(2,1)} %bitcast.97), calls=%async_computation.2 | async-start | bytes 8388608 | tf_op jit(solution)/shard_map/all_to_all | solution.py:67
  173.6 0.7 all-gather.5.cloned.1.call-update
  174.3 0.2 reduce-scatter.2.cloned.1.call-start
  174.5 27.1 %all-gather.5.cloned.1.call-done = bf16[2048,1024]{0,1:T(8,128)(2,1)} async-done(((bf16[2048,512]{0,1:T(8,128)(2,1)}), bf16[2048,1024]{0,1:T(8,128)(2,1)}) %all-gather.5.cloned.1.call-update) | async-done | bytes 4194320 | tf_op jit(solution)/shard_map/all_gather | solution.py:69
  201.7 3.4 convolution_convert_fusion
  205.1 0.7 copy.31
  206.0 0.1 reshape_squeeze_reshape.3
  206.1 29.5 %reduce-scatter.2.cloned.1.call-done = bf16[128,256]{0,1:T(8,128)(2,1)} async-done(((bf16[128,1024]{0,1:T(8,128)(2,1)}), bf16[128,256]{0,1:T(8,128)(2,1)}) %reduce-scatter.2.cloned.1.call-update) | async-done | bytes 65552 | tf_op jit(solution)/shard_map/reduce_scatter | solution.py:79
  235.7 1.6 copy.35
  237.2 1.0 select_reduce_fusion
  238.3 0.1 fusion.14
  238.4 1.0 fusion.15
  239.4 123.1 %all-to-all-done.1 = bf16[128,64,1,256]{3,1,2,0:T(8,128)(2,1)} async-done(((bf16[128,64,1,256]{3,1,2,0:T(8,128)(2,1)}), bf16[128,64,1,256]{3,1,2,0:T(8,128)(2,1)}, u32[]{:S(2)}, u32[]{:S(2)}) %all-to-all-start.1) | async-done | bytes 4194336 | tf_op jit(solution)/shard_map/all_to_all | solution.py:67
  362.5 6.5 %copy.33 = bf16[128,64,1,256]{3,0,1,2:T(8,128)(2,1)} copy(bf16[128,64,1,256]{3,1,2,0:T(8,128)(2,1)} %all-to-all-done.1) | data formatting | bytes 8388608 | tf_op jit(solution)/shard_map/all_to_all | solution.py:67
  369.1 31.7 %while.15 = (s32[]{:T(128)}, f32[1024]{0:T(1024)S(1)}, f32[1024]{0:T(1024)S(1)}, f32[1024,128]{1,0:T(8,128)S(1)}, s32[8,2,8]{2,0,1:T(8,128)S(1)}, /*index=5*/bf1...) while((s32[]{:T(128)}, f32[1024]{0:T(1024)S(1)}, ...), condition=%wide.region_7.8_spmd.clone, body=%wide.region_3.7_spmd.clone.sunk | while | flops 545550336 | bytes 15561037 | solution.py:114
  369.1 0.1 and_reduce_fusion.2
  369.2 1.1 dynamic-slice_bitcast_fusion.2
  370.2 0.7 fusion.44
  371.0 1.0 fusion.45
  372.0 1.0 convolution_add_fusion.2
  373.0 0.1 and_reduce_fusion.2
  373.1 1.1 dynamic-slice_bitcast_fusion.2
  374.2 0.7 fusion.44
  375.0 1.0 fusion.45
  376.0 1.0 convolution_add_fusion.2
  377.0 0.1 and_reduce_fusion.2
  377.1 1.1 dynamic-slice_bitcast_fusion.2
  378.2 0.7 fusion.44
  378.9 1.0 fusion.45
  379.9 1.0 convolution_add_fusion.2
  381.0 0.1 and_reduce_fusion.2
  381.1 1.1 dynamic-slice_bitcast_fusion.2
  382.1 0.7 fusion.44
  382.9 1.0 fusion.45
  383.9 1.0 convolution_add_fusion.2
  384.9 0.1 and_reduce_fusion.2
  385.0 1.1 dynamic-slice_bitcast_fusion.2
  386.1 0.7 fusion.44
  386.9 1.0 fusion.45
  387.8 1.0 convolution_add_fusion.2
  388.9 0.1 and_reduce_fusion.2
  389.0 1.1 dynamic-slice_bitcast_fusion.2
  390.1 0.7 fusion.44
  390.8 1.0 fusion.45
  391.8 1.0 convolution_add_fusion.2
  392.9 0.1 and_reduce_fusion.2
  392.9 1.1 dynamic-slice_bitcast_fusion.2
  394.0 0.7 fusion.44
  394.8 1.0 fusion.45
  395.8 1.0 convolution_add_fusion.2
  396.9 1.1 dynamic-slice_bitcast_fusion.2
  398.0 0.7 fusion.44
  398.7 1.0 fusion.45
  399.7 1.0 convolution_add_fusion.2
  400.7 0.2 divide_convert_fusion
  400.9 0.8 convert_element_type.59
  (67 shorter events, 0.9 us)
Async XLA Ops:
  7.2 194.5 %copy-start = (bf16[128,2048]{1,0:T(8,128)(2,1)S(1)}, bf16[128,2048]{1,0:T(8,128)(2,1)}, u32[]{:S(2)}) copy-start(bf16[128,2048]{1,0:T(8,128)(2,1)} %param.8) | copy-start | bytes 1572868
  7.2 153.4 %all-gather.3.cloned.1.call-start = ((), (), s32[]{:S(2)}) async-start(), calls=%async_computation.3 | async-start | bytes 2129920 | tf_op jit(solution)/shard_map/all_gather | solution.py:59
  160.6 201.9 %all-to-all-start.1 = ((bf16[128,64,1,256]{3,1,2,0:T(8,128)(2,1)}), bf16[128,64,1,256]{3,1,2,0:T(8,128)(2,1)}, u32[]{:S(2)}, u32[]{:S(2)}) async-start(bf16[128,64,1,256]{3,1,2,0:T(8,128)(2,1)} %bitcast.97), calls=%async_computation.2 | async-start | bytes 8388608 | tf_op jit(solution)/shard_map/all_to_all | solution.py:67
  173.5 32.4 %copy-start.2 = (s32[1,2,64]{2,1,0:T(2,128)S(1)}, s32[1,2,64]{2,1,0:T(2,128)}, u32[]{:S(2)}) copy-start(s32[1,2,64]{2,1,0:T(2,128)} %param.13) | copy-start | bytes 1540
  173.6 32.4 %copy-start.1 = (bf16[128,1024]{1,0:T(8,128)(2,1)S(1)}, bf16[128,1024]{1,0:T(8,128)(2,1)}, u32[]{:S(2)}) copy-start(bf16[128,1024]{1,0:T(8,128)(2,1)} %param.10) | copy-start | bytes 786436
  173.6 28.1 %all-gather.5.cloned.1.call-start = ((), (), s32[]{:S(2)}) async-start(), calls=%async_computation.4 | async-start | bytes 6291456 | tf_op jit(solution)/shard_map/all_gather | solution.py:69
  174.3 61.3 %reduce-scatter.2.cloned.1.call-start = ((), (), s32[]{:S(2)}) async-start(), calls=%async_computation.5 | async-start | bytes 327680 | tf_op jit(solution)/shard_map/reduce_scatter | solution.py:79
Sparse Core Ops, SparseCore 0:
  11.0 149.6 all-gather.2
  176.5 25.1 all-gather.4
  206.0 29.6 reduce-scatter.1

commit v4 on v3

--- a/solution.py
+++ b/solution.py
@@ -12,7 +12,6 @@
 KVH = 4
 BLK = 128
 RBLK = 64
-CHIPS = ("px", "pz")
 POOL = ("px", "pz", "pc")
 ID_SPLIT = 32
 
@@ -56,7 +55,8 @@
     wanted_all = (
         id_rows[:, :fetch_count] * ID_SPLIT + id_rows[:, fetch_count : 2 * fetch_count]
     ).astype(jnp.int32)
-    w_chip = lax.all_gather(kv_weight, CHIPS, axis=1, tiled=True)
+    w_chip = lax.all_gather(kv_weight, "pz", axis=1, tiled=True)
+    w_chip = lax.all_gather(w_chip, "px", axis=1, tiled=True)
     picks = (
         wanted_all.reshape(-1)[:, None]
         == jnp.arange(npool * blocks_dev, dtype=jnp.int32)[None, :]
@@ -64,7 +64,7 @@
     reply = jnp.dot(picks, table, preferred_element_type=jnp.float32).astype(jnp.bfloat16)
     reply = reply.reshape(npool, fetch_count, 1, width)
     reply, w_chip = lax.optimization_barrier((reply, w_chip))
-    fetched = lax.all_to_all(reply, POOL, split_axis=0, concat_axis=2, tiled=True)[0]
+    fetched = lax.all_to_all(reply, POOL, split_axis=0, concat_axis=0, tiled=True)
 
     w_all = lax.all_gather(w_chip, "pc", axis=1, tiled=True)
     partial_kv = jnp.dot(hidden_rows, w_all, preferred_element_type=jnp.float32)
@@ -82,15 +82,13 @@
     group = QH // KVH
     scale = float(HD) ** (-0.5)
     local_heads = fresh.shape[1] // (2 * HD)
-    per_step = math.gcd(fetch_count, 8)
-    steps_count = fetch_count // per_step
-    grouped = fetched.reshape(steps_count, per_step * BLK, width)
-    pat_steps = jnp.transpose(
-        pattern[0].reshape(pattern.shape[1], steps_count, per_step), (1, 0, 2)
-    )
+    tokens_step = BLK // math.gcd(BLK, 8)
+    steps_count = BLK // tokens_step
+    grouped = fetched.reshape(steps_count, tokens_step * fetch_count, width)
     token_of_row = jnp.arange(count * group) // group
     block_of_row = token_of_row // RBLK
-    row_blocks = block_of_row[:, None, None] == jnp.arange(pattern.shape[1])[None, :, None]
+    row_pat = jnp.take(pattern[0] != 0, block_of_row, axis=0)
+    mask = jnp.tile(row_pat, (1, tokens_step))
     near_mask = token_of_row[:, None] >= jnp.arange(count)[None, :]
     q_heads = queries.reshape(count, local_heads, group * HD)
     q_rows = q_heads[:, 0].reshape(count * group, HD)
@@ -102,16 +100,13 @@
     total = jnp.sum(weights, axis=1)
     numer = jnp.dot(weights.astype(jnp.bfloat16), near_vals, preferred_element_type=jnp.float32)
 
-    def visit(carry, items):
-        block_rows, pat_now = items
+    def visit(carry, block_rows):
         keys = block_rows[:, 0:HD]
         vals = block_rows[:, HD : 2 * HD]
         scores = rows_by_keys(q_rows, keys) * scale
-        row_pat = jnp.any(row_blocks & (pat_now[None] != 0), axis=1)
-        mask = jnp.repeat(row_pat, BLK, axis=1)
         return (merge(carry, scores, mask, vals), None)
 
-    (top, total, numer), unused = lax.scan(visit, (top, total, numer), (grouped, pat_steps))
+    (top, total, numer), unused = lax.scan(visit, (top, total, numer), grouped)
     results = (numer / total[:, None]).reshape(count, group * HD)
     attended = results.astype(jnp.bfloat16)
     return (attended, fresh)

time: 409 us -> 388 us (0.949)
  waiting for transfers between devices: 246 us -> 207 us
  starting transfers between devices: 13.2 us -> 35.9 us
    all_to_all x1 -> x0, blocking collectives: 76.9 us -> none  [body(): lax.all_to_all(outgoing, POOL, split_axis=1, concat_axis=0, tiled=True)]
    all_gather x0 -> x1, blocking collectives: none -> 74.5 us  [body(): w_chip = lax.all_gather(kv_weight, 'pz', axis=1, tiled=True)]
    all_gather x1, waiting for transfers between devices: 64.9 us -> 30.1 us  [body(): w_chip = lax.all_gather(w_chip, 'px', axis=1, tiled=True)]
    all_to_all x1 -> x2, starting transfers between devices: 12.9 us -> 35.8 us  [the longest x1 19.1 us: body(): lax.all_to_all(outgoing, POOL, split_axis=1, concat_axis=0, tiled=True)]
    all_to_all x1 -> x0, local copies, waits for them, and re-layouts: 6.53 us -> none  [body(): lax.all_to_all(reply, POOL, split_axis=0, concat_axis=2, tiled=True)[0]]
    all_to_all x1 -> x2, waiting for transfers between devices: 123 us -> 123 us  [the longest x1 123 us: body(): lax.all_to_all(reply, POOL, split_axis=0, concat_axis=0, tiled=True)]
  transfers between devices with their start and end apart: 4 -> 5, of which waited for: 4 -> 4; matrix products, arithmetic and copies ran while one was open for 5% -> 5% of each run, Pallas kernels for 0% -> 0%
where the time goes in v4:
time: 388 us; the launch traced here: 387 us
  waiting for transfers between devices  207 us (53%)
  blocking collectives  74.5 us (19%)
  starting transfers between devices  35.9 us (9%)
  matrix products  27.7 us (7%)
  local copies, waits for them, and re-layouts  16.7 us (4%)
  between operations  14 us (4%)
  other arithmetic  10.6 us (3%)
    all_to_all x1, waiting for transfers between devices, body(): lax.all_to_all(reply, POOL, split_axis=0, concat_axis=0, tiled=True)  123 us
    all_gather x1, blocking collectives, body(): w_chip = lax.all_gather(kv_weight, 'pz', axis=1, tiled=True)  74.5 us
    all_gather x1, waiting for transfers between devices, body(): w_chip = lax.all_gather(w_chip, 'px', axis=1, tiled=True)  30.1 us
    all_gather x1, waiting for transfers between devices, body(): w_all = lax.all_gather(w_chip, 'pc', axis=1, tiled=True)  27.3 us
    reduce_scatter x1, waiting for transfers between devices, body(): lax.psum_scatter(partial_kv.astype(jnp.bfloat16), 'tp', scatter_dimension...  26.1 us
    all_to_all x1, starting transfers between devices, body(): lax.all_to_all(outgoing, POOL, split_axis=1, concat_axis=0, tiled=True)  19.1 us
    all_to_all x1, starting transfers between devices, body(): lax.all_to_all(reply, POOL, split_axis=0, concat_axis=0, tiled=True)  16.7 us
    squeeze x8, local copies, waits for them, and re-layouts, body(): (top, total, numer), unused = lax.scan(visit, (top, total, numer), grouped)  8.64 us
  transfers between devices with their start and end apart: 5, of which 4 were waited for; matrix products, arithmetic and copies ran while one was open for 5% of the time, Pallas kernels for 0%

profile of v4, /device:TPU:34, one launch (start us, length us, event | category | flops | bytes accessed | tf_op | source)
XLA Modules:
  0.0 387.1 jit_solution(18049471111629042958)
XLA Ops:
  7.2 0.7 fusion.29
  7.9 1.3 copy.14
  9.3 0.1 pad_maximum_fusion.1
  9.3 0.1 broadcast_in_dim.41
  9.4 1.2 pad_maximum_fusion
  10.6 19.1 %all-to-all-start = ((bf16[9,128,256]{2,0,1:T(8,128)(2,1)}), bf16[9,128,256]{2,0,1:T(8,128)(2,1)S(1)}, u32[]{:S(2)}, u32[]{:S(2)}) async-start(bf16[9,128,256]{2,0,1:T(8,128)(2,1)} %pad_maximum_fusion), calls=%async_computation | async-start | bytes 2097152 | tf_op jit(solution)/shard_map/all_to_all | solution.py:51
  29.7 0.0 all-gather.3.cloned.1.call-start
  29.7 74.5 %all_gather.9 = bf16[2048,128]{0,1:T(8,128)(2,1)} all-gather(bf16[2048,8]{0,1:T(8,128)(2,1)S(1)} %copy-done.2), channel_id=1, replica_groups=mesh['px'=4,'pz'=16,'pc'=2,'tp'=4] {'pz'}, dimensions={1}, use_global_device_ids=true | all-gather | bytes 557056 | tf_op jit(solution)/shard_map/all_gather | solution.py:58
  104.3 0.1 slice_convert_fusion
  104.4 0.1 fusion.20
  104.5 0.1 eq.17
  104.6 8.4 %fusion.11 = bf16[8192,256]{1,0:T(8,128)(2,1)} fusion(s32[8192]{0:T(1024)S(1)} %eq.17, bf16[128,9,256]{2,1,0:T(8,128)(2,1)S(1)} %bitcast.85), kind=kOutput, calls=%fused_computation.19 | convolution fusion | flops 4305453056 | bytes 4751360 | tf_op jit(solution)/shard_map/dot_general | solution.py:64
  112.9 30.1 %all-gather.3.cloned.1.call-done = bf16[2048,512]{0,1:T(8,128)(2,1)} async-done(((bf16[2048,128]{0,1:T(8,128)(2,1)}), bf16[2048,512]{0,1:T(8,128)(2,1)}) %all-gather.3.cloned.1.call-update) | async-done | bytes 2097168 | tf_op jit(solution)/shard_map/all_gather | solution.py:59
  143.1 16.7 %all-to-all-start.1 = ((bf16[128,64,1,256]{3,1,2,0:T(8,128)(2,1)}), bf16[128,64,1,256]{3,1,2,0:T(8,128)(2,1)}, u32[]{:S(2)}, u32[]{:S(2)}) async-start(bf16[128,64,1,256]{3,1,2,0:T(8,128)(2,1)} %bitcast.83), calls=%async_computation.2 | async-start | bytes 8388608 | tf_op jit(solution)/shard_map/all_to_all | solution.py:67
  159.8 0.0 all-gather.5.cloned.1.call-start
  159.8 0.7 all-gather.5.cloned.1.call-update
  160.6 27.3 %all-gather.5.cloned.1.call-done = bf16[2048,1024]{0,1:T(8,128)(2,1)} async-done(((bf16[2048,512]{0,1:T(8,128)(2,1)}), bf16[2048,1024]{0,1:T(8,128)(2,1)}) %all-gather.5.cloned.1.call-update) | async-done | bytes 4194320 | tf_op jit(solution)/shard_map/all_gather | solution.py:69
  187.9 3.4 convolution_convert_fusion
  191.3 0.7 copy.15
  192.1 3.0 gather_fusion
  195.2 0.2 broadcast_select_fusion
  195.4 0.2 copy.17
  195.6 0.1 reshape_squeeze_reshape.3
  195.8 26.1 %reduce-scatter.2.cloned.1.call-done = bf16[128,256]{0,1:T(8,128)(2,1)} async-done(((bf16[128,1024]{0,1:T(8,128)(2,1)}), bf16[128,256]{0,1:T(8,128)(2,1)}) %reduce-scatter.2.cloned.1.call-update) | async-done | bytes 65552 | tf_op jit(solution)/shard_map/reduce_scatter | solution.py:79
  221.9 1.6 copy.18
  223.5 1.0 select_reduce_fusion
  224.5 0.1 fusion.14
  224.6 1.0 fusion.15
  225.7 123.1 %all-to-all-done.1 = bf16[128,64,1,256]{3,1,2,0:T(8,128)(2,1)} async-done(((bf16[128,64,1,256]{3,1,2,0:T(8,128)(2,1)}), bf16[128,64,1,256]{3,1,2,0:T(8,128)(2,1)}, u32[]{:S(2)}, u32[]{:S(2)}) %all-to-all-start.1) | async-done | bytes 4194336 | tf_op jit(solution)/shard_map/all_to_all | solution.py:67
  348.8 30.8 %while.15 = (s32[]{:T(128)}, f32[1024]{0:T(1024)S(1)}, f32[1024]{0:T(1024)S(1)}, f32[1024,128]{1,0:T(8,128)S(1)}, bf16[8,1024,256]{2,1,0:T(8,128)(2,1)}, /*index...) while((s32[]{:T(128)}, f32[1024]{0:T(1024)S(1)}, f32[1024]{0:T(1024)S(1)}, ...), condition=%wide.region_6.7_spmd.clone, body=%wide.region_3.6_spmd.clone.sunk | while | flops 545523712 | bytes 15659105 | solution.py:109
  348.8 1.1 dynamic-slice_bitcast_fusion.2
  349.8 0.7 fusion.44
  350.6 1.0 fusion.45
  351.6 1.0 convolution_add_fusion.2
  352.6 1.1 dynamic-slice_bitcast_fusion.2
  353.7 0.7 fusion.44
  354.5 1.0 fusion.45
  355.5 1.0 convolution_add_fusion.2
  356.5 1.1 dynamic-slice_bitcast_fusion.2
  357.5 0.8 fusion.44
  358.3 1.0 fusion.45
  359.3 1.0 convolution_add_fusion.2
  360.3 1.1 dynamic-slice_bitcast_fusion.2
  361.4 0.7 fusion.44
  362.2 1.0 fusion.45
  363.2 1.0 convolution_add_fusion.2
  364.2 1.1 dynamic-slice_bitcast_fusion.2
  365.3 0.8 fusion.44
  366.0 1.0 fusion.45
  367.0 1.0 convolution_add_fusion.2
  368.0 1.1 dynamic-slice_bitcast_fusion.2
  369.1 0.7 fusion.44
  369.9 1.0 fusion.45
  370.9 1.0 convolution_add_fusion.2
  371.9 1.1 dynamic-slice_bitcast_fusion.2
  373.0 0.8 fusion.44
  373.7 1.0 fusion.45
  374.7 1.0 convolution_add_fusion.2
  375.7 1.1 dynamic-slice_bitcast_fusion.2
  376.8 0.7 fusion.44
  377.6 1.0 fusion.45
  378.6 1.0 convolution_add_fusion.2
  379.6 0.2 divide_convert_fusion
  379.8 0.8 convert_element_type.59
  (43 shorter events, 0.3 us)
Async XLA Ops:
  7.2 180.7 %copy-start = (bf16[128,2048]{1,0:T(8,128)(2,1)S(1)}, bf16[128,2048]{1,0:T(8,128)(2,1)}, u32[]{:S(2)}) copy-start(bf16[128,2048]{1,0:T(8,128)(2,1)} %param.8) | copy-start | bytes 1572868
  7.2 22.5 %copy-start.2 = (bf16[2048,8]{0,1:T(8,128)(2,1)S(1)}, bf16[2048,8]{0,1:T(8,128)(2,1)}, u32[]{:S(2)}) copy-start(bf16[2048,8]{0,1:T(8,128)(2,1)} %param.9) | copy-start | bytes 98308
  10.6 93.7 %all-to-all-start = ((bf16[9,128,256]{2,0,1:T(8,128)(2,1)}), bf16[9,128,256]{2,0,1:T(8,128)(2,1)S(1)}, u32[]{:S(2)}, u32[]{:S(2)}) async-start(bf16[9,128,256]{2,0,1:T(8,128)(2,1)} %pad_maximum_fusion), calls=%async_computation | async-start | bytes 2097152 | tf_op jit(solution)/shard_map/all_to_all | solution.py:51
  29.7 113.4 %all-gather.3.cloned.1.call-start = ((), (), s32[]{:S(2)}) async-start(), calls=%async_computation.3 | async-start | bytes 2621440 | tf_op jit(solution)/shard_map/all_gather | solution.py:59
  143.1 205.7 %all-to-all-start.1 = ((bf16[128,64,1,256]{3,1,2,0:T(8,128)(2,1)}), bf16[128,64,1,256]{3,1,2,0:T(8,128)(2,1)}, u32[]{:S(2)}, u32[]{:S(2)}) async-start(bf16[128,64,1,256]{3,1,2,0:T(8,128)(2,1)} %bitcast.83), calls=%async_computation.2 | async-start | bytes 8388608 | tf_op jit(solution)/shard_map/all_to_all | solution.py:67
  159.8 32.3 %copy-start.3 = (s32[1,2,64]{2,1,0:T(2,128)S(1)}, s32[1,2,64]{2,1,0:T(2,128)}, u32[]{:S(2)}) copy-start(s32[1,2,64]{2,1,0:T(2,128)} %param.13) | copy-start | bytes 1540
  159.8 28.1 %all-gather.5.cloned.1.call-start = ((), (), s32[]{:S(2)}) async-start(), calls=%async_computation.4 | async-start | bytes 6291456 | tf_op jit(solution)/shard_map/all_gather | solution.py:69
  160.5 61.3 %reduce-scatter.2.cloned.1.call-start = ((), (), s32[]{:S(2)}) async-start(), calls=%async_computation.5 | async-start | bytes 327680 | tf_op jit(solution)/shard_map/reduce_scatter | solution.py:79
  160.6 35.0 %copy-start.1 = (bf16[128,1024]{1,0:T(8,128)(2,1)S(1)}, bf16[128,1024]{1,0:T(8,128)(2,1)}, u32[]{:S(2)}) copy-start(bf16[128,1024]{1,0:T(8,128)(2,1)} %param.10) | copy-start | bytes 786436
Sparse Core Ops, SparseCore 0:
  104.4 38.6 all-gather.2
  162.7 25.1 all-gather.4
  192.2 29.6 reduce-scatter.1

commit v5 on v4

--- a/solution.py
+++ b/solution.py
@@ -55,27 +55,31 @@
     wanted_all = (
         id_rows[:, :fetch_count] * ID_SPLIT + id_rows[:, fetch_count : 2 * fetch_count]
     ).astype(jnp.int32)
-    w_chip = lax.all_gather(kv_weight, "pz", axis=1, tiled=True)
-    w_chip = lax.all_gather(w_chip, "px", axis=1, tiled=True)
+    nz = lax.axis_size("pz")
+    w_z = kv_weight
+    dist = 1
+    while dist < nz:
+        perm = [(i, (i - dist) % nz) for i in range(nz)]
+        w_z = jnp.concatenate([w_z, lax.ppermute(w_z, "pz", perm)], axis=1)
+        dist *= 2
     picks = (
         wanted_all.reshape(-1)[:, None]
         == jnp.arange(npool * blocks_dev, dtype=jnp.int32)[None, :]
     ).astype(jnp.bfloat16)
     reply = jnp.dot(picks, table, preferred_element_type=jnp.float32).astype(jnp.bfloat16)
     reply = reply.reshape(npool, fetch_count, 1, width)
-    reply, w_chip = lax.optimization_barrier((reply, w_chip))
+    reply, w_z = lax.optimization_barrier((reply, w_z))
     fetched = lax.all_to_all(reply, POOL, split_axis=0, concat_axis=0, tiled=True)
 
+    w_chip = lax.all_gather(w_z, "px", axis=1, tiled=True)
     w_all = lax.all_gather(w_chip, "pc", axis=1, tiled=True)
     partial_kv = jnp.dot(hidden_rows, w_all, preferred_element_type=jnp.float32)
     ncore = lax.axis_size("pc")
-    nchip = npool // ncore
+    nx = lax.axis_size("px")
     cols = kv_weight.shape[1]
-    partial_kv = (
-        partial_kv.reshape(-1, ncore, nchip, cols)
-        .transpose(0, 2, 1, 3)
-        .reshape(partial_kv.shape[0], -1)
-    )
+    partial_kv = partial_kv.reshape(-1, ncore, nx, nz, cols)
+    partial_kv = jnp.roll(partial_kv, lax.axis_index("pz"), axis=3)
+    partial_kv = partial_kv.transpose(0, 2, 3, 1, 4).reshape(partial_kv.shape[0], -1)
     fresh = lax.psum_scatter(partial_kv.astype(jnp.bfloat16), "tp", scatter_dimension=1, tiled=True)
 
     count = hidden_rows.shape[0]

time: 388 us -> 388 us (level)
  the two profiles are of different devices: /device:TPU:34 before, /device:TPU:42 now
where the time goes in v5:
time: 388 us; the launch traced here: 387 us
  waiting for transfers between devices  246 us (63%)
  starting transfers between devices  70.7 us (18%)
  matrix products  27.7 us (7%)
  local copies, waits for them, and re-layouts  16.7 us (4%)
  between operations  14.1 us (4%)
  other arithmetic  10.8 us (3%)
    all_to_all x1, waiting for transfers between devices, body(): lax.all_to_all(reply, POOL, split_axis=0, concat_axis=0, tiled=True)  79.8 us
    ppermute x4, waiting for transfers between devices, body(): w_z = jnp.concatenate([w_z, lax.ppermute(w_z, 'pz', perm)], axis=1)  69.5 us
    all_gather x1, waiting for transfers between devices, body(): w_chip = lax.all_gather(w_z, 'px', axis=1, tiled=True)  46.2 us
    all_to_all x1, starting transfers between devices, body(): lax.all_to_all(reply, POOL, split_axis=0, concat_axis=0, tiled=True)  27.4 us
    all_gather x1, waiting for transfers between devices, body(): w_all = lax.all_gather(w_chip, 'pc', axis=1, tiled=True)  25.8 us
    reduce_scatter x1, waiting for transfers between devices, body(): lax.psum_scatter(partial_kv.astype(jnp.bfloat16), 'tp', scatter_dimension...  24.3 us
    ppermute x4, starting transfers between devices, body(): w_z = jnp.concatenate([w_z, lax.ppermute(w_z, 'pz', perm)], axis=1)  24 us
    all_to_all x1, starting transfers between devices, body(): lax.all_to_all(outgoing, POOL, split_axis=1, concat_axis=0, tiled=True)  19.1 us
  transfers between devices with their start and end apart: 9, of which 8 were waited for; matrix products, arithmetic and copies ran while one was open for 3% of the time, Pallas kernels for 0%

profile of v5, /device:TPU:42, one launch (start us, length us, event | category | flops | bytes accessed | tf_op | source)
XLA Modules:
  0.0 386.7 jit_solution(6478034551417054082)
XLA Ops:
  7.2 0.7 fusion.30
  7.9 1.3 copy.15
  9.4 1.2 pad_maximum_fusion
  10.6 19.1 %all-to-all-start = ((bf16[9,128,256]{2,0,1:T(8,128)(2,1)}), bf16[9,128,256]{2,0,1:T(8,128)(2,1)S(1)}, u32[]{:S(2)}, u32[]{:S(2)}) async-start(bf16[9,128,256]{2,0,1:T(8,128)(2,1)} %pad_maximum_fusion), calls=%async_computation | async-start | bytes 2097152 | tf_op jit(solution)/shard_map/all_to_all | solution.py:51
  29.7 2.5 collective-permute-start
  32.1 43.0 %collective-permute-done = bf16[2048,8]{0,1:T(8,128)(2,1)S(1)} collective-permute-done((bf16[2048,8]{0,1:T(8,128)(2,1)S(1)}, bf16[2048,8]{0,1:T(8,128)(2,1)S(1)}, u32[]{:S(2)}, u32[]{:S(2)}) %collective-permute-start) | collective-permute-done | bytes 32800 | tf_op jit(solution)/shard_map/ppermute | solution.py:63
  75.2 4.4 %collective-permute-start.1 = (bf16[2048,16]{0,1:T(8,128)(2,1)S(1)}, bf16[2048,16]{0,1:T(8,128)(2,1)S(1)}, u32[]{:S(2)}, u32[]{:S(2)}) collective-permute-start(bf16[2048,16]{0,1:T(8,128)(2,1)S(1)} %pad_maximum_fusion.3), channel_id=1, source_target_pairs={{0,112},{8,120},{16,0},{24,8},{32,16},{40,24},{48,32},{56,40},{64,... | collective-permute-start | bytes 196616 | tf_op jit(solution)/shard_map/ppermute | solution.py:63
  79.6 4.3 %collective-permute-done.1 = bf16[2048,16]{0,1:T(8,128)(2,1)S(1)} collective-permute-done((bf16[2048,16]{0,1:T(8,128)(2,1)S(1)}, bf16[2048,16]{0,1:T(8,128)(2,1)S(1)}, u32[]{:S(2)}, u32[]{:S(2)}) %collective-permute-start.1) | collective-permute-done | bytes 65568 | tf_op jit(solution)/shard_map/ppermute | solution.py:63
  83.9 6.5 %collective-permute-start.2 = (bf16[2048,32]{0,1:T(8,128)(2,1)S(1)}, bf16[2048,32]{0,1:T(8,128)(2,1)S(1)}, u32[]{:S(2)}, u32[]{:S(2)}) collective-permute-start(bf16[2048,32]{0,1:T(8,128)(2,1)S(1)} %pad_maximum_fusion.2), channel_id=1, source_target_pairs={{0,96},{8,104},{16,112},{24,120},{32,0},{40,8},{48,16},{56,24},{64... | collective-permute-start | bytes 393224 | tf_op jit(solution)/shard_map/ppermute | solution.py:63
  90.4 9.7 %collective-permute-done.2 = bf16[2048,32]{0,1:T(8,128)(2,1)S(1)} collective-permute-done((bf16[2048,32]{0,1:T(8,128)(2,1)S(1)}, bf16[2048,32]{0,1:T(8,128)(2,1)S(1)}, u32[]{:S(2)}, u32[]{:S(2)}) %collective-permute-start.2) | collective-permute-done | bytes 131104 | tf_op jit(solution)/shard_map/ppermute | solution.py:63
  100.2 10.6 %collective-permute-start.3 = (bf16[2048,64]{0,1:T(8,128)(2,1)S(1)}, bf16[2048,64]{0,1:T(8,128)(2,1)S(1)}, u32[]{:S(2)}, u32[]{:S(2)}) collective-permute-start(bf16[2048,64]{0,1:T(8,128)(2,1)S(1)} %pad_maximum_fusion.1), channel_id=1, source_target_pairs={{0,64},{8,72},{16,80},{24,88},{32,96},{40,104},{48,112},{56,120},{... | collective-permute-start | bytes 786440 | tf_op jit(solution)/shard_map/ppermute | solution.py:63
  110.8 12.4 %collective-permute-done.3 = bf16[2048,64]{0,1:T(8,128)(2,1)S(1)} collective-permute-done((bf16[2048,64]{0,1:T(8,128)(2,1)S(1)}, bf16[2048,64]{0,1:T(8,128)(2,1)S(1)}, u32[]{:S(2)}, u32[]{:S(2)}) %collective-permute-start.3) | collective-permute-done | bytes 262176 | tf_op jit(solution)/shard_map/ppermute | solution.py:63
  123.5 8.4 %fusion.11 = bf16[8192,256]{1,0:T(8,128)(2,1)} fusion(s32[8192]{0:T(1024)S(1)} %eq.20, bf16[128,9,256]{2,1,0:T(8,128)(2,1)S(1)} %bitcast.85), kind=kOutput, calls=%fused_computation.19 | convolution fusion | flops 4305453056 | bytes 4751360 | tf_op jit(solution)/shard_map/dot_general | solution.py:69
  131.9 27.4 %all-to-all-start.1 = ((bf16[128,64,1,256]{3,1,2,0:T(8,128)(2,1)}), bf16[128,64,1,256]{3,1,2,0:T(8,128)(2,1)}, u32[]{:S(2)}, u32[]{:S(2)}) async-start(bf16[128,64,1,256]{3,1,2,0:T(8,128)(2,1)} %bitcast.83), calls=%async_computation.2 | async-start | bytes 8388608 | tf_op jit(solution)/shard_map/all_to_all | solution.py:72
  159.4 0.7 all-gather.3.cloned.1.call-update
  160.1 46.2 %all-gather.3.cloned.1.call-done = bf16[2048,512]{0,1:T(8,128)(2,1)} async-done(((bf16[2048,128]{0,1:T(8,128)(2,1)}), bf16[2048,512]{0,1:T(8,128)(2,1)}) %all-gather.3.cloned.1.call-update) | async-done | bytes 2097168 | tf_op jit(solution)/shard_map/all_gather | solution.py:74
  206.3 0.2 reduce-scatter.2.cloned.1.call-start
  206.6 25.8 %all-gather.5.cloned.1.call-done = bf16[2048,1024]{0,1:T(8,128)(2,1)} async-done(((bf16[2048,512]{0,1:T(8,128)(2,1)}), bf16[2048,1024]{0,1:T(8,128)(2,1)}) %all-gather.5.cloned.1.call-update) | async-done | bytes 4194320 | tf_op jit(solution)/shard_map/all_gather | solution.py:75
  232.4 3.4 fusion.32
  235.8 0.2 fusion.13
  236.0 0.7 copy.26
  236.8 3.0 gather_fusion
  239.8 0.2 broadcast_select_fusion
  240.0 0.2 copy.19
  240.4 24.3 %reduce-scatter.2.cloned.1.call-done = bf16[128,256]{0,1:T(8,128)(2,1)} async-done(((bf16[128,1024]{0,1:T(8,128)(2,1)}), bf16[128,256]{0,1:T(8,128)(2,1)}) %reduce-scatter.2.cloned.1.call-update) | async-done | bytes 65552 | tf_op jit(solution)/shard_map/reduce_scatter | solution.py:83
  264.7 1.6 copy.20
  266.3 1.0 select_reduce_fusion
  267.4 1.0 fusion.16
  268.5 79.8 %all-to-all-done.1 = bf16[128,64,1,256]{3,1,2,0:T(8,128)(2,1)} async-done(((bf16[128,64,1,256]{3,1,2,0:T(8,128)(2,1)}), bf16[128,64,1,256]{3,1,2,0:T(8,128)(2,1)}, u32[]{:S(2)}, u32[]{:S(2)}) %all-to-all-start.1) | async-done | bytes 4194336 | tf_op jit(solution)/shard_map/all_to_all | solution.py:72
  348.3 30.8 %while.15 = (s32[]{:T(128)}, f32[1024]{0:T(1024)S(1)}, f32[1024]{0:T(1024)S(1)}, f32[1024,128]{1,0:T(8,128)S(1)}, bf16[8,1024,256]{2,1,0:T(8,128)(2,1)}, /*index...) while((s32[]{:T(128)}, f32[1024]{0:T(1024)S(1)}, f32[1024]{0:T(1024)S(1)}, ...), condition=%wide.region_6.7_spmd.clone, body=%wide.region_3.6_spmd.clone.sunk | while | flops 545523712 | bytes 15659105 | solution.py:113
  348.3 1.1 dynamic-slice_bitcast_fusion.2
  349.4 0.7 fusion.46
  350.1 1.0 fusion.47
  351.1 1.0 convolution_add_fusion.2
  352.1 1.1 dynamic-slice_bitcast_fusion.2
  353.2 0.8 fusion.46
  354.0 1.0 fusion.47
  355.0 1.0 convolution_add_fusion.2
  356.0 1.1 dynamic-slice_bitcast_fusion.2
  357.1 0.7 fusion.46
  357.8 1.0 fusion.47
  358.8 1.0 convolution_add_fusion.2
  359.8 1.1 dynamic-slice_bitcast_fusion.2
  360.9 0.8 fusion.46
  361.7 1.0 fusion.47
  362.7 1.0 convolution_add_fusion.2
  363.7 1.1 dynamic-slice_bitcast_fusion.2
  364.8 0.7 fusion.46
  365.5 1.0 fusion.47
  366.5 1.0 convolution_add_fusion.2
  367.5 1.1 dynamic-slice_bitcast_fusion.2
  368.6 0.8 fusion.46
  369.4 1.0 fusion.47
  370.4 1.0 convolution_add_fusion.2
  371.4 1.1 dynamic-slice_bitcast_fusion.2
  372.5 0.7 fusion.46
  373.2 1.0 fusion.47
  374.2 1.0 convolution_add_fusion.2
  375.2 1.1 dynamic-slice_bitcast_fusion.2
  376.3 0.8 fusion.46
  377.1 1.0 fusion.47
  378.1 1.0 convolution_add_fusion.2
  379.1 0.2 divide_convert_fusion
  379.3 0.8 convert_element_type.51
  (61 shorter events, 1.0 us)
Async XLA Ops:
  7.2 225.2 %copy-start = (bf16[128,2048]{1,0:T(8,128)(2,1)S(1)}, bf16[128,2048]{1,0:T(8,128)(2,1)}, u32[]{:S(2)}) copy-start(bf16[128,2048]{1,0:T(8,128)(2,1)} %param.8) | copy-start | bytes 1572868
  7.2 22.5 %copy-start.2 = (bf16[2048,8]{0,1:T(8,128)(2,1)S(1)}, bf16[2048,8]{0,1:T(8,128)(2,1)}, u32[]{:S(2)}) copy-start(bf16[2048,8]{0,1:T(8,128)(2,1)} %param.9) | copy-start | bytes 98308
  10.6 112.7 %all-to-all-start = ((bf16[9,128,256]{2,0,1:T(8,128)(2,1)}), bf16[9,128,256]{2,0,1:T(8,128)(2,1)S(1)}, u32[]{:S(2)}, u32[]{:S(2)}) async-start(bf16[9,128,256]{2,0,1:T(8,128)(2,1)} %pad_maximum_fusion), calls=%async_computation | async-start | bytes 2097152 | tf_op jit(solution)/shard_map/all_to_all | solution.py:51
  29.7 45.5 %collective-permute-start = (bf16[2048,8]{0,1:T(8,128)(2,1)S(1)}, bf16[2048,8]{0,1:T(8,128)(2,1)S(1)}, u32[]{:S(2)}, u32[]{:S(2)}) collective-permute-start(bf16[2048,8]{0,1:T(8,128)(2,1)S(1)} %copy-done.2), channel_id=1, source_target_pairs={{0,120},{8,0},{16,8},{24,16},{32,24},{40,32},{48,40},{56,48},{64,5... | collective-permute-start | bytes 98312 | tf_op jit(solution)/shard_map/ppermute | solution.py:63
  75.2 8.7 %collective-permute-start.1 = (bf16[2048,16]{0,1:T(8,128)(2,1)S(1)}, bf16[2048,16]{0,1:T(8,128)(2,1)S(1)}, u32[]{:S(2)}, u32[]{:S(2)}) collective-permute-start(bf16[2048,16]{0,1:T(8,128)(2,1)S(1)} %pad_maximum_fusion.3), channel_id=1, source_target_pairs={{0,112},{8,120},{16,0},{24,8},{32,16},{40,24},{48,32},{56,40},{64,... | collective-permute-start | bytes 196616 | tf_op jit(solution)/shard_map/ppermute | solution.py:63
  83.9 16.2 %collective-permute-start.2 = (bf16[2048,32]{0,1:T(8,128)(2,1)S(1)}, bf16[2048,32]{0,1:T(8,128)(2,1)S(1)}, u32[]{:S(2)}, u32[]{:S(2)}) collective-permute-start(bf16[2048,32]{0,1:T(8,128)(2,1)S(1)} %pad_maximum_fusion.2), channel_id=1, source_target_pairs={{0,96},{8,104},{16,112},{24,120},{32,0},{40,8},{48,16},{56,24},{64... | collective-permute-start | bytes 393224 | tf_op jit(solution)/shard_map/ppermute | solution.py:63
  100.2 23.0 %collective-permute-start.3 = (bf16[2048,64]{0,1:T(8,128)(2,1)S(1)}, bf16[2048,64]{0,1:T(8,128)(2,1)S(1)}, u32[]{:S(2)}, u32[]{:S(2)}) collective-permute-start(bf16[2048,64]{0,1:T(8,128)(2,1)S(1)} %pad_maximum_fusion.1), channel_id=1, source_target_pairs={{0,64},{8,72},{16,80},{24,88},{32,96},{40,104},{48,112},{56,120},{... | collective-permute-start | bytes 786440 | tf_op jit(solution)/shard_map/ppermute | solution.py:63
  123.2 8.7 %copy-start.1 = (bf16[2048,128]{0,1:T(8,128)(2,1)}, bf16[2048,128]{0,1:T(8,128)(2,1)S(1)}, u32[]{:S(2)}) copy-start(bf16[2048,128]{0,1:T(8,128)(2,1)S(1)} %constant_dynamic-update-slice_fusion) | copy-start | bytes 1572868
  131.9 216.4 %all-to-all-start.1 = ((bf16[128,64,1,256]{3,1,2,0:T(8,128)(2,1)}), bf16[128,64,1,256]{3,1,2,0:T(8,128)(2,1)}, u32[]{:S(2)}, u32[]{:S(2)}) async-start(bf16[128,64,1,256]{3,1,2,0:T(8,128)(2,1)} %bitcast.83), calls=%async_computation.2 | async-start | bytes 8388608 | tf_op jit(solution)/shard_map/all_to_all | solution.py:72
  159.3 46.9 %all-gather.3.cloned.1.call-start = ((), (), s32[]{:S(2)}) async-start(), calls=%async_computation.3 | async-start | bytes 2621440 | tf_op jit(solution)/shard_map/all_gather | solution.py:74
  160.0 72.3 %all-gather.5.cloned.1.call-start = ((), (), s32[]{:S(2)}) async-start(), calls=%async_computation.4 | async-start | bytes 6291456 | tf_op jit(solution)/shard_map/all_gather | solution.py:75
  206.3 30.5 %copy-start.4 = (s32[1,2,64]{2,1,0:T(2,128)S(1)}, s32[1,2,64]{2,1,0:T(2,128)}, u32[]{:S(2)}) copy-start(s32[1,2,64]{2,1,0:T(2,128)} %param.13) | copy-start | bytes 1540
  206.3 58.4 %reduce-scatter.2.cloned.1.call-start = ((), (), s32[]{:S(2)}) async-start(), calls=%async_computation.5 | async-start | bytes 327680 | tf_op jit(solution)/shard_map/reduce_scatter | solution.py:83
  206.6 33.7 %copy-start.3 = (bf16[128,1024]{1,0:T(8,128)(2,1)S(1)}, bf16[128,1024]{1,0:T(8,128)(2,1)}, u32[]{:S(2)}) copy-start(bf16[128,1024]{1,0:T(8,128)(2,1)} %param.10) | copy-start | bytes 786436
Sparse Core Ops, SparseCore 0:
  162.2 43.9 all-gather.2
  208.3 23.9 all-gather.4
  236.9 27.7 reduce-scatter.1

commit v6 on v4

--- a/solution.py
+++ b/solution.py
@@ -55,28 +55,20 @@
     wanted_all = (
         id_rows[:, :fetch_count] * ID_SPLIT + id_rows[:, fetch_count : 2 * fetch_count]
     ).astype(jnp.int32)
-    w_chip = lax.all_gather(kv_weight, "pz", axis=1, tiled=True)
-    w_chip = lax.all_gather(w_chip, "px", axis=1, tiled=True)
     picks = (
         wanted_all.reshape(-1)[:, None]
         == jnp.arange(npool * blocks_dev, dtype=jnp.int32)[None, :]
     ).astype(jnp.bfloat16)
     reply = jnp.dot(picks, table, preferred_element_type=jnp.float32).astype(jnp.bfloat16)
     reply = reply.reshape(npool, fetch_count, 1, width)
-    reply, w_chip = lax.optimization_barrier((reply, w_chip))
     fetched = lax.all_to_all(reply, POOL, split_axis=0, concat_axis=0, tiled=True)
 
-    w_all = lax.all_gather(w_chip, "pc", axis=1, tiled=True)
-    partial_kv = jnp.dot(hidden_rows, w_all, preferred_element_type=jnp.float32)
-    ncore = lax.axis_size("pc")
-    nchip = npool // ncore
-    cols = kv_weight.shape[1]
-    partial_kv = (
-        partial_kv.reshape(-1, ncore, nchip, cols)
-        .transpose(0, 2, 1, 3)
-        .reshape(partial_kv.shape[0], -1)
-    )
-    fresh = lax.psum_scatter(partial_kv.astype(jnp.bfloat16), "tp", scatter_dimension=1, tiled=True)
+    w_head = lax.all_gather(kv_weight, ("pz", "pc"), axis=1, tiled=True)
+    h_ring = lax.all_gather(hidden_rows, "px", axis=0, tiled=False)
+    part = jnp.einsum("xrd,dc->xrc", h_ring, w_head, preferred_element_type=jnp.float32)
+    part = lax.all_to_all(part.astype(jnp.bfloat16), "px", split_axis=0, concat_axis=0, tiled=True)
+    partial_kv = part.transpose(1, 0, 2).reshape(part.shape[1], -1)
+    fresh = lax.psum_scatter(partial_kv, "tp", scatter_dimension=1, tiled=True)
 
     count = hidden_rows.shape[0]
     group = QH // KVH

time: 388 us -> 393 us (1.013)
  waiting for transfers between devices: 207 us -> 223 us
  starting transfers between devices: 35.9 us -> 22.1 us
  blocking collectives: 74.5 us -> 78.6 us
    all_to_all x0 -> x1, blocking collectives: none -> 78.6 us  [body(): lax.all_to_all(outgoing, POOL, split_axis=1, concat_axis=0, tiled=True)]
    all_gather x1 -> x0, blocking collectives: 74.5 us -> none  [body(): w_chip = lax.all_gather(kv_weight, 'pz', axis=1, tiled=True)]
    all_to_all x1, waiting for transfers between devices: 123 us -> 152 us  [body(): lax.all_to_all(reply, POOL, split_axis=0, concat_axis=0, tiled=True)]
    all_gather x2, waiting for transfers between devices: 57.4 us -> 41 us  [the longest x1 37.7 us: body(): h_ring = lax.all_gather(hidden_rows, 'px', axis=0, tiled=False)]
    all_to_all x1, starting transfers between devices: 19.1 us -> 4.87 us  [body(): lax.all_to_all(part.astype(jnp.bfloat16), 'px', split_axis=0, concat_axis...]
where the time goes in v6:
time: 393 us; the launch traced here: 392 us
  waiting for transfers between devices  223 us (57%)
  blocking collectives  78.6 us (20%)
  matrix products  27.6 us (7%)
  starting transfers between devices  22.1 us (6%)
  local copies, waits for them, and re-layouts  16.7 us (4%)
  between operations  13.9 us (4%)
  other arithmetic  9.57 us (2%)
    all_to_all x1, waiting for transfers between devices, body(): lax.all_to_all(reply, POOL, split_axis=0, concat_axis=0, tiled=True)  152 us
    all_to_all x1, blocking collectives, body(): lax.all_to_all(outgoing, POOL, split_axis=1, concat_axis=0, tiled=True)  78.6 us
    all_gather x1, waiting for transfers between devices, body(): h_ring = lax.all_gather(hidden_rows, 'px', axis=0, tiled=False)  37.7 us
    reduce_scatter x1, waiting for transfers between devices, body(): fresh = lax.psum_scatter(partial_kv, 'tp', scatter_dimension=1, tiled=True)  28.9 us
    all_to_all x1, starting transfers between devices, body(): lax.all_to_all(reply, POOL, split_axis=0, concat_axis=0, tiled=True)  17.1 us
    squeeze x8, local copies, waits for them, and re-layouts, body(): (top, total, numer), unused = lax.scan(visit, (top, total, numer), grouped)  8.64 us
    dot_general x1, matrix products, body(): jnp.dot(picks, table, preferred_element_type=jnp.float32)  8.37 us
  transfers between devices with their start and end apart: 5, of which 4 were waited for; matrix products, arithmetic and copies ran while one was open for 5% of the time, Pallas kernels for 0%

profile of v6, /device:TPU:34, one launch (start us, length us, event | category | flops | bytes accessed | tf_op | source)
XLA Modules:
  0.0 391.8 jit_solution(14049546364422569881)
XLA Ops:
  7.2 0.7 all-gather.4.cloned.1.call-update
  7.9 0.7 all-gather.6.cloned.1.call-update
  8.6 0.7 fusion.30
  9.3 1.3 copy.14
  10.7 0.1 pad_maximum_fusion.1
  10.7 0.1 broadcast_in_dim.43
  10.8 0.2 pad_maximum_fusion
  11.0 78.6 %all_to_all.25 = bf16[9,128,256]{2,0,1:T(8,128)(2,1)S(1)} all-to-all(bf16[9,128,256]{2,0,1:T(8,128)(2,1)S(1)} %pad_maximum_fusion), channel_id=1, replica_groups=mesh['px'=4,'pz'=16,'pc'=2,'tp'=4] {'px','pz','pc'}, dimensions={1} | all-to-all | bytes 1179648 | tf_op jit(solution)/shard_map/all_to_all | solution.py:51
  89.6 0.1 slice_convert_fusion
  89.7 0.1 fusion.21
  89.8 0.1 eq.17
  89.8 3.3 all-gather.4.cloned.1.call-done
  93.2 37.7 %all-gather.6.cloned.1.call-done = bf16[512,2048]{1,0:T(8,128)(2,1)} async-done(((bf16[128,2048]{1,0:T(8,128)(2,1)}), bf16[512,2048]{1,0:T(8,128)(2,1)}) %all-gather.6.cloned.1.call-update) | async-done | bytes 2097168 | tf_op jit(solution)/shard_map/all_gather | solution.py:67
  130.8 3.3 convolution_convert_fusion
  134.1 4.9 %all-to-all-start = ((bf16[4,128,256]{2,1,0:T(8,128)(2,1)}), bf16[4,128,256]{2,1,0:T(8,128)(2,1)S(1)}, u32[]{:S(2)}, u32[]{:S(2)}) async-start(bf16[4,128,256]{2,1,0:T(8,128)(2,1)} %convolution_convert_fusion), calls=%async_computation | async-start | bytes 524288 | tf_op jit(solution)/shard_map/all_to_all | solution.py:69
  139.0 8.4 %fusion.11 = bf16[8192,256]{1,0:T(8,128)(2,1)} fusion(s32[8192]{0:T(1024)S(1)} %eq.17, bf16[128,9,256]{2,1,0:T(8,128)(2,1)S(1)} %bitcast.85), kind=kOutput, calls=%fused_computation.19 | convolution fusion | flops 4305453056 | bytes 4751360 | tf_op jit(solution)/shard_map/dot_general | solution.py:62
  147.4 17.1 %all-to-all-start.2 = ((bf16[128,64,1,256]{3,1,2,0:T(8,128)(2,1)}), bf16[128,64,1,256]{3,1,2,0:T(8,128)(2,1)}, u32[]{:S(2)}, u32[]{:S(2)}) async-start(bf16[128,64,1,256]{3,1,2,0:T(8,128)(2,1)} %bitcast.83), calls=%async_computation.3 | async-start | bytes 8388608 | tf_op jit(solution)/shard_map/all_to_all | solution.py:64
  164.5 0.0 reduce-scatter.2.cloned.1.call-start
  164.6 0.8 copy.13
  165.5 3.0 gather_fusion
  168.5 0.2 broadcast_select_fusion
  168.7 0.2 copy.16
  168.9 0.1 reshape_squeeze_reshape.3
  169.1 28.9 %reduce-scatter.2.cloned.1.call-done = bf16[128,256]{0,1:T(8,128)(2,1)} async-done(((bf16[128,1024]{0,1:T(8,128)(2,1)}), bf16[128,256]{0,1:T(8,128)(2,1)}) %reduce-scatter.2.cloned.1.call-update) | async-done | bytes 65552 | tf_op jit(solution)/shard_map/reduce_scatter | solution.py:71
  198.0 1.6 copy.17
  199.6 1.0 select_reduce_fusion
  200.6 0.1 fusion.15
  200.7 1.0 fusion.16
  201.8 151.7 %all-to-all-done.2 = bf16[128,64,1,256]{3,1,2,0:T(8,128)(2,1)} async-done(((bf16[128,64,1,256]{3,1,2,0:T(8,128)(2,1)}), bf16[128,64,1,256]{3,1,2,0:T(8,128)(2,1)}, u32[]{:S(2)}, u32[]{:S(2)}) %all-to-all-start.2) | async-done | bytes 4194336 | tf_op jit(solution)/shard_map/all_to_all | solution.py:64
  353.5 30.8 %while.15 = (s32[]{:T(128)}, f32[1024]{0:T(1024)S(1)}, f32[1024]{0:T(1024)S(1)}, f32[1024,128]{1,0:T(8,128)S(1)}, bf16[8,1024,256]{2,1,0:T(8,128)(2,1)}, /*index...) while((s32[]{:T(128)}, f32[1024]{0:T(1024)S(1)}, f32[1024]{0:T(1024)S(1)}, ...), condition=%wide.region_6.7_spmd.clone, body=%wide.region_3.6_spmd.clone.sunk | while | flops 545523712 | bytes 15659105 | solution.py:101
  353.5 1.1 dynamic-slice_bitcast_fusion.2
  354.6 0.7 fusion.44
  355.3 1.0 fusion.45
  356.3 1.0 convolution_add_fusion.2
  357.3 1.1 dynamic-slice_bitcast_fusion.2
  358.4 0.8 fusion.44
  359.2 1.0 fusion.45
  360.2 1.0 convolution_add_fusion.2
  361.2 1.1 dynamic-slice_bitcast_fusion.2
  362.3 0.7 fusion.44
  363.0 1.0 fusion.45
  364.0 1.0 convolution_add_fusion.2
  365.0 1.1 dynamic-slice_bitcast_fusion.2
  366.1 0.8 fusion.44
  366.9 1.0 fusion.45
  367.9 1.0 convolution_add_fusion.2
  368.9 1.1 dynamic-slice_bitcast_fusion.2
  370.0 0.7 fusion.44
  370.7 1.0 fusion.45
  371.7 1.0 convolution_add_fusion.2
  372.7 1.1 dynamic-slice_bitcast_fusion.2
  373.8 0.8 fusion.44
  374.6 1.0 fusion.45
  375.6 1.0 convolution_add_fusion.2
  376.6 1.1 dynamic-slice_bitcast_fusion.2
  377.7 0.7 fusion.44
  378.4 1.0 fusion.45
  379.4 1.0 convolution_add_fusion.2
  380.4 1.1 dynamic-slice_bitcast_fusion.2
  381.5 0.8 fusion.44
  382.3 1.0 fusion.45
  383.3 1.0 convolution_add_fusion.2
  384.3 0.2 divide_convert_fusion
  384.5 0.8 convert_element_type.43
  (39 shorter events, 0.3 us)
Async XLA Ops:
  7.2 86.0 %all-gather.4.cloned.1.call-start = ((), (), s32[]{:S(2)}) async-start(), calls=%async_computation.4 | async-start | bytes 1081344 | tf_op jit(solution)/shard_map/all_gather | solution.py:66
  7.9 122.9 %all-gather.6.cloned.1.call-start = ((), (), s32[]{:S(2)}) async-start(), calls=%async_computation.6 | async-start | bytes 2621440 | tf_op jit(solution)/shard_map/all_gather | solution.py:67
  134.1 13.2 %all-to-all-start = ((bf16[4,128,256]{2,1,0:T(8,128)(2,1)}), bf16[4,128,256]{2,1,0:T(8,128)(2,1)S(1)}, u32[]{:S(2)}, u32[]{:S(2)}) async-start(bf16[4,128,256]{2,1,0:T(8,128)(2,1)} %convolution_convert_fusion), calls=%async_computation | async-start | bytes 524288 | tf_op jit(solution)/shard_map/all_to_all | solution.py:69
  147.4 18.1 %copy-start.1 = (s32[1,2,64]{2,1,0:T(2,128)S(1)}, s32[1,2,64]{2,1,0:T(2,128)}, u32[]{:S(2)}) copy-start(s32[1,2,64]{2,1,0:T(2,128)} %param.13) | copy-start | bytes 1540
  147.4 21.6 %copy-start = (bf16[128,1024]{1,0:T(8,128)(2,1)S(1)}, bf16[128,1024]{1,0:T(8,128)(2,1)}, u32[]{:S(2)}) copy-start(bf16[128,1024]{1,0:T(8,128)(2,1)} %param.10) | copy-start | bytes 786436
  147.4 206.1 %all-to-all-start.2 = ((bf16[128,64,1,256]{3,1,2,0:T(8,128)(2,1)}), bf16[128,64,1,256]{3,1,2,0:T(8,128)(2,1)}, u32[]{:S(2)}, u32[]{:S(2)}) async-start(bf16[128,64,1,256]{3,1,2,0:T(8,128)(2,1)} %bitcast.83), calls=%async_computation.3 | async-start | bytes 8388608 | tf_op jit(solution)/shard_map/all_to_all | solution.py:64
  164.5 33.5 %reduce-scatter.2.cloned.1.call-start = ((), (), s32[]{:S(2)}) async-start(), calls=%async_computation.5 | async-start | bytes 327680 | tf_op jit(solution)/shard_map/reduce_scatter | solution.py:71
Sparse Core Ops, SparseCore 0:
  10.1 83.0 all-gather.3
  95.3 35.5 all-gather.5
  168.7 29.2 reduce-scatter.1

commit v7 on v6

--- a/solution.py
+++ b/solution.py
@@ -61,14 +61,19 @@
     ).astype(jnp.bfloat16)
     reply = jnp.dot(picks, table, preferred_element_type=jnp.float32).astype(jnp.bfloat16)
     reply = reply.reshape(npool, fetch_count, 1, width)
+    reply, hidden_rows, kv_weight = lax.optimization_barrier((reply, hidden_rows, kv_weight))
     fetched = lax.all_to_all(reply, POOL, split_axis=0, concat_axis=0, tiled=True)
 
     w_head = lax.all_gather(kv_weight, ("pz", "pc"), axis=1, tiled=True)
     h_ring = lax.all_gather(hidden_rows, "px", axis=0, tiled=False)
     part = jnp.einsum("xrd,dc->xrc", h_ring, w_head, preferred_element_type=jnp.float32)
-    part = lax.all_to_all(part.astype(jnp.bfloat16), "px", split_axis=0, concat_axis=0, tiled=True)
-    partial_kv = part.transpose(1, 0, 2).reshape(part.shape[1], -1)
-    fresh = lax.psum_scatter(partial_kv, "tp", scatter_dimension=1, tiled=True)
+    ntp = lax.axis_size("tp")
+    head_slot = jnp.arange(ntp) == lax.axis_index("px")
+    spread = jnp.where(
+        head_slot[None, :, None, None], part.astype(jnp.bfloat16)[:, None], jnp.zeros((), jnp.bfloat16)
+    )
+    spread = spread.reshape(-1, part.shape[1], part.shape[2])
+    fresh = lax.psum_scatter(spread, ("px", "tp"), scatter_dimension=0, tiled=True)[0]
 
     count = hidden_rows.shape[0]
     group = QH // KVH

time: 393 us -> 371 us (0.944)
  the two profiles are of different devices: /device:TPU:34 before, /device:TPU:2 now
where the time goes in v7:
time: 371 us
  waiting for transfers between devices  222 us (60%)
  blocking collectives  75.4 us (20%)
  matrix products  26.9 us (7%)
  local copies, waits for them, and re-layouts  14.4 us (4%)
  between operations  13.9 us (4%)
  other arithmetic  10.5 us (3%)
  starting transfers between devices  7.3 us (2%)
    all_gather x1, waiting for transfers between devices, body(): w_head = lax.all_gather(kv_weight, ('pz', 'pc'), axis=1, tiled=True)  92.9 us
    unnamed x4, waiting for transfers between devices  88.1 us
    all_to_all x1, blocking collectives, body(): lax.all_to_all(outgoing, POOL, split_axis=1, concat_axis=0, tiled=True)  75.4 us
    all_gather x1, waiting for transfers between devices, body(): h_ring = lax.all_gather(hidden_rows, 'px', axis=0, tiled=False)  40.7 us
    squeeze x8, local copies, waits for them, and re-layouts, body(): (top, total, numer), unused = lax.scan(visit, (top, total, numer), grouped)  8.64 us
    dot_general x1, matrix products, body(): jnp.dot(picks, table, preferred_element_type=jnp.float32)  8.36 us
    dot_general x8, matrix products, merge(): jnp.dot(weights_now.astype(jnp.bfloat16), vals, preferred_element_type=jn...  7.84 us
    convert_element_type x8, other arithmetic, merge(): weights_now.astype(jnp.bfloat16)  7.51 us
  transfers between devices with their start and end apart: 4, of which 3 were waited for; matrix products, arithmetic and copies ran while one was open for 3% of the time, Pallas kernels for 0%

profile of v7, /device:TPU:2, one launch (start us, length us, event | category | flops | bytes accessed | tf_op | source)
XLA Modules:
  0.0 370.6 jit_solution(10390083109651068090)
XLA Ops:
  7.2 0.7 fusion.30
  7.8 1.3 copy.11
  9.2 0.1 pad_maximum_fusion.1
  9.3 0.1 broadcast_in_dim.72
  9.3 0.2 pad_maximum_fusion
  9.5 75.4 %all_to_all.20 = bf16[9,128,256]{2,0,1:T(8,128)(2,1)S(1)} all-to-all(bf16[9,128,256]{2,0,1:T(8,128)(2,1)S(1)} %pad_maximum_fusion), channel_id=1, replica_groups=mesh['px'=4,'pz'=16,'pc'=2,'tp'=4] {'px','pz','pc'}, dimensions={1} | all-to-all | bytes 1179648 | tf_op jit(solution)/shard_map/all_to_all | solution.py:51
  84.9 0.1 slice_convert_fusion
  85.0 0.1 fusion.21
  85.1 0.1 eq.29
  85.2 8.4 %fusion.11 = bf16[8192,256]{1,0:T(8,128)(2,1)} fusion(s32[8192]{0:T(1024)S(1)} %eq.29, bf16[128,9,256]{2,1,0:T(8,128)(2,1)S(1)} %bitcast.86), kind=kOutput, calls=%fused_computation.19 | convolution fusion | flops 4305453056 | bytes 4751360 | tf_op jit(solution)/shard_map/dot_general | solution.py:62
  93.6 7.2 %all-to-all-start.1 = ((bf16[128,64,1,256]{3,1,2,0:T(8,128)(2,1)}), bf16[128,64,1,256]{3,1,2,0:T(8,128)(2,1)}, u32[]{:S(2)}, u32[]{:S(2)}) async-start(bf16[128,64,1,256]{3,1,2,0:T(8,128)(2,1)} %bitcast.84), calls=%async_computation.1 | async-start | bytes 8388608 | tf_op jit(solution)/shard_map/all_to_all | solution.py:65
  100.8 0.0 all-gather.4.cloned.1.call-start
  100.8 0.7 all-gather.4.cloned.1.call-update
  101.5 0.0 all-gather.6.cloned.1.call-start
  101.6 0.7 all-gather.6.cloned.1.call-update
  102.3 0.0 reduce-scatter.4.cloned.1.call-start
  102.4 0.1 broadcast_in_dim.69
  102.4 92.9 %all-gather.4.cloned.1.call-done = bf16[2048,256]{0,1:T(8,128)(2,1)} async-done(((bf16[2048,8]{0,1:T(8,128)(2,1)}), bf16[2048,256]{0,1:T(8,128)(2,1)}) %all-gather.4.cloned.1.call-update) | async-done | bytes 1048592 | tf_op jit(solution)/shard_map/all_gather | solution.py:67
  195.3 40.7 %all-gather.6.cloned.1.call-done = bf16[512,2048]{1,0:T(8,128)(2,1)} async-done(((bf16[128,2048]{1,0:T(8,128)(2,1)}), bf16[512,2048]{1,0:T(8,128)(2,1)}) %all-gather.6.cloned.1.call-update) | async-done | bytes 2097168 | tf_op jit(solution)/shard_map/all_gather | solution.py:68
  236.0 2.6 convolution_convert_fusion
  238.6 1.2 bitcast_select_fusion.2
  239.9 3.0 gather_fusion
  242.9 0.2 broadcast_select_fusion
  243.1 0.2 copy.13
  243.3 0.1 reshape_squeeze_reshape.3
  243.5 86.7 %reduce-scatter.4.cloned.1.call-done = bf16[1,128,256]{2,1,0:T(8,128)(2,1)} async-done(((bf16[16,128,256]{2,1,0:T(8,128)(2,1)}), bf16[1,128,256]{2,1,0:T(8,128)(2,1)}) %reduce-scatter.4.cloned.1.call-update) | async-done | bytes 65552
  330.2 1.0 select_reduce_fusion
  331.2 0.1 fusion.15
  331.3 1.0 fusion.16
  332.4 30.6 %while.15 = (s32[]{:T(128)}, f32[1024]{0:T(1024)S(1)}, f32[1024]{0:T(1024)S(1)}, f32[1024,128]{1,0:T(8,128)S(1)}, bf16[8,1024,256]{2,1,0:T(8,128)(2,1)}, /*index...) while((s32[]{:T(128)}, f32[1024]{0:T(1024)S(1)}, f32[1024]{0:T(1024)S(1)}, ...), condition=%wide.region_6.7_spmd.clone, body=%wide.region_3.6_spmd.clone.sunk | while | flops 545523712 | bytes 15659105 | solution.py:106
  332.4 1.1 dynamic-slice_bitcast_fusion.2
  333.5 0.7 fusion.44
  334.2 0.9 fusion.45
  335.2 1.0 convolution_add_fusion.2
  336.2 1.1 dynamic-slice_bitcast_fusion.2
  337.3 0.8 fusion.44
  338.0 0.9 fusion.45
  339.0 1.0 convolution_add_fusion.2
  340.0 1.1 dynamic-slice_bitcast_fusion.2
  341.1 0.8 fusion.44
  341.9 0.9 fusion.45
  342.8 1.0 convolution_add_fusion.2
  343.8 1.1 dynamic-slice_bitcast_fusion.2
  344.9 0.8 fusion.44
  345.7 0.9 fusion.45
  346.7 1.0 convolution_add_fusion.2
  347.7 1.1 dynamic-slice_bitcast_fusion.2
  348.8 0.8 fusion.44
  349.5 0.9 fusion.45
  350.5 1.0 convolution_add_fusion.2
  351.5 1.1 dynamic-slice_bitcast_fusion.2
  352.6 0.8 fusion.44
  353.4 0.9 fusion.45
  354.3 1.0 convolution_add_fusion.2
  355.3 1.1 dynamic-slice_bitcast_fusion.2
  356.4 0.8 fusion.44
  357.2 0.9 fusion.45
  358.2 1.0 convolution_add_fusion.2
  359.2 1.1 dynamic-slice_bitcast_fusion.2
  360.3 0.8 fusion.44
  361.0 0.9 fusion.45
  362.0 1.0 convolution_add_fusion.2
  363.0 0.2 divide_convert_fusion
  363.2 0.8 convert_element_type.43
  (39 shorter events, 0.2 us)
Async XLA Ops:
  93.6 238.8 %all-to-all-start.1 = ((bf16[128,64,1,256]{3,1,2,0:T(8,128)(2,1)}), bf16[128,64,1,256]{3,1,2,0:T(8,128)(2,1)}, u32[]{:S(2)}, u32[]{:S(2)}) async-start(bf16[128,64,1,256]{3,1,2,0:T(8,128)(2,1)} %bitcast.84), calls=%async_computation.1 | async-start | bytes 8388608 | tf_op jit(solution)/shard_map/all_to_all | solution.py:65
  100.8 139.1 %copy-start.1 = (s32[1,2,64]{2,1,0:T(2,128)S(1)}, s32[1,2,64]{2,1,0:T(2,128)}, u32[]{:S(2)}) copy-start(s32[1,2,64]{2,1,0:T(2,128)} %param.13) | copy-start | bytes 1540
  100.8 94.5 %all-gather.4.cloned.1.call-start = ((), (), s32[]{:S(2)}) async-start(), calls=%async_computation.3 | async-start | bytes 1081344 | tf_op jit(solution)/shard_map/all_gather | solution.py:67
  101.5 141.8 %copy-start = (bf16[128,1024]{1,0:T(8,128)(2,1)S(1)}, bf16[128,1024]{1,0:T(8,128)(2,1)}, u32[]{:S(2)}) copy-start(bf16[128,1024]{1,0:T(8,128)(2,1)} %param.10) | copy-start | bytes 786436
  101.5 134.5 %all-gather.6.cloned.1.call-start = ((), (), s32[]{:S(2)}) async-start(), calls=%async_computation.4 | async-start | bytes 2621440 | tf_op jit(solution)/shard_map/all_gather | solution.py:68
  102.3 227.9 %reduce-scatter.4.cloned.1.call-start = ((), (), s32[]{:S(2)}) async-start(), calls=%async_computation.5 | async-start | bytes 1114112
Sparse Core Ops, SparseCore 0:
  103.7 91.5 all-gather.3
  197.4 38.5 all-gather.5
  240.6 89.4 reduce-scatter.3

commit v8 on v7

--- a/solution.py
+++ b/solution.py
@@ -72,8 +72,8 @@
     spread = jnp.where(
         head_slot[None, :, None, None], part.astype(jnp.bfloat16)[:, None], jnp.zeros((), jnp.bfloat16)
     )
-    spread = spread.reshape(-1, part.shape[1], part.shape[2])
-    fresh = lax.psum_scatter(spread, ("px", "tp"), scatter_dimension=0, tiled=True)[0]
+    moved = lax.psum_scatter(spread, "px", scatter_dimension=0, tiled=True)
+    fresh = lax.psum_scatter(moved[0], "tp", scatter_dimension=0, tiled=True)[0]
 
     count = hidden_rows.shape[0]
     group = QH // KVH
@@ -89,13 +89,12 @@
     near_mask = token_of_row[:, None] >= jnp.arange(count)[None, :]
     q_heads = queries.reshape(count, local_heads, group * HD)
     q_rows = q_heads[:, 0].reshape(count * group, HD)
-    near_keys = fresh[:, 0:HD]
-    near_vals = fresh[:, HD : 2 * HD]
-    near_scores = rows_by_keys(q_rows, near_keys) * scale
-    top = jnp.max(jnp.where(near_mask, near_scores, -1e30), axis=1)
-    weights = jnp.where(near_mask, jnp.exp(near_scores - top[:, None]), 0.0)
-    total = jnp.sum(weights, axis=1)
-    numer = jnp.dot(weights.astype(jnp.bfloat16), near_vals, preferred_element_type=jnp.float32)
+    rows = count * group
+    start = (
+        jnp.full((rows,), -1e30, jnp.float32),
+        jnp.zeros((rows,), jnp.float32),
+        jnp.zeros((rows, HD), jnp.float32),
+    )
 
     def visit(carry, block_rows):
         keys = block_rows[:, 0:HD]
@@ -103,7 +102,11 @@
         scores = rows_by_keys(q_rows, keys) * scale
         return (merge(carry, scores, mask, vals), None)
 
-    (top, total, numer), unused = lax.scan(visit, (top, total, numer), grouped)
+    carry, unused = lax.scan(visit, start, grouped)
+    near_keys = fresh[:, 0:HD]
+    near_vals = fresh[:, HD : 2 * HD]
+    near_scores = rows_by_keys(q_rows, near_keys) * scale
+    top, total, numer = merge(carry, near_scores, near_mask, near_vals)
     results = (numer / total[:, None]).reshape(count, group * HD)
     attended = results.astype(jnp.bfloat16)
     return (attended, fresh)

time: 371 us -> 380 us (1.024)
  waiting for transfers between devices: 222 us -> 197 us
  other arithmetic: 10.5 us -> 27.8 us
  matrix products: 26.9 us -> 42.1 us
    unnamed x4, waiting for transfers between devices: 88.1 us -> 1.41 us
    reduce_scatter x0 -> x2, waiting for transfers between devices: none -> 62.3 us  [the longest x1 32.9 us: body(): moved = lax.psum_scatter(spread, 'px', scatter_dimension=0, tiled=True)]
    convert_element_type x8, other arithmetic: 7.51 us -> 25 us  [merge(): weights_now.astype(jnp.bfloat16)]
    dot_general x9, matrix products: 7.06 us -> 22.7 us  [rows_by_keys(): lax.dot_general(left, right, (((1,), (1,)), ((), ())), preferred_element_...]
    dot_general x8 -> x9, matrix products: 7.84 us -> 8.49 us  [merge(): jnp.dot(weights_now.astype(jnp.bfloat16), vals, preferred_element_type=jn...]
  transfers between devices with their start and end apart: 4 -> 5, of which waited for: 3 -> 4; matrix products, arithmetic and copies ran while one was open for 3% -> 2% of each run, Pallas kernels for 0% -> 0%
where the time goes in v8:
time: 380 us; the launch traced here: 379 us
  waiting for transfers between devices  197 us (52%)
  blocking collectives  75.4 us (20%)
  matrix products  42.1 us (11%)
  other arithmetic  27.8 us (7%)
  local copies, waits for them, and re-layouts  14.4 us (4%)
  between operations  14 us (4%)
  starting transfers between devices  7.35 us (2%)
    all_gather x1, waiting for transfers between devices, body(): w_head = lax.all_gather(kv_weight, ('pz', 'pc'), axis=1, tiled=True)  91.7 us
    all_to_all x1, blocking collectives, body(): lax.all_to_all(outgoing, POOL, split_axis=1, concat_axis=0, tiled=True)  75.4 us
    all_gather x1, waiting for transfers between devices, body(): h_ring = lax.all_gather(hidden_rows, 'px', axis=0, tiled=False)  42.1 us
    reduce_scatter x1, waiting for transfers between devices, body(): moved = lax.psum_scatter(spread, 'px', scatter_dimension=0, tiled=True)  32.9 us
    reduce_scatter x1, waiting for transfers between devices, body(): fresh = lax.psum_scatter(moved[0], 'tp', scatter_dimension=0, tiled=True)[0]  29.4 us
    convert_element_type x8, other arithmetic, merge(): weights_now.astype(jnp.bfloat16)  25 us
    dot_general x9, matrix products, rows_by_keys(): lax.dot_general(left, right, (((1,), (1,)), ((), ())), preferred_element_...  22.7 us
    squeeze x8, local copies, waits for them, and re-layouts, body(): carry, unused = lax.scan(visit, start, grouped)  8.67 us
  transfers between devices with their start and end apart: 5, of which 4 were waited for; matrix products, arithmetic and copies ran while one was open for 2% of the time, Pallas kernels for 0%

profile of v8, /device:TPU:2, one launch (start us, length us, event | category | flops | bytes accessed | tf_op | source)
XLA Modules:
  0.0 378.9 jit_solution(8121629199005781808)
XLA Ops:
  7.2 0.7 fusion.32
  7.8 1.3 copy.11
  9.2 0.1 pad_maximum_fusion.1
  9.3 0.1 broadcast_in_dim.74
  9.3 0.2 pad_maximum_fusion
  9.5 75.4 %all_to_all.20 = bf16[9,128,256]{2,0,1:T(8,128)(2,1)S(1)} all-to-all(bf16[9,128,256]{2,0,1:T(8,128)(2,1)S(1)} %pad_maximum_fusion), channel_id=1, replica_groups=mesh['px'=4,'pz'=16,'pc'=2,'tp'=4] {'px','pz','pc'}, dimensions={1} | all-to-all | bytes 1179648 | tf_op jit(solution)/shard_map/all_to_all | solution.py:51
  84.9 0.1 slice_convert_fusion
  85.0 0.1 fusion.23
  85.1 0.1 eq.27
  85.2 8.4 %fusion.12 = bf16[8192,256]{1,0:T(8,128)(2,1)} fusion(s32[8192]{0:T(1024)S(1)} %eq.27, bf16[128,9,256]{2,1,0:T(8,128)(2,1)S(1)} %bitcast.84), kind=kOutput, calls=%fused_computation.22 | convolution fusion | flops 4305453056 | bytes 4751360 | tf_op jit(solution)/shard_map/dot_general | solution.py:62
  93.6 7.2 %all-to-all-start.1 = ((bf16[128,64,1,256]{3,1,2,0:T(8,128)(2,1)}), bf16[128,64,1,256]{3,1,2,0:T(8,128)(2,1)}, u32[]{:S(2)}, u32[]{:S(2)}) async-start(bf16[128,64,1,256]{3,1,2,0:T(8,128)(2,1)} %bitcast.82), calls=%async_computation.1 | async-start | bytes 8388608 | tf_op jit(solution)/shard_map/all_to_all | solution.py:65
  100.8 0.0 all-gather.4.cloned.1.call-start
  100.8 0.7 all-gather.4.cloned.1.call-update
  101.5 0.0 all-gather.6.cloned.1.call-start
  101.6 0.7 all-gather.6.cloned.1.call-update
  102.3 0.0 reduce-scatter.3.cloned.1.call-start
  102.3 91.7 %all-gather.4.cloned.1.call-done = bf16[2048,256]{0,1:T(8,128)(2,1)} async-done(((bf16[2048,8]{0,1:T(8,128)(2,1)}), bf16[2048,256]{0,1:T(8,128)(2,1)}) %all-gather.4.cloned.1.call-update) | async-done | bytes 1048592 | tf_op jit(solution)/shard_map/all_gather | solution.py:67
  194.1 42.1 %all-gather.6.cloned.1.call-done = bf16[512,2048]{1,0:T(8,128)(2,1)} async-done(((bf16[128,2048]{1,0:T(8,128)(2,1)}), bf16[512,2048]{1,0:T(8,128)(2,1)}) %all-gather.6.cloned.1.call-update) | async-done | bytes 2097168 | tf_op jit(solution)/shard_map/all_gather | solution.py:68
  236.1 2.6 convolution_convert_fusion
  238.7 1.2 broadcast_select_fusion
  240.0 0.0 reduce-scatter.5.cloned.1.call-start
  240.0 32.9 %reduce-scatter.3.cloned.1.call-done = bf16[1,4,128,256]{3,2,1,0:T(8,128)(2,1)} async-done(((bf16[4,4,128,256]{3,2,1,0:T(8,128)(2,1)}), bf16[1,4,128,256]{3,2,1,0:T(8,128)(2,1)}) %reduce-scatter.3.cloned.1.call-update) | async-done | bytes 262160 | tf_op jit(solution)/shard_map/reduce_scatter | solution.py:75
  273.0 0.1 reshape_squeeze_reshape.3
  273.1 3.0 gather_fusion
  276.2 0.2 broadcast_select_fusion.1
  276.4 0.2 copy.13
  276.6 29.4 %reduce-scatter.5.cloned.1.call-done = bf16[1,128,256]{2,1,0:T(8,128)(2,1)} async-done(((bf16[4,128,256]{2,1,0:T(8,128)(2,1)}), bf16[1,128,256]{2,1,0:T(8,128)(2,1)}) %reduce-scatter.5.cloned.1.call-update) | async-done | bytes 65552 | tf_op jit(solution)/shard_map/reduce_scatter | solution.py:76
  306.0 1.0 select_reduce_fusion
  307.0 63.8 %while.15 = (s32[]{:T(128)}, f32[1024]{0:T(1024)S(1)}, f32[1024]{0:T(1024)S(1)}, f32[1024,128]{1,0:T(8,128)S(1)}, bf16[8,1024,256]{2,1,0:T(8,128)(2,1)}, /*index...) while((s32[]{:T(128)}, f32[1024]{0:T(1024)S(1)}, ...), condition=%wide.region_3.4_spmd.clone, body=%wide.region_0.3_spmd.clone.sunk | while | flops 545657856 | bytes 15659125 | solution.py:105
  307.1 1.1 dynamic-slice_bitcast_fusion.2
  308.2 2.7 fusion.47
  310.9 3.1 fusion.48
  314.0 1.0 convolution_add_fusion.3
  315.1 1.1 dynamic-slice_bitcast_fusion.2
  316.2 2.7 fusion.47
  318.9 3.1 fusion.48
  322.0 1.0 convolution_add_fusion.3
  323.0 1.1 dynamic-slice_bitcast_fusion.2
  324.1 2.7 fusion.47
  326.8 3.1 fusion.48
  330.0 1.0 convolution_add_fusion.3
  331.0 1.1 dynamic-slice_bitcast_fusion.2
  332.1 2.7 fusion.47
  334.8 3.1 fusion.48
  338.0 1.0 convolution_add_fusion.3
  339.0 1.1 dynamic-slice_bitcast_fusion.2
  340.1 2.7 fusion.47
  342.8 3.1 fusion.48
  345.9 1.0 convolution_add_fusion.3
  347.0 1.1 dynamic-slice_bitcast_fusion.2
  348.1 2.7 fusion.47
  350.8 3.1 fusion.48
  353.9 1.0 convolution_add_fusion.3
  354.9 1.1 dynamic-slice_bitcast_fusion.2
  356.0 2.7 fusion.47
  358.7 3.1 fusion.48
  361.9 1.0 convolution_add_fusion.3
  362.9 1.1 dynamic-slice_bitcast_fusion.2
  364.0 2.7 fusion.47
  366.7 3.1 fusion.48
  369.9 1.0 convolution_add_fusion.3
  370.9 0.1 fusion.17
  371.0 0.5 fusion.15
  371.5 0.8 convert_element_type.43
  (46 shorter events, 0.3 us)
Async XLA Ops:
  93.6 213.4 %all-to-all-start.1 = ((bf16[128,64,1,256]{3,1,2,0:T(8,128)(2,1)}), bf16[128,64,1,256]{3,1,2,0:T(8,128)(2,1)}, u32[]{:S(2)}, u32[]{:S(2)}) async-start(bf16[128,64,1,256]{3,1,2,0:T(8,128)(2,1)} %bitcast.82), calls=%async_computation.1 | async-start | bytes 8388608 | tf_op jit(solution)/shard_map/all_to_all | solution.py:65
  100.8 172.2 %copy-start.2 = (s32[1,2,64]{2,1,0:T(2,128)S(1)}, s32[1,2,64]{2,1,0:T(2,128)}, u32[]{:S(2)}) copy-start(s32[1,2,64]{2,1,0:T(2,128)} %param.13) | copy-start | bytes 1540
  100.8 172.2 %copy-start = (bf16[128,1024]{1,0:T(8,128)(2,1)S(1)}, bf16[128,1024]{1,0:T(8,128)(2,1)}, u32[]{:S(2)}) copy-start(bf16[128,1024]{1,0:T(8,128)(2,1)} %param.10) | copy-start | bytes 786436
  100.8 93.3 %all-gather.4.cloned.1.call-start = ((), (), s32[]{:S(2)}) async-start(), calls=%async_computation.4 | async-start | bytes 1081344 | tf_op jit(solution)/shard_map/all_gather | solution.py:67
  101.5 134.6 %all-gather.6.cloned.1.call-start = ((), (), s32[]{:S(2)}) async-start(), calls=%async_computation.7 | async-start | bytes 2621440 | tf_op jit(solution)/shard_map/all_gather | solution.py:68
  102.3 170.6 %reduce-scatter.3.cloned.1.call-start = ((), (), s32[]{:S(2)}) async-start(), calls=%async_computation.5 | async-start | bytes 1310720 | tf_op jit(solution)/shard_map/reduce_scatter | solution.py:75
  240.0 66.1 %reduce-scatter.5.cloned.1.call-start = ((), (), s32[]{:S(2)}) async-start(), calls=%async_computation.6 | async-start | bytes 327680 | tf_op jit(solution)/shard_map/reduce_scatter | solution.py:76
  307.0 64.0 %copy-start.1 = (bf16[1,128,256]{2,1,0:T(8,128)(2,1)S(1)}, bf16[1,128,256]{2,1,0:T(8,128)(2,1)}, u32[]{:S(2)}) copy-start(bf16[1,128,256]{2,1,0:T(8,128)(2,1)} %reduce-scatter.5.cloned.1.call-done) | copy-start | bytes 196612
Sparse Core Ops, SparseCore 0:
  103.8 90.2 all-gather.3
  196.2 39.9 all-gather.5
  240.1 32.7 reduce-scatter.2
  276.4 29.5 reduce-scatter.4

commit v9 on v7

--- a/solution.py
+++ b/solution.py
@@ -72,8 +72,8 @@
     spread = jnp.where(
         head_slot[None, :, None, None], part.astype(jnp.bfloat16)[:, None], jnp.zeros((), jnp.bfloat16)
     )
-    spread = spread.reshape(-1, part.shape[1], part.shape[2])
-    fresh = lax.psum_scatter(spread, ("px", "tp"), scatter_dimension=0, tiled=True)[0]
+    moved = lax.psum_scatter(spread, "px", scatter_dimension=0, tiled=True)
+    fresh = lax.psum_scatter(moved[0], "tp", scatter_dimension=0, tiled=True)[0]
 
     count = hidden_rows.shape[0]
     group = QH // KVH

time: 371 us -> 347 us (0.935)
  the two profiles are of different devices: /device:TPU:2 before, /device:TPU:4 now
where the time goes in v9:
time: 347 us; the launch traced here: 346 us
  waiting for transfers between devices  197 us (57%)
  blocking collectives  75.3 us (22%)
  matrix products  26.9 us (8%)
  local copies, waits for them, and re-layouts  14.3 us (4%)
  between operations  14 us (4%)
  other arithmetic  10.5 us (3%)
  starting transfers between devices  7.64 us (2%)
    all_gather x1, waiting for transfers between devices, body(): w_head = lax.all_gather(kv_weight, ('pz', 'pc'), axis=1, tiled=True)  92.9 us
    all_to_all x1, blocking collectives, body(): lax.all_to_all(outgoing, POOL, split_axis=1, concat_axis=0, tiled=True)  75.3 us
    all_gather x1, waiting for transfers between devices, body(): h_ring = lax.all_gather(hidden_rows, 'px', axis=0, tiled=False)  40.2 us
    reduce_scatter x1, waiting for transfers between devices, body(): moved = lax.psum_scatter(spread, 'px', scatter_dimension=0, tiled=True)  32.5 us
    reduce_scatter x1, waiting for transfers between devices, body(): fresh = lax.psum_scatter(moved[0], 'tp', scatter_dimension=0, tiled=True)[0]  30.1 us
    squeeze x8, local copies, waits for them, and re-layouts, body(): (top, total, numer), unused = lax.scan(visit, (top, total, numer), grouped)  8.64 us
    dot_general x1, matrix products, body(): jnp.dot(picks, table, preferred_element_type=jnp.float32)  8.36 us
    dot_general x8, matrix products, merge(): jnp.dot(weights_now.astype(jnp.bfloat16), vals, preferred_element_type=jn...  7.84 us
  transfers between devices with their start and end apart: 5, of which 4 were waited for; matrix products, arithmetic and copies ran while one was open for 3% of the time, Pallas kernels for 0%

profile of v9, /device:TPU:4, one launch (start us, length us, event | category | flops | bytes accessed | tf_op | source)
XLA Modules:
  0.0 346.2 jit_solution(15562863635210758173)
XLA Ops:
  7.2 0.7 fusion.30
  7.8 1.3 copy.11
  9.2 0.1 pad_maximum_fusion.1
  9.3 0.1 broadcast_in_dim.64
  9.3 0.2 pad_maximum_fusion
  9.5 75.3 %all_to_all.20 = bf16[9,128,256]{2,0,1:T(8,128)(2,1)S(1)} all-to-all(bf16[9,128,256]{2,0,1:T(8,128)(2,1)S(1)} %pad_maximum_fusion), channel_id=1, replica_groups=mesh['px'=4,'pz'=16,'pc'=2,'tp'=4] {'px','pz','pc'}, dimensions={1} | all-to-all | bytes 1179648 | tf_op jit(solution)/shard_map/all_to_all | solution.py:51
  84.8 0.1 slice_convert_fusion
  84.9 0.1 fusion.21
  85.0 0.1 eq.29
  85.1 8.4 %fusion.11 = bf16[8192,256]{1,0:T(8,128)(2,1)} fusion(s32[8192]{0:T(1024)S(1)} %eq.29, bf16[128,9,256]{2,1,0:T(8,128)(2,1)S(1)} %bitcast.84), kind=kOutput, calls=%fused_computation.19 | convolution fusion | flops 4305453056 | bytes 4751360 | tf_op jit(solution)/shard_map/dot_general | solution.py:62
  93.5 7.5 %all-to-all-start.1 = ((bf16[128,64,1,256]{3,1,2,0:T(8,128)(2,1)}), bf16[128,64,1,256]{3,1,2,0:T(8,128)(2,1)}, u32[]{:S(2)}, u32[]{:S(2)}) async-start(bf16[128,64,1,256]{3,1,2,0:T(8,128)(2,1)} %bitcast.82), calls=%async_computation.3 | async-start | bytes 8388608 | tf_op jit(solution)/shard_map/all_to_all | solution.py:65
  101.0 0.0 all-gather.4.cloned.1.call-start
  101.0 0.7 all-gather.4.cloned.1.call-update
  101.8 0.7 all-gather.6.cloned.1.call-update
  102.5 0.0 reduce-scatter.3.cloned.1.call-start
  102.5 92.9 %all-gather.4.cloned.1.call-done = bf16[2048,256]{0,1:T(8,128)(2,1)} async-done(((bf16[2048,8]{0,1:T(8,128)(2,1)}), bf16[2048,256]{0,1:T(8,128)(2,1)}) %all-gather.4.cloned.1.call-update) | async-done | bytes 1048592 | tf_op jit(solution)/shard_map/all_gather | solution.py:67
  195.4 40.2 %all-gather.6.cloned.1.call-done = bf16[512,2048]{1,0:T(8,128)(2,1)} async-done(((bf16[128,2048]{1,0:T(8,128)(2,1)}), bf16[512,2048]{1,0:T(8,128)(2,1)}) %all-gather.6.cloned.1.call-update) | async-done | bytes 2097168 | tf_op jit(solution)/shard_map/all_gather | solution.py:68
  235.6 2.6 convolution_convert_fusion
  238.2 1.2 broadcast_select_fusion
  239.5 0.0 reduce-scatter.5.cloned.1.call-start
  239.5 32.5 %reduce-scatter.3.cloned.1.call-done = bf16[1,4,128,256]{3,2,1,0:T(8,128)(2,1)} async-done(((bf16[4,4,128,256]{3,2,1,0:T(8,128)(2,1)}), bf16[1,4,128,256]{3,2,1,0:T(8,128)(2,1)}) %reduce-scatter.3.cloned.1.call-update) | async-done | bytes 262160 | tf_op jit(solution)/shard_map/reduce_scatter | solution.py:75
  272.1 3.0 gather_fusion
  275.1 0.2 broadcast_select_fusion.1
  275.3 0.2 copy.13
  275.5 0.1 reshape_squeeze_reshape.3
  275.7 30.1 %reduce-scatter.5.cloned.1.call-done = bf16[1,128,256]{2,1,0:T(8,128)(2,1)} async-done(((bf16[4,128,256]{2,1,0:T(8,128)(2,1)}), bf16[1,128,256]{2,1,0:T(8,128)(2,1)}) %reduce-scatter.5.cloned.1.call-update) | async-done | bytes 65552 | tf_op jit(solution)/shard_map/reduce_scatter | solution.py:76
  305.8 1.0 select_reduce_fusion
  306.8 0.1 fusion.15
  306.9 1.0 fusion.16
  307.9 30.7 %while.15 = (s32[]{:T(128)}, f32[1024]{0:T(1024)S(1)}, f32[1024]{0:T(1024)S(1)}, f32[1024,128]{1,0:T(8,128)S(1)}, bf16[8,1024,256]{2,1,0:T(8,128)(2,1)}, /*index...) while((s32[]{:T(128)}, f32[1024]{0:T(1024)S(1)}, f32[1024]{0:T(1024)S(1)}, ...), condition=%wide.region_7.8_spmd.clone, body=%wide.region_4.7_spmd.clone.sunk | while | flops 545523712 | bytes 15659105 | solution.py:106
  308.0 1.1 dynamic-slice_bitcast_fusion.2
  309.0 0.8 fusion.44
  309.8 0.9 fusion.45
  310.8 1.0 convolution_add_fusion.2
  311.8 1.1 dynamic-slice_bitcast_fusion.2
  312.9 0.8 fusion.44
  313.7 0.9 fusion.45
  314.6 1.0 convolution_add_fusion.2
  315.6 1.1 dynamic-slice_bitcast_fusion.2
  316.7 0.8 fusion.44
  317.5 0.9 fusion.45
  318.5 1.0 convolution_add_fusion.2
  319.5 1.1 dynamic-slice_bitcast_fusion.2
  320.5 0.8 fusion.44
  321.3 0.9 fusion.45
  322.3 1.0 convolution_add_fusion.2
  323.3 1.1 dynamic-slice_bitcast_fusion.2
  324.4 0.8 fusion.44
  325.2 0.9 fusion.45
  326.1 1.0 convolution_add_fusion.2
  327.1 1.1 dynamic-slice_bitcast_fusion.2
  328.2 0.8 fusion.44
  329.0 0.9 fusion.45
  329.9 1.0 convolution_add_fusion.2
  330.9 1.1 dynamic-slice_bitcast_fusion.2
  332.0 0.8 fusion.44
  332.8 0.9 fusion.45
  333.8 1.0 convolution_add_fusion.2
  334.8 1.1 dynamic-slice_bitcast_fusion.2
  335.9 0.8 fusion.44
  336.6 0.9 fusion.45
  337.6 1.0 convolution_add_fusion.2
  338.6 0.2 divide_convert_fusion
  338.8 0.8 convert_element_type.43
  (40 shorter events, 0.3 us)
Async XLA Ops:
  93.5 214.5 %all-to-all-start.1 = ((bf16[128,64,1,256]{3,1,2,0:T(8,128)(2,1)}), bf16[128,64,1,256]{3,1,2,0:T(8,128)(2,1)}, u32[]{:S(2)}, u32[]{:S(2)}) async-start(bf16[128,64,1,256]{3,1,2,0:T(8,128)(2,1)} %bitcast.82), calls=%async_computation.3 | async-start | bytes 8388608 | tf_op jit(solution)/shard_map/all_to_all | solution.py:65
  101.0 171.1 %copy-start.1 = (s32[1,2,64]{2,1,0:T(2,128)S(1)}, s32[1,2,64]{2,1,0:T(2,128)}, u32[]{:S(2)}) copy-start(s32[1,2,64]{2,1,0:T(2,128)} %param.13) | copy-start | bytes 1540
  101.0 94.5 %all-gather.4.cloned.1.call-start = ((), (), s32[]{:S(2)}) async-start(), calls=%async_computation.4 | async-start | bytes 1081344 | tf_op jit(solution)/shard_map/all_gather | solution.py:67
  101.7 133.9 %all-gather.6.cloned.1.call-start = ((), (), s32[]{:S(2)}) async-start(), calls=%async_computation.7 | async-start | bytes 2621440 | tf_op jit(solution)/shard_map/all_gather | solution.py:68
  102.5 173.1 %copy-start = (bf16[128,1024]{1,0:T(8,128)(2,1)S(1)}, bf16[128,1024]{1,0:T(8,128)(2,1)}, u32[]{:S(2)}) copy-start(bf16[128,1024]{1,0:T(8,128)(2,1)} %param.10) | copy-start | bytes 786436
  102.5 169.5 %reduce-scatter.3.cloned.1.call-start = ((), (), s32[]{:S(2)}) async-start(), calls=%async_computation.5 | async-start | bytes 1310720 | tf_op jit(solution)/shard_map/reduce_scatter | solution.py:75
  239.5 66.3 %reduce-scatter.5.cloned.1.call-start = ((), (), s32[]{:S(2)}) async-start(), calls=%async_computation.6 | async-start | bytes 327680 | tf_op jit(solution)/shard_map/reduce_scatter | solution.py:76
Sparse Core Ops, SparseCore 0:
  103.9 91.4 all-gather.3
  197.5 38.0 all-gather.5
  239.6 32.3 reduce-scatter.2
  275.5 30.2 reduce-scatter.4

commit v10 on v9

--- a/solution.py
+++ b/solution.py
@@ -48,8 +48,14 @@
     )
     id_block = jnp.broadcast_to(id_row[None, None, :], (1, blk, width))
     outgoing = jnp.concatenate([cache_table, id_block], axis=0)
-    by_token = lax.all_to_all(outgoing, POOL, split_axis=1, concat_axis=0, tiled=True)
-    by_token = by_token.reshape(npool, blocks_dev + 1, width)
+    nx, nz, nc = (lax.axis_size(a) for a in POOL)
+    rows_out = blocks_dev + 1
+    step = outgoing.reshape(rows_out, nx, nz, nc, width)
+    step = lax.all_to_all(step, "pz", split_axis=2, concat_axis=2, tiled=True)
+    step = step.transpose(0, 1, 3, 2, 4).reshape(rows_out, nx * nc, nz, width)
+    step = lax.all_to_all(step, ("px", "pc"), split_axis=1, concat_axis=1, tiled=True)
+    step = step.reshape(rows_out, nx, nc, nz, width).transpose(1, 3, 2, 0, 4)
+    by_token = step.reshape(npool, rows_out, width)
     table = by_token[:, :blocks_dev].reshape(npool * blocks_dev, width)
     id_rows = by_token[:, blocks_dev].astype(jnp.float32)
     wanted_all = (

time: 347 us -> 338 us (0.974)
  the two profiles are of different devices: /device:TPU:4 before, /device:TPU:2 now
where the time goes in v10:
time: 338 us; the launch traced here: 337 us
  waiting for transfers between devices  197 us (58%)
  blocking collectives  64.2 us (19%)
  matrix products  27.7 us (8%)
  local copies, waits for them, and re-layouts  14.5 us (4%)
  between operations  14 us (4%)
  other arithmetic  11.3 us (3%)
  starting transfers between devices  8.15 us (2%)
    all_gather x1, waiting for transfers between devices, body(): w_head = lax.all_gather(kv_weight, ('pz', 'pc'), axis=1, tiled=True)  92.8 us
    all_to_all x1, blocking collectives, body(): step = lax.all_to_all(step, 'pz', split_axis=2, concat_axis=2, tiled=True)  49.9 us
    all_gather x1, waiting for transfers between devices, body(): h_ring = lax.all_gather(hidden_rows, 'px', axis=0, tiled=False)  40.7 us
    reduce_scatter x1, waiting for transfers between devices, body(): moved = lax.psum_scatter(spread, 'px', scatter_dimension=0, tiled=True)  32.8 us
    reduce_scatter x1, waiting for transfers between devices, body(): fresh = lax.psum_scatter(moved[0], 'tp', scatter_dimension=0, tiled=True)[0]  29.1 us
    all_to_all x1, blocking collectives, body(): lax.all_to_all(step, ('px', 'pc'), split_axis=1, concat_axis=1, tiled=True)  14.3 us
    dot_general x1, matrix products, body(): jnp.dot(picks, table, preferred_element_type=jnp.float32)  9.17 us
    squeeze x8, local copies, waits for them, and re-layouts, body(): (top, total, numer), unused = lax.scan(visit, (top, total, numer), grouped)  8.64 us
  transfers between devices with their start and end apart: 5, of which 4 were waited for; matrix products, arithmetic and copies ran while one was open for 3% of the time, Pallas kernels for 0%

profile of v10, /device:TPU:2, one launch (start us, length us, event | category | flops | bytes accessed | tf_op | source)
XLA Modules:
  0.0 337.0 jit_solution(4702239854958198335)
XLA Ops:
  7.2 0.7 fusion.33
  7.8 0.1 pad_maximum_fusion.1
  7.9 1.1 pad_maximum_fusion
  9.0 0.2 reshape.154
  9.3 0.4 copy.15
  9.7 49.9 %all_to_all.15 = bf16[9,4,16,2,256]{4,3,1,0,2:T(2,128)(2,1)S(1)} all-to-all(bf16[9,4,16,2,256]{4,3,1,0,2:T(2,128)(2,1)S(1)} %copy.15), channel_id=1, replica_groups=mesh['px'=4,'pz'=16,'pc'=2,'tp'=4] {'pz'}, dimensions={2} | all-to-all | bytes 1179648 | tf_op jit(solution)/shard_map/all_to_all | solution.py:54
  59.6 0.1 copy.22
  59.7 14.3 %all_to_all.16 = bf16[9,8,16,256]{3,2,0,1:T(8,128)(2,1)S(1)} all-to-all(bf16[9,8,16,256]{3,2,0,1:T(8,128)(2,1)S(1)} %bitcast.89), channel_id=1, replica_groups=mesh['px'=4,'pz'=16,'pc'=2,'tp'=4] {'px','pc'}, dimensions={1} | all-to-all | bytes 1179648 | tf_op jit(solution)/shard_map/all_to_all | solution.py:56
  74.0 0.6 copy.28
  74.6 0.2 reshape.157
  74.9 0.1 fusion.23
  75.0 0.1 eq.29
  75.0 9.2 %fusion.11 = bf16[8192,256]{1,0:T(8,128)(2,1)} fusion(s32[8192]{0:T(1024)S(1)} %eq.29, bf16[128,8,256]{2,0,1:T(8,128)(2,1)S(1)} %slice.39), kind=kOutput, calls=%fused_computation.19 | convolution fusion | flops 4305453056 | bytes 4751360 | tf_op jit(solution)/shard_map/dot_general | solution.py:68
  84.2 8.0 %all-to-all-start.2 = ((bf16[128,64,1,256]{3,1,2,0:T(8,128)(2,1)}), bf16[128,64,1,256]{3,1,2,0:T(8,128)(2,1)}, u32[]{:S(2)}, u32[]{:S(2)}) async-start(bf16[128,64,1,256]{3,1,2,0:T(8,128)(2,1)} %bitcast.88), calls=%async_computation.4 | async-start | bytes 8388608 | tf_op jit(solution)/shard_map/all_to_all | solution.py:71
  92.3 0.7 all-gather.4.cloned.1.call-update
  93.0 0.7 all-gather.6.cloned.1.call-update
  93.8 92.8 %all-gather.4.cloned.1.call-done = bf16[2048,256]{0,1:T(8,128)(2,1)} async-done(((bf16[2048,8]{0,1:T(8,128)(2,1)}), bf16[2048,256]{0,1:T(8,128)(2,1)}) %all-gather.4.cloned.1.call-update) | async-done | bytes 1048592 | tf_op jit(solution)/shard_map/all_gather | solution.py:73
  186.6 40.7 %all-gather.6.cloned.1.call-done = bf16[512,2048]{1,0:T(8,128)(2,1)} async-done(((bf16[128,2048]{1,0:T(8,128)(2,1)}), bf16[512,2048]{1,0:T(8,128)(2,1)}) %all-gather.6.cloned.1.call-update) | async-done | bytes 2097168 | tf_op jit(solution)/shard_map/all_gather | solution.py:74
  227.3 2.6 convolution_convert_fusion
  229.9 1.2 broadcast_select_fusion
  231.2 32.8 %reduce-scatter.3.cloned.1.call-done = bf16[1,4,128,256]{3,2,1,0:T(8,128)(2,1)} async-done(((bf16[4,4,128,256]{3,2,1,0:T(8,128)(2,1)}), bf16[1,4,128,256]{3,2,1,0:T(8,128)(2,1)}) %reduce-scatter.3.cloned.1.call-update) | async-done | bytes 262160 | tf_op jit(solution)/shard_map/reduce_scatter | solution.py:81
  264.0 3.0 gather_fusion
  267.0 0.2 broadcast_select_fusion.1
  267.2 0.2 copy.21
  267.4 0.1 reshape_squeeze_reshape.3
  267.6 29.1 %reduce-scatter.5.cloned.1.call-done = bf16[1,128,256]{2,1,0:T(8,128)(2,1)} async-done(((bf16[4,128,256]{2,1,0:T(8,128)(2,1)}), bf16[1,128,256]{2,1,0:T(8,128)(2,1)}) %reduce-scatter.5.cloned.1.call-update) | async-done | bytes 65552 | tf_op jit(solution)/shard_map/reduce_scatter | solution.py:82
  296.6 1.0 select_reduce_fusion
  297.7 0.1 fusion.17
  297.8 1.0 fusion.18
  298.8 30.6 %while.15 = (s32[]{:T(128)}, f32[1024]{0:T(1024)S(1)}, f32[1024]{0:T(1024)S(1)}, f32[1024,128]{1,0:T(8,128)S(1)}, bf16[8,1024,256]{2,1,0:T(8,128)(2,1)}, /*index...) while((s32[]{:T(128)}, f32[1024]{0:T(1024)S(1)}, f32[1024]{0:T(1024)S(1)}, ...), condition=%wide.region_7.8_spmd.clone, body=%wide.region_4.7_spmd.clone.sunk | while | flops 545523712 | bytes 15659105 | solution.py:112
  298.9 1.1 dynamic-slice_bitcast_fusion.2
  299.9 0.7 fusion.47
  300.7 0.9 fusion.48
  301.7 1.0 convolution_add_fusion.2
  302.7 1.1 dynamic-slice_bitcast_fusion.2
  303.8 0.8 fusion.47
  304.5 0.9 fusion.48
  305.5 1.0 convolution_add_fusion.2
  306.5 1.1 dynamic-slice_bitcast_fusion.2
  307.6 0.8 fusion.47
  308.4 0.9 fusion.48
  309.3 1.0 convolution_add_fusion.2
  310.3 1.1 dynamic-slice_bitcast_fusion.2
  311.4 0.8 fusion.47
  312.2 0.9 fusion.48
  313.2 1.0 convolution_add_fusion.2
  314.2 1.1 dynamic-slice_bitcast_fusion.2
  315.2 0.8 fusion.47
  316.0 0.9 fusion.48
  317.0 1.0 convolution_add_fusion.2
  318.0 1.1 dynamic-slice_bitcast_fusion.2
  319.1 0.8 fusion.47
  319.9 0.9 fusion.48
  320.8 1.0 convolution_add_fusion.2
  321.8 1.1 dynamic-slice_bitcast_fusion.2
  322.9 0.8 fusion.47
  323.7 0.9 fusion.48
  324.7 1.0 convolution_add_fusion.2
  325.7 1.1 dynamic-slice_bitcast_fusion.2
  326.7 0.8 fusion.47
  327.5 0.9 fusion.48
  328.5 1.0 convolution_add_fusion.2
  329.5 0.2 divide_convert_fusion
  329.7 0.8 convert_element_type.43
  (45 shorter events, 0.5 us)
Async XLA Ops:
  84.2 214.6 %all-to-all-start.2 = ((bf16[128,64,1,256]{3,1,2,0:T(8,128)(2,1)}), bf16[128,64,1,256]{3,1,2,0:T(8,128)(2,1)}, u32[]{:S(2)}, u32[]{:S(2)}) async-start(bf16[128,64,1,256]{3,1,2,0:T(8,128)(2,1)} %bitcast.88), calls=%async_computation.4 | async-start | bytes 8388608 | tf_op jit(solution)/shard_map/all_to_all | solution.py:71
  92.2 171.7 %copy-start.1 = (s32[1,2,64]{2,1,0:T(2,128)S(1)}, s32[1,2,64]{2,1,0:T(2,128)}, u32[]{:S(2)}) copy-start(s32[1,2,64]{2,1,0:T(2,128)} %param.13) | copy-start | bytes 1540
  92.2 94.4 %all-gather.4.cloned.1.call-start = ((), (), s32[]{:S(2)}) async-start(), calls=%async_computation.5 | async-start | bytes 1081344 | tf_op jit(solution)/shard_map/all_gather | solution.py:73
  93.0 134.3 %all-gather.6.cloned.1.call-start = ((), (), s32[]{:S(2)}) async-start(), calls=%async_computation.8 | async-start | bytes 2621440 | tf_op jit(solution)/shard_map/all_gather | solution.py:74
  93.7 173.7 %copy-start = (bf16[128,1024]{1,0:T(8,128)(2,1)S(1)}, bf16[128,1024]{1,0:T(8,128)(2,1)}, u32[]{:S(2)}) copy-start(bf16[128,1024]{1,0:T(8,128)(2,1)} %param.10) | copy-start | bytes 786436
  93.7 170.2 %reduce-scatter.3.cloned.1.call-start = ((), (), s32[]{:S(2)}) async-start(), calls=%async_computation.6 | async-start | bytes 1310720 | tf_op jit(solution)/shard_map/reduce_scatter | solution.py:81
  231.1 65.6 %reduce-scatter.5.cloned.1.call-start = ((), (), s32[]{:S(2)}) async-start(), calls=%async_computation.7 | async-start | bytes 327680 | tf_op jit(solution)/shard_map/reduce_scatter | solution.py:82
Sparse Core Ops, SparseCore 0:
  95.2 91.3 all-gather.3
  188.7 38.5 all-gather.5
  231.2 32.6 reduce-scatter.2
  267.4 29.2 reduce-scatter.4

commit v11 on v10

--- a/solution.py
+++ b/solution.py
@@ -109,7 +109,7 @@
         scores = rows_by_keys(q_rows, keys) * scale
         return (merge(carry, scores, mask, vals), None)
 
-    (top, total, numer), unused = lax.scan(visit, (top, total, numer), grouped)
+    (top, total, numer), unused = lax.scan(visit, (top, total, numer), grouped, unroll=True)
     results = (numer / total[:, None]).reshape(count, group * HD)
     attended = results.astype(jnp.bfloat16)
     return (attended, fresh)

time: 338 us -> 356 us (1.053)
  matrix products: 27.7 us -> 42.2 us
  other arithmetic: 11.3 us -> 17.2 us
    dot_general x9, matrix products: 7.07 us -> 22.1 us  [rows_by_keys(): lax.dot_general(left, right, (((1,), (1,)), ((), ())), preferred_element_...]
    reduce_sum x0 -> x1, other arithmetic: none -> 13.7 us  [merge(): total_new = total_now * factor + jnp.sum(weights_now, axis=1)]
    squeeze x8 -> x0, local copies, waits for them, and re-layouts: 8.64 us -> none  [body(): (top, total, numer), unused = lax.scan(visit, (top, total, numer), grouped)]
    convert_element_type x9 -> x0, other arithmetic: 7.72 us -> none  [the longest x8 7.51 us: merge(): weights_now.astype(jnp.bfloat16)]
  transfers between devices with their start and end apart: 5 -> 5, of which waited for: 4 -> 4; matrix products, arithmetic and copies ran while one was open for 3% -> 2% of each run, Pallas kernels for 0% -> 0%
where the time goes in v11:
time: 356 us
  waiting for transfers between devices  197 us (55%)
  blocking collectives  64.2 us (18%)
  matrix products  42.2 us (12%)
  other arithmetic  17.2 us (5%)
  between operations  14.3 us (4%)
  local copies, waits for them, and re-layouts  12.6 us (4%)
  starting transfers between devices  8.14 us (2%)
    all_gather x1, waiting for transfers between devices, body(): w_head = lax.all_gather(kv_weight, ('pz', 'pc'), axis=1, tiled=True)  92.3 us
    all_to_all x1, blocking collectives, body(): step = lax.all_to_all(step, 'pz', split_axis=2, concat_axis=2, tiled=True)  49.9 us
    all_gather x1, waiting for transfers between devices, body(): h_ring = lax.all_gather(hidden_rows, 'px', axis=0, tiled=False)  41.5 us
    reduce_scatter x1, waiting for transfers between devices, body(): moved = lax.psum_scatter(spread, 'px', scatter_dimension=0, tiled=True)  32.8 us
    reduce_scatter x1, waiting for transfers between devices, body(): fresh = lax.psum_scatter(moved[0], 'tp', scatter_dimension=0, tiled=True)[0]  29.3 us
    dot_general x9, matrix products, rows_by_keys(): lax.dot_general(left, right, (((1,), (1,)), ((), ())), preferred_element_...  22.1 us
    all_to_all x1, blocking collectives, body(): lax.all_to_all(step, ('px', 'pc'), split_axis=1, concat_axis=1, tiled=True)  14.3 us
    reduce_sum x1, other arithmetic, merge(): total_new = total_now * factor + jnp.sum(weights_now, axis=1)  13.7 us
  transfers between devices with their start and end apart: 5, of which 4 were waited for; matrix products, arithmetic and copies ran while one was open for 2% of the time, Pallas kernels for 0%

profile of v11, /device:TPU:2, one launch (start us, length us, event | category | flops | bytes accessed | tf_op | source)
XLA Modules:
  0.0 355.9 jit_solution(3701149605787695406)
XLA Ops:
  7.2 0.7 fusion.88
  7.8 0.1 pad_maximum_fusion.1
  7.9 1.1 pad_maximum_fusion
  9.0 0.2 reshape.417
  9.3 0.4 copy.15
  9.7 49.9 %all_to_all.15 = bf16[9,4,16,2,256]{4,3,1,0,2:T(2,128)(2,1)S(1)} all-to-all(bf16[9,4,16,2,256]{4,3,1,0,2:T(2,128)(2,1)S(1)} %copy.15), channel_id=1, replica_groups=mesh['px'=4,'pz'=16,'pc'=2,'tp'=4] {'pz'}, dimensions={2} | all-to-all | bytes 1179648 | tf_op jit(solution)/shard_map/all_to_all | solution.py:54
  59.6 0.1 copy.22
  59.7 14.3 %all_to_all.16 = bf16[9,8,16,256]{3,2,0,1:T(8,128)(2,1)S(1)} all-to-all(bf16[9,8,16,256]{3,2,0,1:T(8,128)(2,1)S(1)} %bitcast.227), channel_id=1, replica_groups=mesh['px'=4,'pz'=16,'pc'=2,'tp'=4] {'px','pc'}, dimensions={1} | all-to-all | bytes 1179648 | tf_op jit(solution)/shard_map/all_to_all | solution.py:56
  74.0 0.6 copy.28
  74.6 0.2 reshape.420
  74.9 0.1 fusion.78
  75.0 0.1 eq.29
  75.0 9.1 %fusion.2 = bf16[8192,256]{1,0:T(8,128)(2,1)} fusion(s32[8192]{0:T(1024)S(1)} %eq.29, bf16[128,8,256]{2,0,1:T(8,128)(2,1)S(1)} %slice.133), kind=kOutput, calls=%fused_computation.20 | convolution fusion | flops 4305453056 | bytes 4751360 | tf_op jit(solution)/shard_map/dot_general | solution.py:68
  84.2 8.0 %all-to-all-start.2 = ((bf16[128,64,1,256]{3,1,2,0:T(8,128)(2,1)}), bf16[128,64,1,256]{3,1,2,0:T(8,128)(2,1)}, u32[]{:S(2)}, u32[]{:S(2)}) async-start(bf16[128,64,1,256]{3,1,2,0:T(8,128)(2,1)} %bitcast.226), calls=%async_computation.4 | async-start | bytes 8388608 | tf_op jit(solution)/shard_map/all_to_all | solution.py:71
  92.2 0.0 all-gather.4.cloned.1.call-start
  92.2 0.7 all-gather.4.cloned.1.call-update
  92.9 0.0 all-gather.6.cloned.1.call-start
  93.0 0.7 all-gather.6.cloned.1.call-update
  93.7 0.0 reduce-scatter.3.cloned.1.call-start
  93.7 92.3 %all-gather.4.cloned.1.call-done = bf16[2048,256]{0,1:T(8,128)(2,1)} async-done(((bf16[2048,8]{0,1:T(8,128)(2,1)}), bf16[2048,256]{0,1:T(8,128)(2,1)}) %all-gather.4.cloned.1.call-update) | async-done | bytes 1048592 | tf_op jit(solution)/shard_map/all_gather | solution.py:73
  186.1 41.5 %all-gather.6.cloned.1.call-done = bf16[512,2048]{1,0:T(8,128)(2,1)} async-done(((bf16[128,2048]{1,0:T(8,128)(2,1)}), bf16[512,2048]{1,0:T(8,128)(2,1)}) %all-gather.6.cloned.1.call-update) | async-done | bytes 2097168 | tf_op jit(solution)/shard_map/all_gather | solution.py:74
  227.5 2.6 convolution_convert_fusion
  230.2 1.2 broadcast_select_fusion
  231.4 0.0 reduce-scatter.3.cloned.1.call-update
  231.4 0.0 reduce-scatter.5.cloned.1.call-start
  231.5 32.8 %reduce-scatter.3.cloned.1.call-done = bf16[1,4,128,256]{3,2,1,0:T(8,128)(2,1)} async-done(((bf16[4,4,128,256]{3,2,1,0:T(8,128)(2,1)}), bf16[1,4,128,256]{3,2,1,0:T(8,128)(2,1)}) %reduce-scatter.3.cloned.1.call-update) | async-done | bytes 262160 | tf_op jit(solution)/shard_map/reduce_scatter | solution.py:81
  264.4 0.1 reshape_squeeze_reshape.3
  264.5 3.2 gather_fusion
  267.7 0.2 broadcast_select_fusion.1
  267.9 0.2 copy.20
  268.2 29.3 %reduce-scatter.5.cloned.1.call-done = bf16[1,128,256]{2,1,0:T(8,128)(2,1)} async-done(((bf16[4,128,256]{2,1,0:T(8,128)(2,1)}), bf16[1,128,256]{2,1,0:T(8,128)(2,1)}) %reduce-scatter.5.cloned.1.call-update) | async-done | bytes 65552 | tf_op jit(solution)/shard_map/reduce_scatter | solution.py:82
  297.4 1.0 select_reduce_fusion
  298.4 0.1 fusion.48
  298.5 3.3 fusion.91
  301.9 0.7 fusion.70
  302.6 2.7 fusion.3
  305.4 0.7 fusion.55
  306.1 0.7 fusion.58
  306.8 0.7 fusion.61
  307.6 3.2 fusion.64
  310.8 2.7 fusion.67
  313.5 9.7 %fusion.19 = (f32[1024]{0:T(1024)S(1)}, f32[1024]{0:T(1024)S(1)}, f32[1024]{0:T(1024)S(1)}, f32[1024]{0:T(1024)S(1)}, f32[1024]{0:T(1024)S(1)}, /*index=5*/f32[1...) fusion(f32[1024,1024]{1,0:T(8,128)} %get-tuple-element.60, ...), kind=kOutput, calls=%fused_computation.45 | convolution fusion | flops 295690240 | bytes 36278272 | tf_op jit(solution)/shard_map/eval_jaxpr/dot_general | solution.py:20
  323.2 13.7 %fusion.21 = (f32[1024]{0:T(1024)S(1)}, f32[1024]{0:T(1024)S(1)}, f32[1024]{0:T(1024)S(1)}, f32[1024]{0:T(1024)S(1)}, f32[1024]{0:T(1024)S(1)}, /*index=5*/f32[1...) fusion(f32[1024,1024]{1,0:T(8,128)S(1)} %fusion.70, ...), kind=kLoop, calls=%fused_computation.47 | loop fusion | flops 36692992 | bytes 44163072 | tf_op jit(solution)/shard_map/eval_jaxpr/reduce_sum | solution.py:30
  336.9 0.3 convolution_multiply_fusion
  337.3 2.6 fusion.43
  339.9 0.8 fusion.42
  340.7 0.7 copy-done.6
  341.4 0.1 copy-done.16
  341.5 0.8 fusion.41
  342.3 0.1 copy-done.5
  342.4 0.1 copy-done.14
  342.5 0.8 fusion.40
  343.3 0.6 copy-done.4
  343.9 0.1 copy-done.12
  344.0 0.8 fusion.39
  344.8 0.3 copy-done.3
  345.1 0.1 copy-done.10
  345.2 0.8 fusion.38
  346.0 0.5 copy-done.2
  346.5 0.8 fusion.37
  347.3 0.4 copy-done.8
  347.7 0.1 copy-done.21
  347.8 0.8 fusion.44
  348.5 0.8 convert_element_type.72
  (54 shorter events, 0.3 us)
Async XLA Ops:
  84.2 214.4 %all-to-all-start.2 = ((bf16[128,64,1,256]{3,1,2,0:T(8,128)(2,1)}), bf16[128,64,1,256]{3,1,2,0:T(8,128)(2,1)}, u32[]{:S(2)}, u32[]{:S(2)}) async-start(bf16[128,64,1,256]{3,1,2,0:T(8,128)(2,1)} %bitcast.226), calls=%async_computation.4 | async-start | bytes 8388608 | tf_op jit(solution)/shard_map/all_to_all | solution.py:71
  92.2 172.2 %copy-start.24 = (s32[1,2,64]{2,1,0:T(2,128)S(1)}, s32[1,2,64]{2,1,0:T(2,128)}, u32[]{:S(2)}) copy-start(s32[1,2,64]{2,1,0:T(2,128)} %param.11) | copy-start | bytes 1540
  92.2 172.2 %copy-start.22 = (bf16[128,1024]{1,0:T(8,128)(2,1)S(1)}, bf16[128,1024]{1,0:T(8,128)(2,1)}, u32[]{:S(2)}) copy-start(bf16[128,1024]{1,0:T(8,128)(2,1)} %param.8) | copy-start | bytes 786436
  92.2 93.9 %all-gather.4.cloned.1.call-start = ((), (), s32[]{:S(2)}) async-start(), calls=%async_computation.5 | async-start | bytes 1081344 | tf_op jit(solution)/shard_map/all_gather | solution.py:73
  92.9 134.6 %all-gather.6.cloned.1.call-start = ((), (), s32[]{:S(2)}) async-start(), calls=%async_computation.8 | async-start | bytes 2621440 | tf_op jit(solution)/shard_map/all_gather | solution.py:74
  93.7 170.6 %reduce-scatter.3.cloned.1.call-start = ((), (), s32[]{:S(2)}) async-start(), calls=%async_computation.6 | async-start | bytes 1310720 | tf_op jit(solution)/shard_map/reduce_scatter | solution.py:81
  231.4 66.0 %reduce-scatter.5.cloned.1.call-start = ((), (), s32[]{:S(2)}) async-start(), calls=%async_computation.7 | async-start | bytes 327680 | tf_op jit(solution)/shard_map/reduce_scatter | solution.py:82
  301.9 3.5 copy-start.17
  301.9 3.5 copy-start.19
  301.9 4.2 %copy-start.9 = (bf16[16,64,1,256]{3,1,2,0:T(8,128)(2,1)}, bf16[16,64,1,256]{3,1,2,0:T(8,128)(2,1)S(1)}, u32[]{:S(2)}) copy-start(bf16[16,64,1,256]{3,1,2,0:T(8,128)(2,1)S(1)} %get-tuple-element.50) | copy-start | bytes 1572868
  301.9 4.9 %copy-start.11 = (bf16[16,64,1,256]{3,1,2,0:T(8,128)(2,1)}, bf16[16,64,1,256]{3,1,2,0:T(8,128)(2,1)S(1)}, u32[]{:S(2)}) copy-start(bf16[16,64,1,256]{3,1,2,0:T(8,128)(2,1)S(1)} %get-tuple-element.51) | copy-start | bytes 1572868
  301.9 5.6 %copy-start.13 = (bf16[16,64,1,256]{3,1,2,0:T(8,128)(2,1)}, bf16[16,64,1,256]{3,1,2,0:T(8,128)(2,1)S(1)}, u32[]{:S(2)}) copy-start(bf16[16,64,1,256]{3,1,2,0:T(8,128)(2,1)S(1)} %get-tuple-element.52) | copy-start | bytes 1572868
  301.9 8.8 %copy-start.15 = (bf16[16,64,1,256]{3,1,2,0:T(8,128)(2,1)}, bf16[16,64,1,256]{3,1,2,0:T(8,128)(2,1)S(1)}, u32[]{:S(2)}) copy-start(bf16[16,64,1,256]{3,1,2,0:T(8,128)(2,1)S(1)} %get-tuple-element.47) | copy-start | bytes 1572868
  306.8 6.6 %copy-start = (f32[1024,1024]{1,0:T(8,128)}, f32[1024,1024]{1,0:T(8,128)S(1)}, u32[]{:S(2)}) copy-start(f32[1024,1024]{1,0:T(8,128)S(1)} %fusion.58) | copy-start | bytes 12582916
  307.5 5.9 %copy-start.1 = (f32[1024,1024]{1,0:T(8,128)}, f32[1024,1024]{1,0:T(8,128)S(1)}, u32[]{:S(2)}) copy-start(f32[1024,1024]{1,0:T(8,128)S(1)} %fusion.61) | copy-start | bytes 12582916
  307.6 5.9 %copy-start.20 = (bf16[16,64,1,256]{3,1,2,0:T(8,128)(2,1)S(1)}, bf16[16,64,1,256]{3,1,2,0:T(8,128)(2,1)}, u32[]{:S(2)}) copy-start(bf16[16,64,1,256]{3,1,2,0:T(8,128)(2,1)} %get-tuple-element.48) | copy-start | bytes 1572868
  323.1 13.7 %copy-start.23 = (bf16[1,128,256]{2,1,0:T(8,128)(2,1)S(1)}, bf16[1,128,256]{2,1,0:T(8,128)(2,1)}, u32[]{:S(2)}) copy-start(bf16[1,128,256]{2,1,0:T(8,128)(2,1)} %reduce-scatter.5.cloned.1.call-done) | copy-start | bytes 196612
  336.8 3.0 copy-start.7
  336.8 3.0 copy-start.18
  339.8 1.6 copy-start.6
  339.8 1.7 copy-start.16
  340.6 1.8 copy-start.5
  340.6 1.9 copy-start.14
  342.3 1.7 copy-start.4
  342.3 1.7 copy-start.12
  343.3 1.8 copy-start.3
  343.3 1.9 copy-start.10
  344.8 1.7 copy-start.2
  345.9 1.7 copy-start.8
  346.0 1.8 copy-start.21
Sparse Core Ops, SparseCore 0:
  95.2 90.8 all-gather.3
  188.2 39.3 all-gather.5
  231.5 32.7 reduce-scatter.2
  267.8 29.5 reduce-scatter.4

commit v12 on v10

--- a/solution.py
+++ b/solution.py
@@ -71,15 +71,9 @@
     fetched = lax.all_to_all(reply, POOL, split_axis=0, concat_axis=0, tiled=True)
 
     w_head = lax.all_gather(kv_weight, ("pz", "pc"), axis=1, tiled=True)
-    h_ring = lax.all_gather(hidden_rows, "px", axis=0, tiled=False)
-    part = jnp.einsum("xrd,dc->xrc", h_ring, w_head, preferred_element_type=jnp.float32)
-    ntp = lax.axis_size("tp")
-    head_slot = jnp.arange(ntp) == lax.axis_index("px")
-    spread = jnp.where(
-        head_slot[None, :, None, None], part.astype(jnp.bfloat16)[:, None], jnp.zeros((), jnp.bfloat16)
-    )
-    moved = lax.psum_scatter(spread, "px", scatter_dimension=0, tiled=True)
-    fresh = lax.psum_scatter(moved[0], "tp", scatter_dimension=0, tiled=True)[0]
+    w_all = lax.all_gather(w_head, "px", axis=1, tiled=True)
+    partial_kv = jnp.dot(hidden_rows, w_all, preferred_element_type=jnp.float32)
+    fresh = lax.psum_scatter(partial_kv.astype(jnp.bfloat16), "tp", scatter_dimension=1, tiled=True)
 
     count = hidden_rows.shape[0]
     group = QH // KVH

time: 338 us -> 325 us (0.962)
  waiting for transfers between devices: 197 us -> 183 us
    reduce_scatter x2 -> x1, waiting for transfers between devices: 61.8 us -> 26.4 us  [body(): lax.psum_scatter(partial_kv.astype(jnp.bfloat16), 'tp', scatter_dimension...]
    all_gather x1, waiting for transfers between devices: 40.7 us -> 63.2 us  [body(): w_all = lax.all_gather(w_head, 'px', axis=1, tiled=True)]
  transfers between devices with their start and end apart: 5 -> 4, of which waited for: 4 -> 3; matrix products, arithmetic and copies ran while one was open for 3% -> 3% of each run, Pallas kernels for 0% -> 0%
where the time goes in v12:
time: 325 us; the launch traced here: 324 us
  waiting for transfers between devices  183 us (56%)
  blocking collectives  64.2 us (20%)
  matrix products  29.5 us (9%)
  local copies, waits for them, and re-layouts  14.5 us (4%)
  between operations  13.9 us (4%)
  other arithmetic  10.5 us (3%)
  starting transfers between devices  8.1 us (2%)
    all_gather x1, waiting for transfers between devices, body(): w_head = lax.all_gather(kv_weight, ('pz', 'pc'), axis=1, tiled=True)  93.1 us
    all_gather x1, waiting for transfers between devices, body(): w_all = lax.all_gather(w_head, 'px', axis=1, tiled=True)  63.2 us
    all_to_all x1, blocking collectives, body(): step = lax.all_to_all(step, 'pz', split_axis=2, concat_axis=2, tiled=True)  49.9 us
    reduce_scatter x1, waiting for transfers between devices, body(): lax.psum_scatter(partial_kv.astype(jnp.bfloat16), 'tp', scatter_dimension...  26.4 us
    all_to_all x1, blocking collectives, body(): lax.all_to_all(step, ('px', 'pc'), split_axis=1, concat_axis=1, tiled=True)  14.3 us
    dot_general x1, matrix products, body(): jnp.dot(picks, table, preferred_element_type=jnp.float32)  9.18 us
    squeeze x8, local copies, waits for them, and re-layouts, body(): (top, total, numer), unused = lax.scan(visit, (top, total, numer), grouped)  8.64 us
    all_to_all x1, starting transfers between devices, body(): lax.all_to_all(reply, POOL, split_axis=0, concat_axis=0, tiled=True)  7.98 us
  transfers between devices with their start and end apart: 4, of which 3 were waited for; matrix products, arithmetic and copies ran while one was open for 3% of the time, Pallas kernels for 0%

profile of v12, /device:TPU:2, one launch (start us, length us, event | category | flops | bytes accessed | tf_op | source)
XLA Modules:
  0.0 324.5 jit_solution(12387347128276291437)
XLA Ops:
  7.2 0.7 fusion.32
  7.9 0.1 pad_maximum_fusion.1
  8.0 1.1 pad_maximum_fusion
  9.1 0.2 reshape.149
  9.3 0.4 copy.15
  9.7 49.9 %all_to_all.15 = bf16[9,4,16,2,256]{4,3,1,0,2:T(2,128)(2,1)S(1)} all-to-all(bf16[9,4,16,2,256]{4,3,1,0,2:T(2,128)(2,1)S(1)} %copy.15), channel_id=1, replica_groups=mesh['px'=4,'pz'=16,'pc'=2,'tp'=4] {'pz'}, dimensions={2} | all-to-all | bytes 1179648 | tf_op jit(solution)/shard_map/all_to_all | solution.py:54
  59.7 0.1 copy.22
  59.8 14.3 %all_to_all.16 = bf16[9,8,16,256]{3,2,0,1:T(8,128)(2,1)S(1)} all-to-all(bf16[9,8,16,256]{3,2,0,1:T(8,128)(2,1)S(1)} %bitcast.84), channel_id=1, replica_groups=mesh['px'=4,'pz'=16,'pc'=2,'tp'=4] {'px','pc'}, dimensions={1} | all-to-all | bytes 1179648 | tf_op jit(solution)/shard_map/all_to_all | solution.py:56
  74.1 0.6 copy.28
  74.6 0.2 reshape.152
  74.9 0.1 fusion.22
  75.0 0.1 eq.17
  75.1 9.2 %fusion.11 = bf16[8192,256]{1,0:T(8,128)(2,1)} fusion(s32[8192]{0:T(1024)S(1)} %eq.17, bf16[128,8,256]{2,0,1:T(8,128)(2,1)S(1)} %slice.39), kind=kOutput, calls=%fused_computation.19 | convolution fusion | flops 4305453056 | bytes 4751360 | tf_op jit(solution)/shard_map/dot_general | solution.py:68
  84.3 8.0 %all-to-all-start.2 = ((bf16[128,64,1,256]{3,1,2,0:T(8,128)(2,1)}), bf16[128,64,1,256]{3,1,2,0:T(8,128)(2,1)}, u32[]{:S(2)}, u32[]{:S(2)}) async-start(bf16[128,64,1,256]{3,1,2,0:T(8,128)(2,1)} %bitcast.83), calls=%async_computation.3 | async-start | bytes 8388608 | tf_op jit(solution)/shard_map/all_to_all | solution.py:71
  92.3 0.0 all-gather.3.cloned.1.call-start
  92.4 0.7 all-gather.3.cloned.1.call-update
  93.0 0.0 all-gather.5.cloned.1.call-start
  93.1 93.1 %all-gather.3.cloned.1.call-done = bf16[2048,256]{0,1:T(8,128)(2,1)} async-done(((bf16[2048,8]{0,1:T(8,128)(2,1)}), bf16[2048,256]{0,1:T(8,128)(2,1)}) %all-gather.3.cloned.1.call-update) | async-done | bytes 1048592 | tf_op jit(solution)/shard_map/all_gather | solution.py:73
  186.2 0.0 reduce-scatter.2.cloned.1.call-start
  186.3 63.2 %all-gather.5.cloned.1.call-done = bf16[2048,1024]{0,1:T(8,128)(2,1)} async-done(((bf16[2048,256]{0,1:T(8,128)(2,1)}), bf16[2048,1024]{0,1:T(8,128)(2,1)}) %all-gather.5.cloned.1.call-update) | async-done | bytes 4194320 | tf_op jit(solution)/shard_map/all_gather | solution.py:74
  249.4 4.4 %convolution_convert_fusion = bf16[128,1024]{1,0:T(8,128)(2,1)} fusion(bf16[128,2048]{1,0:T(8,128)(2,1)S(1)} %copy-done, bf16[2048,1024]{0,1:T(8,128)(2,1)} %all-gather.5.cloned.1.call-done), kind=kOutput, calls=%fused_computation.22 | convolution fusion | flops 537001984 | bytes 4980736 | tf_op jit(solution)/shard_map/dot_general | solution.py:75
  253.9 3.0 gather_fusion
  256.9 0.2 broadcast_select_fusion
  257.2 0.2 copy.21
  257.4 0.1 reshape_squeeze_reshape.3
  257.5 26.4 %reduce-scatter.2.cloned.1.call-done = bf16[128,256]{1,0:T(8,128)(2,1)} async-done(((bf16[128,1024]{1,0:T(8,128)(2,1)}), bf16[128,256]{1,0:T(8,128)(2,1)}) %reduce-scatter.2.cloned.1.call-update) | async-done | bytes 65552 | tf_op jit(solution)/shard_map/reduce_scatter | solution.py:76
  283.9 1.0 select_reduce_fusion
  284.9 0.1 fusion.16
  285.0 1.0 fusion.17
  286.1 30.8 %while.15 = (s32[]{:T(128)}, f32[1024]{0:T(1024)S(1)}, f32[1024]{0:T(1024)S(1)}, f32[1024,128]{1,0:T(8,128)S(1)}, bf16[8,1024,256]{2,1,0:T(8,128)(2,1)}, /*index...) while((s32[]{:T(128)}, f32[1024]{0:T(1024)S(1)}, f32[1024]{0:T(1024)S(1)}, ...), condition=%wide.region_6.7_spmd.clone, body=%wide.region_3.6_spmd.clone.sunk | while | flops 545523712 | bytes 15659105 | solution.py:106
  286.1 1.1 dynamic-slice_bitcast_fusion.2
  287.2 0.7 fusion.47
  288.0 1.0 fusion.48
  289.0 1.0 convolution_add_fusion.2
  290.0 1.1 dynamic-slice_bitcast_fusion.2
  291.1 0.8 fusion.47
  291.8 1.0 fusion.48
  292.8 1.0 convolution_add_fusion.2
  293.8 1.1 dynamic-slice_bitcast_fusion.2
  294.9 0.7 fusion.47
  295.7 1.0 fusion.48
  296.7 1.0 convolution_add_fusion.2
  297.7 1.1 dynamic-slice_bitcast_fusion.2
  298.8 0.8 fusion.47
  299.5 1.0 fusion.48
  300.5 1.0 convolution_add_fusion.2
  301.5 1.1 dynamic-slice_bitcast_fusion.2
  302.6 0.7 fusion.47
  303.4 1.0 fusion.48
  304.4 1.0 convolution_add_fusion.2
  305.4 1.1 dynamic-slice_bitcast_fusion.2
  306.5 0.8 fusion.47
  307.2 1.0 fusion.48
  308.2 1.0 convolution_add_fusion.2
  309.2 1.1 dynamic-slice_bitcast_fusion.2
  310.3 0.7 fusion.47
  311.1 1.0 fusion.48
  312.1 1.0 convolution_add_fusion.2
  313.1 1.1 dynamic-slice_bitcast_fusion.2
  314.2 0.8 fusion.47
  314.9 1.0 fusion.48
  315.9 1.0 convolution_add_fusion.2
  316.9 0.2 divide_convert_fusion
  317.2 0.8 convert_element_type.43
  (42 shorter events, 0.3 us)
Async XLA Ops:
  7.2 242.3 %copy-start = (bf16[128,2048]{1,0:T(8,128)(2,1)S(1)}, bf16[128,2048]{1,0:T(8,128)(2,1)}, u32[]{:S(2)}) copy-start(bf16[128,2048]{1,0:T(8,128)(2,1)} %param.8) | copy-start | bytes 1572868
  84.3 201.8 %all-to-all-start.2 = ((bf16[128,64,1,256]{3,1,2,0:T(8,128)(2,1)}), bf16[128,64,1,256]{3,1,2,0:T(8,128)(2,1)}, u32[]{:S(2)}, u32[]{:S(2)}) async-start(bf16[128,64,1,256]{3,1,2,0:T(8,128)(2,1)} %bitcast.83), calls=%async_computation.3 | async-start | bytes 8388608 | tf_op jit(solution)/shard_map/all_to_all | solution.py:71
  92.3 161.6 %copy-start.2 = (s32[1,2,64]{2,1,0:T(2,128)S(1)}, s32[1,2,64]{2,1,0:T(2,128)}, u32[]{:S(2)}) copy-start(s32[1,2,64]{2,1,0:T(2,128)} %param.13) | copy-start | bytes 1540
  92.3 165.1 %copy-start.1 = (bf16[128,1024]{1,0:T(8,128)(2,1)S(1)}, bf16[128,1024]{1,0:T(8,128)(2,1)}, u32[]{:S(2)}) copy-start(bf16[128,1024]{1,0:T(8,128)(2,1)} %param.10) | copy-start | bytes 786436
  92.3 93.9 %all-gather.3.cloned.1.call-start = ((), (), s32[]{:S(2)}) async-start(), calls=%async_computation.4 | async-start | bytes 1081344 | tf_op jit(solution)/shard_map/all_gather | solution.py:73
  93.0 156.4 %all-gather.5.cloned.1.call-start = ((), (), s32[]{:S(2)}) async-start(), calls=%async_computation.5 | async-start | bytes 5242880 | tf_op jit(solution)/shard_map/all_gather | solution.py:74
  186.2 97.7 %reduce-scatter.2.cloned.1.call-start = ((), (), s32[]{:S(2)}) async-start(), calls=%async_computation.6 | async-start | bytes 327680 | tf_op jit(solution)/shard_map/reduce_scatter | solution.py:76
Sparse Core Ops, SparseCore 0:
  95.3 90.8 all-gather.2
  188.3 61.1 all-gather.4
  254.0 29.8 reduce-scatter.1

commit v13 on v12

--- a/solution.py
+++ b/solution.py
@@ -50,11 +50,14 @@
     outgoing = jnp.concatenate([cache_table, id_block], axis=0)
     nx, nz, nc = (lax.axis_size(a) for a in POOL)
     rows_out = blocks_dev + 1
-    step = outgoing.reshape(rows_out, nx, nz, nc, width)
-    step = lax.all_to_all(step, "pz", split_axis=2, concat_axis=2, tiled=True)
-    step = step.transpose(0, 1, 3, 2, 4).reshape(rows_out, nx * nc, nz, width)
-    step = lax.all_to_all(step, ("px", "pc"), split_axis=1, concat_axis=1, tiled=True)
-    step = step.reshape(rows_out, nx, nc, nz, width).transpose(1, 3, 2, 0, 4)
+    lanes = 128
+    step = outgoing.reshape(rows_out, nx, nz, nc, width).transpose(2, 0, 1, 3, 4)
+    step = step.reshape(nz, -1, lanes)
+    step = lax.all_to_all(step, "pz", split_axis=0, concat_axis=0, tiled=True)
+    step = step.reshape(nz, rows_out, nx, nc, width).transpose(2, 3, 0, 1, 4)
+    step = step.reshape(nx * nc, -1, lanes)
+    step = lax.all_to_all(step, ("px", "pc"), split_axis=0, concat_axis=0, tiled=True)
+    step = step.reshape(nx, nc, nz, rows_out, width).transpose(0, 2, 1, 3, 4)
     by_token = step.reshape(npool, rows_out, width)
     table = by_token[:, :blocks_dev].reshape(npool * blocks_dev, width)
     id_rows = by_token[:, blocks_dev].astype(jnp.float32)

time: 325 us -> 327 us (level)
  the two profiles are of different devices: /device:TPU:2 before, /device:TPU:4 now
where the time goes in v13:
time: 327 us; the launch traced here: 326 us
  waiting for transfers between devices  183 us (56%)
  blocking collectives  63.1 us (19%)
  matrix products  29.5 us (9%)
  local copies, waits for them, and re-layouts  16 us (5%)
  between operations  14 us (4%)
  other arithmetic  10.5 us (3%)
  starting transfers between devices  9.58 us (3%)
    all_gather x1, waiting for transfers between devices, body(): w_head = lax.all_gather(kv_weight, ('pz', 'pc'), axis=1, tiled=True)  93.9 us
    all_gather x1, waiting for transfers between devices, body(): w_all = lax.all_gather(w_head, 'px', axis=1, tiled=True)  61.7 us
    all_to_all x1, blocking collectives, body(): step = lax.all_to_all(step, 'pz', split_axis=0, concat_axis=0, tiled=True)  49.9 us
    reduce_scatter x1, waiting for transfers between devices, body(): lax.psum_scatter(partial_kv.astype(jnp.bfloat16), 'tp', scatter_dimension...  26.7 us
    all_to_all x1, blocking collectives, body(): lax.all_to_all(step, ('px', 'pc'), split_axis=0, concat_axis=0, tiled=True)  13.2 us
    all_to_all x1, starting transfers between devices, body(): lax.all_to_all(reply, POOL, split_axis=0, concat_axis=0, tiled=True)  9.28 us
    dot_general x1, matrix products, body(): jnp.dot(picks, table, preferred_element_type=jnp.float32)  9.18 us
    squeeze x8, local copies, waits for them, and re-layouts, body(): (top, total, numer), unused = lax.scan(visit, (top, total, numer), grouped)  8.64 us
  transfers between devices with their start and end apart: 4, of which 3 were waited for; matrix products, arithmetic and copies ran while one was open for 3% of the time, Pallas kernels for 0%

profile of v13, /device:TPU:4, one launch (start us, length us, event | category | flops | bytes accessed | tf_op | source)
XLA Modules:
  0.0 326.1 jit_solution(6123139590422423552)
XLA Ops:
  7.2 0.7 fusion.32
  8.0 1.1 pad_maximum_fusion
  9.1 0.2 reshape.155
  9.3 0.4 copy.31
  9.7 0.4 reshape.156
  10.1 49.9 %all_to_all.15 = bf16[16,144,128]{2,1,0:T(8,128)(2,1)S(1)} all-to-all(bf16[16,144,128]{2,1,0:T(8,128)(2,1)S(1)} %reshape.156), channel_id=1, replica_groups=mesh['px'=4,'pz'=16,'pc'=2,'tp'=4] {'pz'}, dimensions={0} | all-to-all | bytes 1179648 | tf_op jit(solution)/shard_map/all_to_all | solution.py:56
  60.1 0.4 reshape.157
  60.4 0.2 copy.30
  60.6 0.3 reshape.158
  61.0 13.2 %all_to_all.16 = bf16[8,288,128]{2,1,0:T(8,128)(2,1)S(1)} all-to-all(bf16[8,288,128]{2,1,0:T(8,128)(2,1)S(1)} %reshape.158), channel_id=1, replica_groups=mesh['px'=4,'pz'=16,'pc'=2,'tp'=4] {'px','pc'}, dimensions={0} | all-to-all | bytes 1179648 | tf_op jit(solution)/shard_map/all_to_all | solution.py:59
  74.1 0.3 reshape.159
  74.4 0.6 copy.20
  75.1 0.2 reshape.160
  75.4 0.1 fusion.22
  75.6 9.2 %fusion.11 = bf16[8192,256]{1,0:T(8,128)(2,1)} fusion(s32[8192]{0:T(1024)S(1)} %eq.17, bf16[128,8,256]{2,0,1:T(8,128)(2,1)S(1)} %slice.39), kind=kOutput, calls=%fused_computation.19 | convolution fusion | flops 4305453056 | bytes 4751360 | tf_op jit(solution)/shard_map/dot_general | solution.py:71
  84.7 9.3 %all-to-all-start.2 = ((bf16[128,64,1,256]{3,1,2,0:T(8,128)(2,1)}), bf16[128,64,1,256]{3,1,2,0:T(8,128)(2,1)}, u32[]{:S(2)}, u32[]{:S(2)}) async-start(bf16[128,64,1,256]{3,1,2,0:T(8,128)(2,1)} %bitcast.83), calls=%async_computation.3 | async-start | bytes 8388608 | tf_op jit(solution)/shard_map/all_to_all | solution.py:74
  94.1 0.7 all-gather.3.cloned.1.call-update
  94.8 93.9 %all-gather.3.cloned.1.call-done = bf16[2048,256]{0,1:T(8,128)(2,1)} async-done(((bf16[2048,8]{0,1:T(8,128)(2,1)}), bf16[2048,256]{0,1:T(8,128)(2,1)}) %all-gather.3.cloned.1.call-update) | async-done | bytes 1048592 | tf_op jit(solution)/shard_map/all_gather | solution.py:76
  188.8 0.2 reduce-scatter.2.cloned.1.call-start
  189.0 61.7 %all-gather.5.cloned.1.call-done = bf16[2048,1024]{0,1:T(8,128)(2,1)} async-done(((bf16[2048,256]{0,1:T(8,128)(2,1)}), bf16[2048,1024]{0,1:T(8,128)(2,1)}) %all-gather.5.cloned.1.call-update) | async-done | bytes 4194320 | tf_op jit(solution)/shard_map/all_gather | solution.py:77
  250.7 4.4 %convolution_convert_fusion = bf16[128,1024]{1,0:T(8,128)(2,1)} fusion(bf16[128,2048]{1,0:T(8,128)(2,1)S(1)} %copy-done, bf16[2048,1024]{0,1:T(8,128)(2,1)} %all-gather.5.cloned.1.call-done), kind=kOutput, calls=%fused_computation.22 | convolution fusion | flops 537001984 | bytes 4980736 | tf_op jit(solution)/shard_map/dot_general | solution.py:78
  255.2 3.0 gather_fusion
  258.2 0.2 broadcast_select_fusion
  258.4 0.2 copy.23
  258.6 0.1 reshape_squeeze_reshape.3
  258.8 26.7 %reduce-scatter.2.cloned.1.call-done = bf16[128,256]{1,0:T(8,128)(2,1)} async-done(((bf16[128,1024]{1,0:T(8,128)(2,1)}), bf16[128,256]{1,0:T(8,128)(2,1)}) %reduce-scatter.2.cloned.1.call-update) | async-done | bytes 65552 | tf_op jit(solution)/shard_map/reduce_scatter | solution.py:79
  285.4 1.0 select_reduce_fusion
  286.4 0.1 fusion.16
  286.6 1.0 fusion.17
  287.6 30.9 %while.15 = (s32[]{:T(128)}, f32[1024]{0:T(1024)S(1)}, f32[1024]{0:T(1024)S(1)}, f32[1024,128]{1,0:T(8,128)S(1)}, bf16[8,1024,256]{2,1,0:T(8,128)(2,1)}, /*index...) while((s32[]{:T(128)}, f32[1024]{0:T(1024)S(1)}, f32[1024]{0:T(1024)S(1)}, ...), condition=%wide.region_6.7_spmd.clone, body=%wide.region_3.6_spmd.clone.sunk | while | flops 545523712 | bytes 15659105 | solution.py:109
  287.6 1.1 dynamic-slice_bitcast_fusion.2
  288.7 0.8 fusion.47
  289.5 1.0 fusion.48
  290.5 1.0 convolution_add_fusion.2
  291.5 1.1 dynamic-slice_bitcast_fusion.2
  292.6 0.8 fusion.47
  293.4 1.0 fusion.48
  294.4 1.0 convolution_add_fusion.2
  295.4 1.1 dynamic-slice_bitcast_fusion.2
  296.5 0.8 fusion.47
  297.2 1.0 fusion.48
  298.2 1.0 convolution_add_fusion.2
  299.2 1.1 dynamic-slice_bitcast_fusion.2
  300.3 0.8 fusion.47
  301.1 1.0 fusion.48
  302.1 1.0 convolution_add_fusion.2
  303.1 1.1 dynamic-slice_bitcast_fusion.2
  304.2 0.8 fusion.47
  305.0 1.0 fusion.48
  306.0 1.0 convolution_add_fusion.2
  307.0 1.1 dynamic-slice_bitcast_fusion.2
  308.0 0.8 fusion.47
  308.8 1.0 fusion.48
  309.8 1.0 convolution_add_fusion.2
  310.8 1.1 dynamic-slice_bitcast_fusion.2
  311.9 0.8 fusion.47
  312.7 1.0 fusion.48
  313.7 1.0 convolution_add_fusion.2
  314.7 1.1 dynamic-slice_bitcast_fusion.2
  315.8 0.8 fusion.47
  316.5 1.0 fusion.48
  317.5 1.0 convolution_add_fusion.2
  318.5 0.2 divide_convert_fusion
  318.7 0.8 convert_element_type.43
  (46 shorter events, 0.5 us)
Async XLA Ops:
  7.2 243.5 %copy-start = (bf16[128,2048]{1,0:T(8,128)(2,1)S(1)}, bf16[128,2048]{1,0:T(8,128)(2,1)}, u32[]{:S(2)}) copy-start(bf16[128,2048]{1,0:T(8,128)(2,1)} %param.8) | copy-start | bytes 1572868
  84.7 202.9 %all-to-all-start.2 = ((bf16[128,64,1,256]{3,1,2,0:T(8,128)(2,1)}), bf16[128,64,1,256]{3,1,2,0:T(8,128)(2,1)}, u32[]{:S(2)}, u32[]{:S(2)}) async-start(bf16[128,64,1,256]{3,1,2,0:T(8,128)(2,1)} %bitcast.83), calls=%async_computation.3 | async-start | bytes 8388608 | tf_op jit(solution)/shard_map/all_to_all | solution.py:74
  94.0 161.1 %copy-start.2 = (s32[1,2,64]{2,1,0:T(2,128)S(1)}, s32[1,2,64]{2,1,0:T(2,128)}, u32[]{:S(2)}) copy-start(s32[1,2,64]{2,1,0:T(2,128)} %param.13) | copy-start | bytes 1540
  94.0 164.6 %copy-start.1 = (bf16[128,1024]{1,0:T(8,128)(2,1)S(1)}, bf16[128,1024]{1,0:T(8,128)(2,1)}, u32[]{:S(2)}) copy-start(bf16[128,1024]{1,0:T(8,128)(2,1)} %param.10) | copy-start | bytes 786436
  94.0 94.7 %all-gather.3.cloned.1.call-start = ((), (), s32[]{:S(2)}) async-start(), calls=%async_computation.4 | async-start | bytes 1081344 | tf_op jit(solution)/shard_map/all_gather | solution.py:76
  94.8 155.9 %all-gather.5.cloned.1.call-start = ((), (), s32[]{:S(2)}) async-start(), calls=%async_computation.5 | async-start | bytes 5242880 | tf_op jit(solution)/shard_map/all_gather | solution.py:77
  188.8 96.7 %reduce-scatter.2.cloned.1.call-start = ((), (), s32[]{:S(2)}) async-start(), calls=%async_computation.6 | async-start | bytes 327680 | tf_op jit(solution)/shard_map/reduce_scatter | solution.py:79
Sparse Core Ops, SparseCore 0:
  97.0 91.6 all-gather.2
  190.8 59.8 all-gather.4
  255.3 30.1 reduce-scatter.1

commit v14 on v12

--- a/solution.py
+++ b/solution.py
@@ -50,10 +50,10 @@
     outgoing = jnp.concatenate([cache_table, id_block], axis=0)
     nx, nz, nc = (lax.axis_size(a) for a in POOL)
     rows_out = blocks_dev + 1
-    step = outgoing.reshape(rows_out, nx, nz, nc, width)
+    step = outgoing.reshape(rows_out, nx, nz, nc, width).transpose(0, 1, 3, 2, 4)
+    step = step.reshape(rows_out, nx * nc, nz, width)
+    step = lax.all_to_all(step, ("px", "pc"), split_axis=1, concat_axis=1, tiled=True)
     step = lax.all_to_all(step, "pz", split_axis=2, concat_axis=2, tiled=True)
-    step = step.transpose(0, 1, 3, 2, 4).reshape(rows_out, nx * nc, nz, width)
-    step = lax.all_to_all(step, ("px", "pc"), split_axis=1, concat_axis=1, tiled=True)
     step = step.reshape(rows_out, nx, nc, nz, width).transpose(1, 3, 2, 0, 4)
     by_token = step.reshape(npool, rows_out, width)
     table = by_token[:, :blocks_dev].reshape(npool * blocks_dev, width)

time: 325 us -> 325 us (level)
    all_to_all x1, blocking collectives: 49.9 us -> 46.2 us  [body(): step = lax.all_to_all(step, 'pz', split_axis=2, concat_axis=2, tiled=True)]
    all_to_all x1, blocking collectives: 14.3 us -> 17.9 us  [body(): lax.all_to_all(step, ('px', 'pc'), split_axis=1, concat_axis=1, tiled=True)]
where the time goes in v14:
time: 325 us; the launch traced here: 324 us
  waiting for transfers between devices  183 us (56%)
  blocking collectives  64.1 us (20%)
  matrix products  29.5 us (9%)
  local copies, waits for them, and re-layouts  14.5 us (4%)
  between operations  14 us (4%)
  other arithmetic  10.5 us (3%)
  starting transfers between devices  8.1 us (2%)
    all_gather x1, waiting for transfers between devices, body(): w_head = lax.all_gather(kv_weight, ('pz', 'pc'), axis=1, tiled=True)  93.1 us
    all_gather x1, waiting for transfers between devices, body(): w_all = lax.all_gather(w_head, 'px', axis=1, tiled=True)  63.2 us
    all_to_all x1, blocking collectives, body(): step = lax.all_to_all(step, 'pz', split_axis=2, concat_axis=2, tiled=True)  46.2 us
    reduce_scatter x1, waiting for transfers between devices, body(): lax.psum_scatter(partial_kv.astype(jnp.bfloat16), 'tp', scatter_dimension...  26.4 us
    all_to_all x1, blocking collectives, body(): lax.all_to_all(step, ('px', 'pc'), split_axis=1, concat_axis=1, tiled=True)  17.9 us
    dot_general x1, matrix products, body(): jnp.dot(picks, table, preferred_element_type=jnp.float32)  9.18 us
    squeeze x8, local copies, waits for them, and re-layouts, body(): (top, total, numer), unused = lax.scan(visit, (top, total, numer), grouped)  8.64 us
    all_to_all x1, starting transfers between devices, body(): lax.all_to_all(reply, POOL, split_axis=0, concat_axis=0, tiled=True)  7.98 us
  transfers between devices with their start and end apart: 4, of which 3 were waited for; matrix products, arithmetic and copies ran while one was open for 3% of the time, Pallas kernels for 0%

profile of v14, /device:TPU:2, one launch (start us, length us, event | category | flops | bytes accessed | tf_op | source)
XLA Modules:
  0.0 324.4 jit_solution(2684077313897743125)
XLA Ops:
  7.2 0.7 fusion.32
  7.9 0.1 pad_maximum_fusion.1
  8.0 1.1 pad_maximum_fusion
  9.1 0.2 reshape.149
  9.3 0.1 copy.22
  9.4 17.9 %all_to_all.15 = bf16[9,8,16,256]{3,2,0,1:T(8,128)(2,1)S(1)} all-to-all(bf16[9,8,16,256]{3,2,0,1:T(8,128)(2,1)S(1)} %bitcast.88), channel_id=1, replica_groups=mesh['px'=4,'pz'=16,'pc'=2,'tp'=4] {'px','pc'}, dimensions={1} | all-to-all | bytes 1179648 | tf_op jit(solution)/shard_map/all_to_all | solution.py:55
  27.3 0.2 copy.17
  27.5 46.2 %all_to_all.16 = bf16[9,8,16,256]{3,1,0,2:T(8,128)(2,1)S(1)} all-to-all(bf16[9,8,16,256]{3,1,0,2:T(8,128)(2,1)S(1)} %copy.17), channel_id=1, replica_groups=mesh['px'=4,'pz'=16,'pc'=2,'tp'=4] {'pz'}, dimensions={2} | all-to-all | bytes 1179648 | tf_op jit(solution)/shard_map/all_to_all | solution.py:56
  73.7 0.2 reshape.151
  73.9 0.6 copy.28
  74.5 0.2 reshape.152
  74.8 0.1 fusion.22
  74.9 0.1 eq.17
  75.0 9.2 %fusion.11 = bf16[8192,256]{1,0:T(8,128)(2,1)} fusion(s32[8192]{0:T(1024)S(1)} %eq.17, bf16[128,8,256]{2,0,1:T(8,128)(2,1)S(1)} %slice.39), kind=kOutput, calls=%fused_computation.19 | convolution fusion | flops 4305453056 | bytes 4751360 | tf_op jit(solution)/shard_map/dot_general | solution.py:68
  84.2 8.0 %all-to-all-start.2 = ((bf16[128,64,1,256]{3,1,2,0:T(8,128)(2,1)}), bf16[128,64,1,256]{3,1,2,0:T(8,128)(2,1)}, u32[]{:S(2)}, u32[]{:S(2)}) async-start(bf16[128,64,1,256]{3,1,2,0:T(8,128)(2,1)} %bitcast.86), calls=%async_computation.3 | async-start | bytes 8388608 | tf_op jit(solution)/shard_map/all_to_all | solution.py:71
  92.2 0.0 all-gather.3.cloned.1.call-start
  92.2 0.7 all-gather.3.cloned.1.call-update
  93.0 93.1 %all-gather.3.cloned.1.call-done = bf16[2048,256]{0,1:T(8,128)(2,1)} async-done(((bf16[2048,8]{0,1:T(8,128)(2,1)}), bf16[2048,256]{0,1:T(8,128)(2,1)}) %all-gather.3.cloned.1.call-update) | async-done | bytes 1048592 | tf_op jit(solution)/shard_map/all_gather | solution.py:73
  186.1 0.0 reduce-scatter.2.cloned.1.call-start
  186.2 63.2 %all-gather.5.cloned.1.call-done = bf16[2048,1024]{0,1:T(8,128)(2,1)} async-done(((bf16[2048,256]{0,1:T(8,128)(2,1)}), bf16[2048,1024]{0,1:T(8,128)(2,1)}) %all-gather.5.cloned.1.call-update) | async-done | bytes 4194320 | tf_op jit(solution)/shard_map/all_gather | solution.py:74
  249.3 4.4 %convolution_convert_fusion = bf16[128,1024]{1,0:T(8,128)(2,1)} fusion(bf16[128,2048]{1,0:T(8,128)(2,1)S(1)} %copy-done, bf16[2048,1024]{0,1:T(8,128)(2,1)} %all-gather.5.cloned.1.call-done), kind=kOutput, calls=%fused_computation.22 | convolution fusion | flops 537001984 | bytes 4980736 | tf_op jit(solution)/shard_map/dot_general | solution.py:75
  253.8 3.0 gather_fusion
  256.8 0.2 broadcast_select_fusion
  257.0 0.2 copy.21
  257.3 0.1 reshape_squeeze_reshape.3
  257.4 26.4 %reduce-scatter.2.cloned.1.call-done = bf16[128,256]{1,0:T(8,128)(2,1)} async-done(((bf16[128,1024]{1,0:T(8,128)(2,1)}), bf16[128,256]{1,0:T(8,128)(2,1)}) %reduce-scatter.2.cloned.1.call-update) | async-done | bytes 65552 | tf_op jit(solution)/shard_map/reduce_scatter | solution.py:76
  283.8 1.0 select_reduce_fusion
  284.8 0.1 fusion.16
  284.9 1.0 fusion.17
  286.0 30.8 %while.15 = (s32[]{:T(128)}, f32[1024]{0:T(1024)S(1)}, f32[1024]{0:T(1024)S(1)}, f32[1024,128]{1,0:T(8,128)S(1)}, bf16[8,1024,256]{2,1,0:T(8,128)(2,1)}, /*index...) while((s32[]{:T(128)}, f32[1024]{0:T(1024)S(1)}, f32[1024]{0:T(1024)S(1)}, ...), condition=%wide.region_6.7_spmd.clone, body=%wide.region_3.6_spmd.clone.sunk | while | flops 545523712 | bytes 15659105 | solution.py:106
  286.0 1.1 dynamic-slice_bitcast_fusion.2
  287.1 0.7 fusion.47
  287.9 1.0 fusion.48
  288.9 1.0 convolution_add_fusion.2
  289.9 1.1 dynamic-slice_bitcast_fusion.2
  290.9 0.8 fusion.47
  291.7 1.0 fusion.48
  292.7 1.0 convolution_add_fusion.2
  293.7 1.1 dynamic-slice_bitcast_fusion.2
  294.8 0.7 fusion.47
  295.6 1.0 fusion.48
  296.6 1.0 convolution_add_fusion.2
  297.6 1.1 dynamic-slice_bitcast_fusion.2
  298.6 0.8 fusion.47
  299.4 1.0 fusion.48
  300.4 1.0 convolution_add_fusion.2
  301.4 1.1 dynamic-slice_bitcast_fusion.2
  302.5 0.7 fusion.47
  303.3 1.0 fusion.48
  304.3 1.0 convolution_add_fusion.2
  305.3 1.1 dynamic-slice_bitcast_fusion.2
  306.3 0.8 fusion.47
  307.1 1.0 fusion.48
  308.1 1.0 convolution_add_fusion.2
  309.1 1.1 dynamic-slice_bitcast_fusion.2
  310.2 0.7 fusion.47
  311.0 1.0 fusion.48
  312.0 1.0 convolution_add_fusion.2
  313.0 1.1 dynamic-slice_bitcast_fusion.2
  314.1 0.8 fusion.47
  314.8 1.0 fusion.48
  315.8 1.0 convolution_add_fusion.2
  316.8 0.2 divide_convert_fusion
  317.0 0.8 convert_element_type.43
  (43 shorter events, 0.3 us)
Async XLA Ops:
  7.2 242.2 %copy-start = (bf16[128,2048]{1,0:T(8,128)(2,1)S(1)}, bf16[128,2048]{1,0:T(8,128)(2,1)}, u32[]{:S(2)}) copy-start(bf16[128,2048]{1,0:T(8,128)(2,1)} %param.8) | copy-start | bytes 1572868
  84.2 201.8 %all-to-all-start.2 = ((bf16[128,64,1,256]{3,1,2,0:T(8,128)(2,1)}), bf16[128,64,1,256]{3,1,2,0:T(8,128)(2,1)}, u32[]{:S(2)}, u32[]{:S(2)}) async-start(bf16[128,64,1,256]{3,1,2,0:T(8,128)(2,1)} %bitcast.86), calls=%async_computation.3 | async-start | bytes 8388608 | tf_op jit(solution)/shard_map/all_to_all | solution.py:71
  92.2 161.6 %copy-start.2 = (s32[1,2,64]{2,1,0:T(2,128)S(1)}, s32[1,2,64]{2,1,0:T(2,128)}, u32[]{:S(2)}) copy-start(s32[1,2,64]{2,1,0:T(2,128)} %param.13) | copy-start | bytes 1540
  92.2 165.1 %copy-start.1 = (bf16[128,1024]{1,0:T(8,128)(2,1)S(1)}, bf16[128,1024]{1,0:T(8,128)(2,1)}, u32[]{:S(2)}) copy-start(bf16[128,1024]{1,0:T(8,128)(2,1)} %param.10) | copy-start | bytes 786436
  92.2 93.9 %all-gather.3.cloned.1.call-start = ((), (), s32[]{:S(2)}) async-start(), calls=%async_computation.4 | async-start | bytes 1081344 | tf_op jit(solution)/shard_map/all_gather | solution.py:73
  92.9 156.4 %all-gather.5.cloned.1.call-start = ((), (), s32[]{:S(2)}) async-start(), calls=%async_computation.5 | async-start | bytes 5242880 | tf_op jit(solution)/shard_map/all_gather | solution.py:74
  186.1 97.7 %reduce-scatter.2.cloned.1.call-start = ((), (), s32[]{:S(2)}) async-start(), calls=%async_computation.6 | async-start | bytes 327680 | tf_op jit(solution)/shard_map/reduce_scatter | solution.py:76
Sparse Core Ops, SparseCore 0:
  95.1 90.8 all-gather.2
  188.1 61.1 all-gather.4
  253.9 29.8 reduce-scatter.1

commit v15 on v14

--- a/solution.py
+++ b/solution.py
@@ -12,7 +12,8 @@
 KVH = 4
 BLK = 128
 RBLK = 64
-POOL = ("px", "pz", "pc")
+POOL = ("px", "pzh", "pzl", "pc")
+Z_AXES = ("pzh", "pzl")
 ID_SPLIT = 32
 
 
@@ -48,13 +49,14 @@
     )
     id_block = jnp.broadcast_to(id_row[None, None, :], (1, blk, width))
     outgoing = jnp.concatenate([cache_table, id_block], axis=0)
-    nx, nz, nc = (lax.axis_size(a) for a in POOL)
+    nx, nzh, nzl, nc = (lax.axis_size(a) for a in POOL)
     rows_out = blocks_dev + 1
-    step = outgoing.reshape(rows_out, nx, nz, nc, width).transpose(0, 1, 3, 2, 4)
-    step = step.reshape(rows_out, nx * nc, nz, width)
+    step = outgoing.reshape(rows_out, nx, nzh, nzl, nc, width).transpose(0, 1, 4, 2, 3, 5)
+    step = step.reshape(rows_out, nx * nc, nzh, nzl, width)
     step = lax.all_to_all(step, ("px", "pc"), split_axis=1, concat_axis=1, tiled=True)
-    step = lax.all_to_all(step, "pz", split_axis=2, concat_axis=2, tiled=True)
-    step = step.reshape(rows_out, nx, nc, nz, width).transpose(1, 3, 2, 0, 4)
+    step = lax.all_to_all(step, "pzl", split_axis=3, concat_axis=3, tiled=True)
+    step = lax.all_to_all(step, "pzh", split_axis=2, concat_axis=2, tiled=True)
+    step = step.reshape(rows_out, nx, nc, nzh, nzl, width).transpose(1, 3, 4, 2, 0, 5)
     by_token = step.reshape(npool, rows_out, width)
     table = by_token[:, :blocks_dev].reshape(npool * blocks_dev, width)
     id_rows = by_token[:, blocks_dev].astype(jnp.float32)
@@ -70,7 +72,7 @@
     reply, hidden_rows, kv_weight = lax.optimization_barrier((reply, hidden_rows, kv_weight))
     fetched = lax.all_to_all(reply, POOL, split_axis=0, concat_axis=0, tiled=True)
 
-    w_head = lax.all_gather(kv_weight, ("pz", "pc"), axis=1, tiled=True)
+    w_head = lax.all_gather(kv_weight, Z_AXES + ("pc",), axis=1, tiled=True)
     w_all = lax.all_gather(w_head, "px", axis=1, tiled=True)
     partial_kv = jnp.dot(hidden_rows, w_all, preferred_element_type=jnp.float32)
     fresh = lax.psum_scatter(partial_kv.astype(jnp.bfloat16), "tp", scatter_dimension=1, tiled=True)
@@ -113,9 +115,11 @@
     npool = mesh.shape["pool"]
     ntp = mesh.shape["tp"]
     nx = 4 if npool % 8 == 0 else 1
+    nz = npool // (2 * nx)
+    nzh = 4 if nz % 4 == 0 else 1
     fine = Mesh(
-        np.asarray(mesh.devices).reshape(nx, npool // (2 * nx), 2, ntp),
-        ("px", "pz", "pc", "tp"),
+        np.asarray(mesh.devices).reshape(nx, nzh, nz // nzh, 2, ntp),
+        ("px", "pzh", "pzl", "pc", "tp"),
     )
     placed = (
         P(POOL, "tp"),

time: 325 us -> 343 us (1.055)
  blocking collectives: 64.1 us -> 81.7 us
    all_to_all x1 -> x2, blocking collectives: 46.2 us -> 63.8 us  [the longest x1 45.3 us: body(): step = lax.all_to_all(step, 'pzh', split_axis=2, concat_axis=2, tiled=True)]
where the time goes in v15:
time: 343 us
  waiting for transfers between devices  183 us (53%)
  blocking collectives  81.7 us (24%)
  matrix products  29.5 us (9%)
  local copies, waits for them, and re-layouts  15 us (4%)
  between operations  14 us (4%)
  other arithmetic  10.5 us (3%)
  starting transfers between devices  8.1 us (2%)
    all_gather x1, waiting for transfers between devices, body(): w_head = lax.all_gather(kv_weight, Z_AXES + ('pc',), axis=1, tiled=True)  91.1 us
    all_gather x1, waiting for transfers between devices, body(): w_all = lax.all_gather(w_head, 'px', axis=1, tiled=True)  65.2 us
    all_to_all x1, blocking collectives, body(): step = lax.all_to_all(step, 'pzh', split_axis=2, concat_axis=2, tiled=True)  45.3 us
    reduce_scatter x1, waiting for transfers between devices, body(): lax.psum_scatter(partial_kv.astype(jnp.bfloat16), 'tp', scatter_dimension...  26.4 us
    all_to_all x1, blocking collectives, body(): step = lax.all_to_all(step, 'pzl', split_axis=3, concat_axis=3, tiled=True)  18.5 us
    all_to_all x1, blocking collectives, body(): lax.all_to_all(step, ('px', 'pc'), split_axis=1, concat_axis=1, tiled=True)  17.9 us
    dot_general x1, matrix products, body(): jnp.dot(picks, table, preferred_element_type=jnp.float32)  9.19 us
    squeeze x8, local copies, waits for them, and re-layouts, body(): (top, total, numer), unused = lax.scan(visit, (top, total, numer), grouped)  8.64 us
  transfers between devices with their start and end apart: 4, of which 3 were waited for; matrix products, arithmetic and copies ran while one was open for 3% of the time, Pallas kernels for 0%

profile of v15, /device:TPU:2, one launch (start us, length us, event | category | flops | bytes accessed | tf_op | source)
XLA Modules:
  0.0 342.5 jit_solution(8103692505925425952)
XLA Ops:
  7.2 0.7 fusion.32
  7.9 0.1 pad_maximum_fusion.1
  8.0 1.1 pad_maximum_fusion
  9.1 0.2 reshape.149
  9.3 0.3 copy.24
  9.6 17.9 %all_to_all.20 = bf16[9,8,4,4,256]{4,3,2,0,1:T(4,128)(2,1)S(1)} all-to-all(bf16[9,8,4,4,256]{4,3,2,0,1:T(4,128)(2,1)S(1)} %bitcast.84), channel_id=1, replica_groups=mesh['px'=4,'pzh'=4,'pzl'=4,'pc'=2,'tp'=4] {'px','pc'}, dimensions={1} | all-to-all | bytes 1179648 | tf_op jit(solution)/shard_map/all_to_all | solution.py:56
  27.5 0.3 copy.18
  27.8 18.5 %all_to_all.21 = bf16[9,8,4,4,256]{4,2,1,0,3:T(4,128)(2,1)S(1)} all-to-all(bf16[9,8,4,4,256]{4,2,1,0,3:T(4,128)(2,1)S(1)} %copy.18), channel_id=1, replica_groups=mesh['px'=4,'pzh'=4,'pzl'=4,'pc'=2,'tp'=4] {'pzl'}, dimensions={3} | all-to-all | bytes 1179648 | tf_op jit(solution)/shard_map/all_to_all | solution.py:57
  46.3 0.5 copy.19
  46.8 45.3 %all_to_all.22 = bf16[9,8,4,4,256]{4,3,1,0,2:T(4,128)(2,1)S(1)} all-to-all(bf16[9,8,4,4,256]{4,3,1,0,2:T(4,128)(2,1)S(1)} %copy.19), channel_id=1, replica_groups=mesh['px'=4,'pzh'=4,'pzl'=4,'pc'=2,'tp'=4] {'pzh'}, dimensions={2} | all-to-all | bytes 1179648 | tf_op jit(solution)/shard_map/all_to_all | solution.py:58
  92.1 0.6 copy.30
  92.7 0.2 reshape.152
  93.0 0.1 fusion.22
  93.1 0.1 eq.17
  93.1 9.2 %fusion.11 = bf16[8192,256]{1,0:T(8,128)(2,1)} fusion(s32[8192]{0:T(1024)S(1)} %eq.17, bf16[128,8,256]{2,0,1:T(8,128)(2,1)S(1)} %slice.39), kind=kOutput, calls=%fused_computation.19 | convolution fusion | flops 4305453056 | bytes 4751360 | tf_op jit(solution)/shard_map/dot_general | solution.py:70
  102.3 8.0 %all-to-all-start.3 = ((bf16[128,64,1,256]{3,1,2,0:T(8,128)(2,1)}), bf16[128,64,1,256]{3,1,2,0:T(8,128)(2,1)}, u32[]{:S(2)}, u32[]{:S(2)}) async-start(bf16[128,64,1,256]{3,1,2,0:T(8,128)(2,1)} %bitcast.83), calls=%async_computation.4 | async-start | bytes 8388608 | tf_op jit(solution)/shard_map/all_to_all | solution.py:73
  110.3 0.0 all-gather.3.cloned.1.call-start
  110.4 0.7 all-gather.3.cloned.1.call-update
  111.1 91.1 %all-gather.3.cloned.1.call-done = bf16[2048,256]{0,1:T(8,128)(2,1)} async-done(((bf16[2048,8]{0,1:T(8,128)(2,1)}), bf16[2048,256]{0,1:T(8,128)(2,1)}) %all-gather.3.cloned.1.call-update) | async-done | bytes 1048592 | tf_op jit(solution)/shard_map/all_gather | solution.py:75
  202.3 65.2 %all-gather.5.cloned.1.call-done = bf16[2048,1024]{0,1:T(8,128)(2,1)} async-done(((bf16[2048,256]{0,1:T(8,128)(2,1)}), bf16[2048,1024]{0,1:T(8,128)(2,1)}) %all-gather.5.cloned.1.call-update) | async-done | bytes 4194320 | tf_op jit(solution)/shard_map/all_gather | solution.py:76
  267.5 4.4 %convolution_convert_fusion = bf16[128,1024]{1,0:T(8,128)(2,1)} fusion(bf16[128,2048]{1,0:T(8,128)(2,1)S(1)} %copy-done, bf16[2048,1024]{0,1:T(8,128)(2,1)} %all-gather.5.cloned.1.call-done), kind=kOutput, calls=%fused_computation.22 | convolution fusion | flops 537001984 | bytes 4980736 | tf_op jit(solution)/shard_map/dot_general | solution.py:77
  271.9 3.0 gather_fusion
  275.0 0.2 broadcast_select_fusion
  275.2 0.2 copy.23
  275.4 0.1 reshape_squeeze_reshape.3
  275.5 26.4 %reduce-scatter.2.cloned.1.call-done = bf16[128,256]{1,0:T(8,128)(2,1)} async-done(((bf16[128,1024]{1,0:T(8,128)(2,1)}), bf16[128,256]{1,0:T(8,128)(2,1)}) %reduce-scatter.2.cloned.1.call-update) | async-done | bytes 65552 | tf_op jit(solution)/shard_map/reduce_scatter | solution.py:78
  301.9 1.0 select_reduce_fusion
  303.0 0.1 fusion.16
  303.1 1.0 fusion.17
  304.1 30.8 %while.15 = (s32[]{:T(128)}, f32[1024]{0:T(1024)S(1)}, f32[1024]{0:T(1024)S(1)}, f32[1024,128]{1,0:T(8,128)S(1)}, bf16[8,1024,256]{2,1,0:T(8,128)(2,1)}, /*index...) while((s32[]{:T(128)}, f32[1024]{0:T(1024)S(1)}, f32[1024]{0:T(1024)S(1)}, ...), condition=%wide.region_6.7_spmd.clone, body=%wide.region_3.6_spmd.clone.sunk | while | flops 545523712 | bytes 15659105 | solution.py:108
  304.2 1.1 dynamic-slice_bitcast_fusion.2
  305.2 0.7 fusion.47
  306.0 1.0 fusion.48
  307.0 1.0 convolution_add_fusion.2
  308.0 1.1 dynamic-slice_bitcast_fusion.2
  309.1 0.8 fusion.47
  309.9 1.0 fusion.48
  310.9 1.0 convolution_add_fusion.2
  311.9 1.1 dynamic-slice_bitcast_fusion.2
  312.9 0.7 fusion.47
  313.7 1.0 fusion.48
  314.7 1.0 convolution_add_fusion.2
  315.7 1.1 dynamic-slice_bitcast_fusion.2
  316.8 0.8 fusion.47
  317.6 1.0 fusion.48
  318.6 1.0 convolution_add_fusion.2
  319.6 1.1 dynamic-slice_bitcast_fusion.2
  320.6 0.7 fusion.47
  321.4 1.0 fusion.48
  322.4 1.0 convolution_add_fusion.2
  323.4 1.1 dynamic-slice_bitcast_fusion.2
  324.5 0.8 fusion.47
  325.3 1.0 fusion.48
  326.3 1.0 convolution_add_fusion.2
  327.3 1.1 dynamic-slice_bitcast_fusion.2
  328.4 0.7 fusion.47
  329.1 1.0 fusion.48
  330.1 1.0 convolution_add_fusion.2
  331.1 1.1 dynamic-slice_bitcast_fusion.2
  332.2 0.8 fusion.47
  333.0 1.0 fusion.48
  334.0 1.0 convolution_add_fusion.2
  335.0 0.2 divide_convert_fusion
  335.2 0.8 convert_element_type.43
  (44 shorter events, 0.4 us)
Async XLA Ops:
  7.2 260.3 %copy-start = (bf16[128,2048]{1,0:T(8,128)(2,1)S(1)}, bf16[128,2048]{1,0:T(8,128)(2,1)}, u32[]{:S(2)}) copy-start(bf16[128,2048]{1,0:T(8,128)(2,1)} %param.8) | copy-start | bytes 1572868
  102.3 201.8 %all-to-all-start.3 = ((bf16[128,64,1,256]{3,1,2,0:T(8,128)(2,1)}), bf16[128,64,1,256]{3,1,2,0:T(8,128)(2,1)}, u32[]{:S(2)}, u32[]{:S(2)}) async-start(bf16[128,64,1,256]{3,1,2,0:T(8,128)(2,1)} %bitcast.83), calls=%async_computation.4 | async-start | bytes 8388608 | tf_op jit(solution)/shard_map/all_to_all | solution.py:73
  110.3 161.6 %copy-start.2 = (s32[1,2,64]{2,1,0:T(2,128)S(1)}, s32[1,2,64]{2,1,0:T(2,128)}, u32[]{:S(2)}) copy-start(s32[1,2,64]{2,1,0:T(2,128)} %param.13) | copy-start | bytes 1540
  110.3 165.1 %copy-start.1 = (bf16[128,1024]{1,0:T(8,128)(2,1)S(1)}, bf16[128,1024]{1,0:T(8,128)(2,1)}, u32[]{:S(2)}) copy-start(bf16[128,1024]{1,0:T(8,128)(2,1)} %param.10) | copy-start | bytes 786436
  110.3 91.9 %all-gather.3.cloned.1.call-start = ((), (), s32[]{:S(2)}) async-start(), calls=%async_computation.5 | async-start | bytes 1081344 | tf_op jit(solution)/shard_map/all_gather | solution.py:75
  111.1 156.4 %all-gather.5.cloned.1.call-start = ((), (), s32[]{:S(2)}) async-start(), calls=%async_computation.6 | async-start | bytes 5242880 | tf_op jit(solution)/shard_map/all_gather | solution.py:76
  202.2 99.7 %reduce-scatter.2.cloned.1.call-start = ((), (), s32[]{:S(2)}) async-start(), calls=%async_computation.7 | async-start | bytes 327680 | tf_op jit(solution)/shard_map/reduce_scatter | solution.py:78
Sparse Core Ops, SparseCore 0:
  113.3 88.8 all-gather.2
  204.3 63.1 all-gather.4
  272.0 29.8 reduce-scatter.1

commit v16 on v14

--- a/solution.py
+++ b/solution.py
@@ -65,7 +65,7 @@
         wanted_all.reshape(-1)[:, None]
         == jnp.arange(npool * blocks_dev, dtype=jnp.int32)[None, :]
     ).astype(jnp.bfloat16)
-    reply = jnp.dot(picks, table, preferred_element_type=jnp.float32).astype(jnp.bfloat16)
+    reply = jnp.dot(picks, table, preferred_element_type=jnp.bfloat16)
     reply = reply.reshape(npool, fetch_count, 1, width)
     reply, hidden_rows, kv_weight = lax.optimization_barrier((reply, hidden_rows, kv_weight))
     fetched = lax.all_to_all(reply, POOL, split_axis=0, concat_axis=0, tiled=True)

time: 325 us -> 328 us (level)
  local copies, waits for them, and re-layouts: 14.5 us -> 18.8 us
    optimization_barrier x0 -> x1, local copies, waits for them, and re-layouts: none -> 4.4 us  [body(): lax.optimization_barrier((reply, hidden_rows, kv_weight))]
where the time goes in v16:
time: 328 us; the launch traced here: 327 us
  waiting for transfers between devices  183 us (56%)
  blocking collectives  64.1 us (20%)
  matrix products  27.6 us (8%)
  local copies, waits for them, and re-layouts  18.8 us (6%)
  between operations  14 us (4%)
  other arithmetic  10.5 us (3%)
  starting transfers between devices  8.28 us (3%)
    all_gather x1, waiting for transfers between devices, body(): w_head = lax.all_gather(kv_weight, ('pz', 'pc'), axis=1, tiled=True)  94.1 us
    all_gather x1, waiting for transfers between devices, body(): w_all = lax.all_gather(w_head, 'px', axis=1, tiled=True)  62 us
    all_to_all x1, blocking collectives, body(): step = lax.all_to_all(step, 'pz', split_axis=2, concat_axis=2, tiled=True)  46.2 us
    reduce_scatter x1, waiting for transfers between devices, body(): lax.psum_scatter(partial_kv.astype(jnp.bfloat16), 'tp', scatter_dimension...  26.4 us
    all_to_all x1, blocking collectives, body(): lax.all_to_all(step, ('px', 'pc'), split_axis=1, concat_axis=1, tiled=True)  17.9 us
    squeeze x8, local copies, waits for them, and re-layouts, body(): (top, total, numer), unused = lax.scan(visit, (top, total, numer), grouped)  8.64 us
    all_to_all x1, starting transfers between devices, body(): lax.all_to_all(reply, POOL, split_axis=0, concat_axis=0, tiled=True)  7.98 us
    dot_general x8, matrix products, merge(): jnp.dot(weights_now.astype(jnp.bfloat16), vals, preferred_element_type=jn...  7.85 us
  transfers between devices with their start and end apart: 4, of which 3 were waited for; matrix products, arithmetic and copies ran while one was open for 3% of the time, Pallas kernels for 0%

profile of v16, /device:TPU:2, one launch (start us, length us, event | category | flops | bytes accessed | tf_op | source)
XLA Modules:
  0.0 326.8 jit_solution(9818864553391584039)
XLA Ops:
  7.2 0.7 fusion.36
  7.9 0.1 pad_maximum_fusion.1
  8.0 1.1 pad_maximum_fusion
  9.1 0.2 reshape.172
  9.3 0.1 copy.28
  9.4 17.9 %all_to_all.15 = bf16[9,8,16,256]{3,2,0,1:T(8,128)(2,1)S(1)} all-to-all(bf16[9,8,16,256]{3,2,0,1:T(8,128)(2,1)S(1)} %bitcast.90), channel_id=1, replica_groups=mesh['px'=4,'pz'=16,'pc'=2,'tp'=4] {'px','pc'}, dimensions={1} | all-to-all | bytes 1179648 | tf_op jit(solution)/shard_map/all_to_all | solution.py:55
  27.3 0.2 copy.21
  27.5 46.2 %all_to_all.16 = bf16[9,8,16,256]{3,1,0,2:T(8,128)(2,1)S(1)} all-to-all(bf16[9,8,16,256]{3,1,0,2:T(8,128)(2,1)S(1)} %copy.21), channel_id=1, replica_groups=mesh['px'=4,'pz'=16,'pc'=2,'tp'=4] {'pz'}, dimensions={2} | all-to-all | bytes 1179648 | tf_op jit(solution)/shard_map/all_to_all | solution.py:56
  73.7 0.1 copy.22
  73.8 0.6 copy.23
  74.4 0.2 reshape.175
  74.7 0.1 fusion.26
  74.8 0.1 copy.24
  74.8 7.3 %fusion.13 = bf16[128,64,1,256]{3,0,1,2:T(8,128)(2,1)S(1)} fusion(s32[128,64]{0,1:T(8,128)S(1)} %copy.24, bf16[128,8,256]{2,0,1:T(8,128)(2,1)S(1)} %slice.39), kind=kOutput, calls=%fused_computation.20 | convolution fusion | flops 4303355904 | bytes 4751360 | tf_op jit(solution)/shard_map/dot_general | solution.py:68
  82.2 4.4 %copy.26 = bf16[128,64,1,256]{3,1,2,0:T(8,128)(2,1)} copy(bf16[128,64,1,256]{3,0,1,2:T(8,128)(2,1)S(1)} %fusion.13) | data formatting | bytes 8388608 | tf_op jit(solution)/shard_map/optimization_barrier | solution.py:70
  86.6 8.0 %all-to-all-start.2 = ((bf16[128,64,1,256]{3,1,2,0:T(8,128)(2,1)}), bf16[128,64,1,256]{3,1,2,0:T(8,128)(2,1)}, u32[]{:S(2)}, u32[]{:S(2)}) async-start(bf16[128,64,1,256]{3,1,2,0:T(8,128)(2,1)} %copy.26), calls=%async_computation.3 | async-start | bytes 8388608 | tf_op jit(solution)/shard_map/all_to_all | solution.py:71
  94.6 0.7 all-gather.3.cloned.1.call-update
  95.4 94.1 %all-gather.3.cloned.1.call-done = bf16[2048,256]{0,1:T(8,128)(2,1)} async-done(((bf16[2048,8]{0,1:T(8,128)(2,1)}), bf16[2048,256]{0,1:T(8,128)(2,1)}) %all-gather.3.cloned.1.call-update) | async-done | bytes 1048592 | tf_op jit(solution)/shard_map/all_gather | solution.py:73
  189.5 0.2 reduce-scatter.2.cloned.1.call-start
  189.7 62.0 %all-gather.5.cloned.1.call-done = bf16[2048,1024]{0,1:T(8,128)(2,1)} async-done(((bf16[2048,256]{0,1:T(8,128)(2,1)}), bf16[2048,1024]{0,1:T(8,128)(2,1)}) %all-gather.5.cloned.1.call-update) | async-done | bytes 4194320 | tf_op jit(solution)/shard_map/all_gather | solution.py:74
  251.7 4.4 %convolution_convert_fusion = bf16[128,1024]{1,0:T(8,128)(2,1)} fusion(bf16[128,2048]{1,0:T(8,128)(2,1)S(1)} %copy-done, bf16[2048,1024]{0,1:T(8,128)(2,1)} %all-gather.5.cloned.1.call-done), kind=kOutput, calls=%fused_computation.23 | convolution fusion | flops 537001984 | bytes 4980736 | tf_op jit(solution)/shard_map/dot_general | solution.py:75
  256.2 3.0 gather_fusion
  259.2 0.2 broadcast_select_fusion
  259.4 0.2 copy.27
  259.6 0.1 reshape_squeeze_reshape.3
  259.8 26.4 %reduce-scatter.2.cloned.1.call-done = bf16[128,256]{1,0:T(8,128)(2,1)} async-done(((bf16[128,1024]{1,0:T(8,128)(2,1)}), bf16[128,256]{1,0:T(8,128)(2,1)}) %reduce-scatter.2.cloned.1.call-update) | async-done | bytes 65552 | tf_op jit(solution)/shard_map/reduce_scatter | solution.py:76
  286.2 1.0 select_reduce_fusion
  287.2 0.1 fusion.20
  287.3 1.0 fusion.21
  288.4 30.8 %while.15 = (s32[]{:T(128)}, f32[1024]{0:T(1024)S(1)}, f32[1024]{0:T(1024)S(1)}, f32[1024,128]{1,0:T(8,128)S(1)}, bf16[8,1024,256]{2,1,0:T(8,128)(2,1)}, /*index...) while((s32[]{:T(128)}, f32[1024]{0:T(1024)S(1)}, f32[1024]{0:T(1024)S(1)}, ...), condition=%wide.region_6.7_spmd.clone, body=%wide.region_3.6_spmd.clone.sunk | while | flops 545523712 | bytes 15659105 | solution.py:106
  288.4 1.1 dynamic-slice_bitcast_fusion.2
  289.5 0.7 fusion.51
  290.2 1.0 fusion.52
  291.2 1.0 convolution_add_fusion.2
  292.2 1.1 dynamic-slice_bitcast_fusion.2
  293.3 0.7 fusion.51
  294.1 1.0 fusion.52
  295.1 1.0 convolution_add_fusion.2
  296.1 1.1 dynamic-slice_bitcast_fusion.2
  297.2 0.8 fusion.51
  297.9 1.0 fusion.52
  298.9 1.0 convolution_add_fusion.2
  299.9 1.1 dynamic-slice_bitcast_fusion.2
  301.0 0.7 fusion.51
  301.8 1.0 fusion.52
  302.8 1.0 convolution_add_fusion.2
  303.8 1.1 dynamic-slice_bitcast_fusion.2
  304.9 0.8 fusion.51
  305.7 1.0 fusion.52
  306.7 1.0 convolution_add_fusion.2
  307.7 1.1 dynamic-slice_bitcast_fusion.2
  308.7 0.7 fusion.51
  309.5 1.0 fusion.52
  310.5 1.0 convolution_add_fusion.2
  311.5 1.1 dynamic-slice_bitcast_fusion.2
  312.6 0.8 fusion.51
  313.4 1.0 fusion.52
  314.4 1.0 convolution_add_fusion.2
  315.4 1.1 dynamic-slice_bitcast_fusion.2
  316.4 0.7 fusion.51
  317.2 1.0 fusion.52
  318.2 1.0 convolution_add_fusion.2
  319.2 0.2 divide_convert_fusion
  319.4 0.8 convert_element_type.39
  (44 shorter events, 0.4 us)
Async XLA Ops:
  7.2 244.5 %copy-start = (bf16[128,2048]{1,0:T(8,128)(2,1)S(1)}, bf16[128,2048]{1,0:T(8,128)(2,1)}, u32[]{:S(2)}) copy-start(bf16[128,2048]{1,0:T(8,128)(2,1)} %param.8) | copy-start | bytes 1572868
  86.6 201.8 %all-to-all-start.2 = ((bf16[128,64,1,256]{3,1,2,0:T(8,128)(2,1)}), bf16[128,64,1,256]{3,1,2,0:T(8,128)(2,1)}, u32[]{:S(2)}, u32[]{:S(2)}) async-start(bf16[128,64,1,256]{3,1,2,0:T(8,128)(2,1)} %copy.26), calls=%async_computation.3 | async-start | bytes 8388608 | tf_op jit(solution)/shard_map/all_to_all | solution.py:71
  94.5 161.6 %copy-start.2 = (s32[1,2,64]{2,1,0:T(2,128)S(1)}, s32[1,2,64]{2,1,0:T(2,128)}, u32[]{:S(2)}) copy-start(s32[1,2,64]{2,1,0:T(2,128)} %param.13) | copy-start | bytes 1540
  94.6 165.1 %copy-start.1 = (bf16[128,1024]{1,0:T(8,128)(2,1)S(1)}, bf16[128,1024]{1,0:T(8,128)(2,1)}, u32[]{:S(2)}) copy-start(bf16[128,1024]{1,0:T(8,128)(2,1)} %param.10) | copy-start | bytes 786436
  94.6 94.9 %all-gather.3.cloned.1.call-start = ((), (), s32[]{:S(2)}) async-start(), calls=%async_computation.4 | async-start | bytes 1081344 | tf_op jit(solution)/shard_map/all_gather | solution.py:73
  95.3 156.4 %all-gather.5.cloned.1.call-start = ((), (), s32[]{:S(2)}) async-start(), calls=%async_computation.5 | async-start | bytes 5242880 | tf_op jit(solution)/shard_map/all_gather | solution.py:74
  189.5 96.7 %reduce-scatter.2.cloned.1.call-start = ((), (), s32[]{:S(2)}) async-start(), calls=%async_computation.6 | async-start | bytes 327680 | tf_op jit(solution)/shard_map/reduce_scatter | solution.py:76
Sparse Core Ops, SparseCore 0:
  97.5 91.8 all-gather.2
  191.5 60.1 all-gather.4
  256.3 29.8 reduce-scatter.1

commit v17 on v14

--- a/solution.py
+++ b/solution.py
@@ -79,7 +79,7 @@
     group = QH // KVH
     scale = float(HD) ** (-0.5)
     local_heads = fresh.shape[1] // (2 * HD)
-    tokens_step = BLK // math.gcd(BLK, 8)
+    tokens_step = BLK // math.gcd(BLK, 4)
     steps_count = BLK // tokens_step
     grouped = fetched.reshape(steps_count, tokens_step * fetch_count, width)
     token_of_row = jnp.arange(count * group) // group

time: 325 us -> 319 us (0.982)
  the two profiles are of different devices: /device:TPU:2 before, /device:TPU:34 now
where the time goes in v17:
time: 319 us; the launch traced here: 318 us
  waiting for transfers between devices  184 us (58%)
  blocking collectives  63.7 us (20%)
  matrix products  27 us (8%)
  between operations  13.9 us (4%)
  local copies, waits for them, and re-layouts  11 us (3%)
  other arithmetic  10.4 us (3%)
  starting transfers between devices  8.39 us (3%)
    all_gather x1, waiting for transfers between devices, body(): w_head = lax.all_gather(kv_weight, ('pz', 'pc'), axis=1, tiled=True)  91.3 us
    all_gather x1, waiting for transfers between devices, body(): w_all = lax.all_gather(w_head, 'px', axis=1, tiled=True)  66.6 us
    all_to_all x1, blocking collectives, body(): step = lax.all_to_all(step, 'pz', split_axis=2, concat_axis=2, tiled=True)  49.4 us
    reduce_scatter x1, waiting for transfers between devices, body(): lax.psum_scatter(partial_kv.astype(jnp.bfloat16), 'tp', scatter_dimension...  24.5 us
    all_to_all x1, blocking collectives, body(): lax.all_to_all(step, ('px', 'pc'), split_axis=1, concat_axis=1, tiled=True)  14.3 us
    dot_general x1, matrix products, body(): jnp.dot(picks, table, preferred_element_type=jnp.float32)  9.18 us
    all_to_all x1, starting transfers between devices, body(): lax.all_to_all(reply, POOL, split_axis=0, concat_axis=0, tiled=True)  8.1 us
    convert_element_type x4, other arithmetic, merge(): weights_now.astype(jnp.bfloat16)  7.79 us
  transfers between devices with their start and end apart: 4, of which 4 were waited for; matrix products, arithmetic and copies ran while one was open for 3% of the time, Pallas kernels for 0%

profile of v17, /device:TPU:34, one launch (start us, length us, event | category | flops | bytes accessed | tf_op | source)
XLA Modules:
  0.0 318.3 jit_solution(7537971316295151175)
XLA Ops:
  7.2 0.0 copy-start
  7.2 0.7 fusion.32
  7.9 0.1 pad_maximum_fusion.1
  8.0 1.1 pad_maximum_fusion
  9.1 0.2 reshape.149
  9.3 0.1 copy.22
  9.4 14.3 %all_to_all.15 = bf16[9,8,16,256]{3,2,0,1:T(8,128)(2,1)S(1)} all-to-all(bf16[9,8,16,256]{3,2,0,1:T(8,128)(2,1)S(1)} %bitcast.88), channel_id=1, replica_groups=mesh['px'=4,'pz'=16,'pc'=2,'tp'=4] {'px','pc'}, dimensions={1} | all-to-all | bytes 1179648 | tf_op jit(solution)/shard_map/all_to_all | solution.py:55
  23.7 0.2 copy.17
  23.9 49.4 %all_to_all.16 = bf16[9,8,16,256]{3,1,0,2:T(8,128)(2,1)S(1)} all-to-all(bf16[9,8,16,256]{3,1,0,2:T(8,128)(2,1)S(1)} %copy.17), channel_id=1, replica_groups=mesh['px'=4,'pz'=16,'pc'=2,'tp'=4] {'pz'}, dimensions={2} | all-to-all | bytes 1179648 | tf_op jit(solution)/shard_map/all_to_all | solution.py:56
  73.3 0.2 reshape.151
  73.5 0.6 copy.28
  74.1 0.2 reshape.152
  74.4 0.1 fusion.22
  74.5 0.1 eq.17
  74.6 9.2 %fusion.11 = bf16[8192,256]{1,0:T(8,128)(2,1)} fusion(s32[8192]{0:T(1024)S(1)} %eq.17, bf16[128,8,256]{2,0,1:T(8,128)(2,1)S(1)} %slice.39), kind=kOutput, calls=%fused_computation.19 | convolution fusion | flops 4305453056 | bytes 4751360 | tf_op jit(solution)/shard_map/dot_general | solution.py:68
  83.8 0.0 copy-start.2
  83.8 0.0 copy-start.1
  83.8 8.1 %all-to-all-start.2 = ((bf16[128,64,1,256]{3,1,2,0:T(8,128)(2,1)}), bf16[128,64,1,256]{3,1,2,0:T(8,128)(2,1)}, u32[]{:S(2)}, u32[]{:S(2)}) async-start(bf16[128,64,1,256]{3,1,2,0:T(8,128)(2,1)} %bitcast.86), calls=%async_computation.3 | async-start | bytes 8388608 | tf_op jit(solution)/shard_map/all_to_all | solution.py:71
  91.9 0.0 all-gather.3.cloned.1.call-start
  91.9 0.7 all-gather.3.cloned.1.call-update
  92.6 0.0 all-gather.5.cloned.1.call-start
  92.6 91.3 %all-gather.3.cloned.1.call-done = bf16[2048,256]{0,1:T(8,128)(2,1)} async-done(((bf16[2048,8]{0,1:T(8,128)(2,1)}), bf16[2048,256]{0,1:T(8,128)(2,1)}) %all-gather.3.cloned.1.call-update) | async-done | bytes 1048592 | tf_op jit(solution)/shard_map/all_gather | solution.py:73
  183.9 0.0 all-gather.5.cloned.1.call-update
  184.0 0.2 reduce-scatter.2.cloned.1.call-start
  184.2 66.6 %all-gather.5.cloned.1.call-done = bf16[2048,1024]{0,1:T(8,128)(2,1)} async-done(((bf16[2048,256]{0,1:T(8,128)(2,1)}), bf16[2048,1024]{0,1:T(8,128)(2,1)}) %all-gather.5.cloned.1.call-update) | async-done | bytes 4194320 | tf_op jit(solution)/shard_map/all_gather | solution.py:74
  250.8 0.0 copy-done
  250.8 4.4 %convolution_convert_fusion = bf16[128,1024]{1,0:T(8,128)(2,1)} fusion(bf16[128,2048]{1,0:T(8,128)(2,1)S(1)} %copy-done, bf16[2048,1024]{0,1:T(8,128)(2,1)} %all-gather.5.cloned.1.call-done), kind=kOutput, calls=%fused_computation.22 | convolution fusion | flops 537001984 | bytes 4980736 | tf_op jit(solution)/shard_map/dot_general | solution.py:75
  255.2 0.0 reduce-scatter.2.cloned.1.call-update
  255.2 0.0 copy-done.2
  255.3 3.0 gather_fusion
  258.3 0.2 broadcast_select_fusion
  258.5 0.2 copy.21
  258.7 0.0 copy-done.1
  258.7 0.1 reshape_squeeze_reshape.3
  258.9 24.5 %reduce-scatter.2.cloned.1.call-done = bf16[128,256]{1,0:T(8,128)(2,1)} async-done(((bf16[128,1024]{1,0:T(8,128)(2,1)}), bf16[128,256]{1,0:T(8,128)(2,1)}) %reduce-scatter.2.cloned.1.call-update) | async-done | bytes 65552 | tf_op jit(solution)/shard_map/reduce_scatter | solution.py:76
  283.3 1.0 select_reduce_fusion
  284.3 0.1 fusion.16
  284.5 1.0 fusion.17
  285.5 0.6 all-to-all-done.2
  286.1 24.6 %while.15 = (s32[]{:T(128)}, f32[1024]{0:T(1024)S(1)}, f32[1024]{0:T(1024)S(1)}, f32[1024,128]{1,0:T(8,128)S(1)}, bf16[4,2048,256]{2,1,0:T(8,128)(2,1)}, /*index...) while((s32[]{:T(128)}, f32[1024]{0:T(1024)S(1)}, f32[1024]{0:T(1024)S(1)}, ...), condition=%wide.region_6.7_spmd.clone, body=%wide.region_3.6_spmd.clone.sunk | while | flops 1090783232 | bytes 29814880 | solution.py:106
  286.1 1.3 dynamic-slice_bitcast_fusion.2
  287.4 1.3 fusion.47
  288.7 1.9 fusion.48
  290.7 1.5 convolution_add_fusion.2
  292.3 1.3 dynamic-slice_bitcast_fusion.2
  293.6 1.3 fusion.47
  294.9 1.9 fusion.48
  296.9 1.5 convolution_add_fusion.2
  298.4 1.3 dynamic-slice_bitcast_fusion.2
  299.7 1.3 fusion.47
  301.1 1.9 fusion.48
  303.0 1.5 convolution_add_fusion.2
  304.6 1.3 dynamic-slice_bitcast_fusion.2
  305.9 1.3 fusion.47
  307.2 1.9 fusion.48
  309.2 1.5 convolution_add_fusion.2
  310.7 0.2 divide_convert_fusion
  311.0 0.8 convert_element_type.43
  (21 shorter events, 0.2 us)
Async XLA Ops:
  7.2 243.6 %copy-start = (bf16[128,2048]{1,0:T(8,128)(2,1)S(1)}, bf16[128,2048]{1,0:T(8,128)(2,1)}, u32[]{:S(2)}) copy-start(bf16[128,2048]{1,0:T(8,128)(2,1)} %param.8) | copy-start | bytes 1572868
  83.8 171.5 %copy-start.2 = (s32[1,2,64]{2,1,0:T(2,128)S(1)}, s32[1,2,64]{2,1,0:T(2,128)}, u32[]{:S(2)}) copy-start(s32[1,2,64]{2,1,0:T(2,128)} %param.13) | copy-start | bytes 1540
  83.8 175.0 %copy-start.1 = (bf16[128,1024]{1,0:T(8,128)(2,1)S(1)}, bf16[128,1024]{1,0:T(8,128)(2,1)}, u32[]{:S(2)}) copy-start(bf16[128,1024]{1,0:T(8,128)(2,1)} %param.10) | copy-start | bytes 786436
  83.8 202.4 %all-to-all-start.2 = ((bf16[128,64,1,256]{3,1,2,0:T(8,128)(2,1)}), bf16[128,64,1,256]{3,1,2,0:T(8,128)(2,1)}, u32[]{:S(2)}, u32[]{:S(2)}) async-start(bf16[128,64,1,256]{3,1,2,0:T(8,128)(2,1)} %bitcast.86), calls=%async_computation.3 | async-start | bytes 8388608 | tf_op jit(solution)/shard_map/all_to_all | solution.py:71
  91.9 92.1 %all-gather.3.cloned.1.call-start = ((), (), s32[]{:S(2)}) async-start(), calls=%async_computation.4 | async-start | bytes 1081344 | tf_op jit(solution)/shard_map/all_gather | solution.py:73
  92.6 158.2 %all-gather.5.cloned.1.call-start = ((), (), s32[]{:S(2)}) async-start(), calls=%async_computation.5 | async-start | bytes 5242880 | tf_op jit(solution)/shard_map/all_gather | solution.py:74
  184.0 99.4 %reduce-scatter.2.cloned.1.call-start = ((), (), s32[]{:S(2)}) async-start(), calls=%async_computation.6 | async-start | bytes 327680 | tf_op jit(solution)/shard_map/reduce_scatter | solution.py:76
Sparse Core Ops, SparseCore 0:
  94.8 89.0 all-gather.2
  186.0 64.7 all-gather.4
  255.4 27.9 reduce-scatter.1
